TPU v7x, 256 devices: a whole 4x4x8 slice. The times are simulated.
256 devices in a mesh: ctx: 32 (over z, x), head: 8 (over y, core).
Axes of the slice: x: 4, y: 4, z: 8, core: 2. Of those that a mesh axis runs over, the one named last changes fastest.
Arguments:
- query_matrix: bfloat16 [32768, 4096], P(('ctx', 'head')), may hold values from -5 to 5
- key_matrix: bfloat16 [32768, 1024], P(('ctx', 'head')), may hold values from -5 to 5
- value_matrix: bfloat16 [32768, 1024], P(('ctx', 'head')), may hold values from -12 to 12
- output_gradient: bfloat16 [32768, 4096], P('ctx', 'head'), may hold values from -12 to 12
- doc_start: int32 [128], replicated, may hold values from 0 to 1, as said below
Outputs:
- attended: bfloat16 [32768, 4096], P('ctx', 'head')
- grad_q: bfloat16 [32768, 4096], P('ctx', 'head')
- grad_k: bfloat16 [32768, 1024], P('ctx', 'head')
- grad_v: bfloat16 [32768, 1024], P('ctx', 'head')
Inputs may be any that keep to these rules, and one draw needn't show every extreme that they name: `doc_start`: entry 0 is 1; a document starts at each unit whose entry is 1 and lasts to the next start or the end; every document has 1 to 4 units, and some document has exactly 1024 tokens.
All inputs are finite; a program needn't handle non-finite values.
Results may differ from a plain program's by a relative error of at most 0.019.
Values may be sent and summed in bfloat16 or wider, within the bound.
No kernel may reach another device: no remote copies, remote signals or barrier semaphores. Data moves between devices by JAX's collectives and lax.ppermute only.
A program may use at most 64 MiB of HBM per device.

v0:
```python
import jax
import jax.numpy as jnp
from jax import lax
from jax.sharding import PartitionSpec as P

QUERY_HEADS = 32
KEY_VALUE_HEADS = 8
HEAD_SIZE = 128


def from_behind(block, axis, distance):
    devices = range(lax.axis_size(axis))
    route = [(i - distance, i) for i in devices if i - distance in devices]
    return lax.ppermute(block, axis, route)


def tile_grads(query_tile, grad_tile, key_rows, value_rows, query_doc, key_doc, query_pos, key_pos):
    score_scale = query_tile.shape[-1] ** (-0.5)
    scores = (
        jnp.einsum("tgrd,ngd->grtn", query_tile, key_rows, preferred_element_type=jnp.float32)
        * score_scale
    )
    visible = (key_doc[None, :] == query_doc[:, None]) & (key_pos[None, :] <= query_pos[:, None])
    scores = jnp.where(visible, scores, -jnp.inf)
    row_top = jnp.max(scores, axis=-1, keepdims=True)
    log_total = row_top + jnp.log(jnp.sum(jnp.exp(scores - row_top), axis=-1, keepdims=True))
    weights = jnp.exp(scores - log_total)
    weights_low = weights.astype(jnp.bfloat16)
    attended = jnp.einsum(
        "grtn,ngd->tgrd", weights_low, value_rows, preferred_element_type=jnp.float32
    ).astype(jnp.bfloat16)
    row_delta = jnp.sum(grad_tile.astype(jnp.float32) * attended.astype(jnp.float32), axis=-1)
    row_delta = jnp.transpose(row_delta, (1, 2, 0))[..., None]
    grad_weights = jnp.einsum(
        "tgrd,ngd->grtn", grad_tile, value_rows, preferred_element_type=jnp.float32
    )
    grad_scores = (weights * (grad_weights - row_delta)).astype(jnp.bfloat16)
    grad_query = (
        jnp.einsum("grtn,ngd->tgrd", grad_scores, key_rows, preferred_element_type=jnp.float32)
        * score_scale
    ).astype(jnp.bfloat16)
    grad_key = (
        jnp.einsum("grtn,tgrd->ngd", grad_scores, query_tile, preferred_element_type=jnp.float32)
        * score_scale
    )
    grad_value = jnp.einsum(
        "grtn,tgrd->ngd", weights_low, grad_tile, preferred_element_type=jnp.float32
    )
    return (attended, grad_query, grad_key, grad_value)


def local(query_matrix, key_matrix, value_matrix, output_gradient, doc_start):
    token_per_shard = query_matrix.shape[0]
    query_heads = query_matrix.reshape(token_per_shard, QUERY_HEADS, HEAD_SIZE)
    heads_of_keys = key_matrix.reshape(token_per_shard, KEY_VALUE_HEADS, HEAD_SIZE)
    heads_of_values = value_matrix.reshape(token_per_shard, KEY_VALUE_HEADS, HEAD_SIZE)
    query_array, own_keys, own_values = (
        lax.all_to_all(query_heads, "head", split_axis=1, concat_axis=0, tiled=True),
        lax.all_to_all(heads_of_keys, "head", split_axis=1, concat_axis=0, tiled=True),
        lax.all_to_all(heads_of_values, "head", split_axis=1, concat_axis=0, tiled=True),
    )
    ctx_rows = own_keys.shape[0]
    unit_rows = 2 * token_per_shard
    earlier_keys, earlier_values = from_behind((own_keys, own_values), "ctx", 1)
    kv_local = own_keys.shape[1]
    heads_per_group = query_array.shape[1] // kv_local
    query_array = query_array.reshape(ctx_rows, kv_local, heads_per_group, HEAD_SIZE)
    gradient_per_head = output_gradient.reshape(ctx_rows, kv_local, heads_per_group, HEAD_SIZE)
    per_shard = ctx_rows // unit_rows
    ctx_index = lax.axis_index("ctx")
    unit_doc = jnp.cumsum(doc_start)
    own_units = lax.dynamic_slice_in_dim(unit_doc, ctx_index * per_shard, per_shard)
    prior_units = lax.dynamic_slice_in_dim(
        unit_doc, jnp.maximum(ctx_index - 1, 0) * per_shard, per_shard
    )
    prior_units = jnp.where(ctx_index > 0, prior_units, -1)
    own_doc = jnp.repeat(own_units, unit_rows, total_repeat_length=ctx_rows)
    prior_doc = jnp.repeat(prior_units, unit_rows, total_repeat_length=ctx_rows)[
        ctx_rows - ctx_rows :
    ]
    joined_keys = jnp.concatenate([earlier_keys, own_keys], axis=0)
    joined_values = jnp.concatenate([earlier_values, own_values], axis=0)
    joined_doc = jnp.concatenate([prior_doc, own_doc], axis=0)
    joined_pos = jnp.arange(ctx_rows + ctx_rows, dtype=jnp.int32) - ctx_rows
    before = ctx_rows - unit_rows
    key_grad = jnp.zeros((ctx_rows + ctx_rows, kv_local, HEAD_SIZE), jnp.float32)
    value_grad = jnp.zeros((ctx_rows + ctx_rows, kv_local, HEAD_SIZE), jnp.float32)
    pieces = []
    query_grads = []
    for unit_number in range(per_shard):
        first_row = unit_number * unit_rows
        end_row = first_row + unit_rows
        window_start = ctx_rows - before + first_row
        window_end = window_start + ctx_rows
        query_tile = query_array[first_row:end_row]
        grad_tile = gradient_per_head[first_row:end_row]
        query_doc = own_doc[first_row:end_row]
        query_pos = jnp.arange(first_row, end_row, dtype=jnp.int32)
        results = tile_grads(
            query_tile,
            grad_tile,
            joined_keys[window_start:window_end],
            joined_values[window_start:window_end],
            query_doc,
            joined_doc[window_start:window_end],
            query_pos,
            joined_pos[window_start:window_end],
        )
        attended, grad_query, grad_key, grad_value = results
        pieces.append(attended)
        query_grads.append(grad_query)
        key_grad = key_grad.at[window_start:window_end].add(grad_key)
        value_grad = value_grad.at[window_start:window_end].add(grad_value)
    later_keys, later_values = (
        from_behind(key_grad[:ctx_rows].astype(jnp.bfloat16), "ctx", -1).astype(jnp.float32),
        from_behind(value_grad[:ctx_rows].astype(jnp.bfloat16), "ctx", -1).astype(jnp.float32),
    )
    key_own = key_grad[ctx_rows:].at[ctx_rows - ctx_rows :].add(later_keys)
    value_own = value_grad[ctx_rows:].at[ctx_rows - ctx_rows :].add(later_values)
    summed_keys = key_own.astype(jnp.bfloat16).reshape(ctx_rows, kv_local * HEAD_SIZE)
    summed_values = value_own.astype(jnp.bfloat16).reshape(ctx_rows, kv_local * HEAD_SIZE)
    attended_all = jnp.concatenate(pieces, axis=0).reshape(
        ctx_rows, kv_local * heads_per_group * HEAD_SIZE
    )
    query_total = jnp.concatenate(query_grads, axis=0).reshape(
        ctx_rows, kv_local * heads_per_group * HEAD_SIZE
    )
    return (attended_all, query_total, summed_keys, summed_values)


def solution(mesh):
    placed = (
        P(("ctx", "head"), None),
        P(("ctx", "head"), None),
        P(("ctx", "head"), None),
        P("ctx", "head"),
        P(),
    )
    return jax.shard_map(
        local,
        mesh=mesh,
        in_specs=placed,
        out_specs=(P("ctx", "head"), P("ctx", "head"), P("ctx", "head"), P("ctx", "head")),
        check_vma=False,
    )
```

profile of v0, /device:TPU:138, one launch (start us, length us, event | category | flops | bytes accessed | tf_op | source)
XLA Modules:
  0.0 108.5 jit_solution(9466815986551676609)
XLA Ops:
  0.7 0.9 copy-done
  1.6 0.8 copy_bitcast_fusion.1
  2.3 4.9 %all-to-all-start.1 = ((bf16[128,8,128]{2,0,1:T(8,128)(2,1)}), bf16[128,8,128]{2,0,1:T(8,128)(2,1)S(1)}, u32[]{:S(2)}, u32[]{:S(2)}) async-start(bf16[128,8,128]{2,0,1:T(8,128)(2,1)} %copy_bitcast_fusion.1), calls=%async_computation.1 | async-start | bytes 524288 | tf_op jit(solution)/shard_map/all_to_all | solution.py:59
  7.3 0.8 copy.115
  8.4 0.7 fusion.173
  9.0 5.7 %select_select_fusion.1 = (s32[1024]{0:T(1024)S(1)}, s32[1024]{0:T(1024)S(1)}) fusion(pred[1024]{0:T(1024)(128)(4,1)} %constant.409, pred[1024]{0:T(1024)(128)(4,1)} %constant.410, pred[1024]{0:T(1024)(128)(4,1)} %constant.411, s32[]{:T(128)} %bitcast.9, s32[]{:T(128)} %bitcast.8, s32[]{:T(128)} %bitcast.7, s32[]{:T(128)} %bitcast.6, s32[]{:T(128)} %bitcast.13, ...), kind=kLoop, calls=%fused_computation.146 | loop fusion | flops 6144 | bytes 11296 | tf_op jit(solution)/shard_map/jit(_take)/gather | solution.py:78
  14.8 2.3 %copy.117 = bf16[128,4096]{0,1:T(8,128)(2,1)} copy(bf16[128,4096]{1,0:T(8,128)(2,1)} %param.35) | data formatting | bytes 2097152 | tf_op args[0]
  17.1 0.8 copy.113
  18.0 0.3 compare_and_fusion
  18.3 1.0 compare_and_fusion.2
  19.3 4.8 %all-to-all-start = ((bf16[128,8,128]{0,2,1:T(8,128)(2,1)}), bf16[128,8,128]{0,2,1:T(8,128)(2,1)S(1)}, u32[]{:S(2)}, u32[]{:S(2)}) async-start(bf16[128,8,128]{0,2,1:T(8,128)(2,1)} %bitcast), calls=%async_computation | async-start | bytes 524288 | tf_op jit(solution)/shard_map/all_to_all | solution.py:60
  24.1 1.0 fusion.132
  25.2 5.0 %all-to-all-done = bf16[128,8,128]{0,2,1:T(8,128)(2,1)S(1)} async-done(((bf16[128,8,128]{0,2,1:T(8,128)(2,1)}), bf16[128,8,128]{0,2,1:T(8,128)(2,1)S(1)}, u32[]{:S(2)}, u32[]{:S(2)}) %all-to-all-start) | async-done | bytes 262176 | tf_op jit(solution)/shard_map/all_to_all | solution.py:60
  30.2 4.9 %all-to-all-start.2 = ((bf16[128,32,128]{0,2,1:T(8,128)(2,1)}), bf16[128,32,128]{0,2,1:T(8,128)(2,1)S(1)}, u32[]{:S(2)}, u32[]{:S(2)}) async-start(bf16[128,32,128]{0,2,1:T(8,128)(2,1)} %bitcast.19), calls=%async_computation.2 | async-start | bytes 2097152 | tf_op jit(solution)/shard_map/all_to_all | solution.py:58
  35.1 0.7 copy_bitcast_fusion
  35.9 3.4 %collective-permute-start = (bf16[1024,1,128]{0,2,1:T(8,128)(2,1)}, bf16[1024,1,128]{0,2,1:T(8,128)(2,1)}, u32[]{:S(2)}, u32[]{:S(2)}) collective-permute-start(bf16[1024,1,128]{0,2,1:T(8,128)(2,1)} %copy_bitcast_fusion), channel_id=1, source_target_pairs={{0,8},{8,16},{16,24},{24,32},{32,40},{40,48},{48,56},{56,64},{64,7... | collective-permute-start | bytes 786440 | tf_op jit(solution)/shard_map/ppermute | solution.py:14
  39.3 0.8 copy.184
  40.1 0.8 copy.185
  41.0 0.8 copy.186
  41.8 0.8 copy.187
  42.6 0.3 compare_and_fusion.1
  43.0 3.3 %collective-permute-start.1 = (bf16[1024,1,128]{2,0,1:T(8,128)(2,1)S(1)}, bf16[1024,1,128]{2,0,1:T(8,128)(2,1)S(1)}, u32[]{:S(2)}, u32[]{:S(2)}) collective-permute-start(bf16[1024,1,128]{2,0,1:T(8,128)(2,1)S(1)} %bitcast.523), channel_id=1, source_target_pairs={{0,8},{8,16},{16,24},{24,32},{32,40},{40,48},{48,56},{56,64},{64,7... | collective-permute-start | bytes 786440 | tf_op jit(solution)/shard_map/ppermute | solution.py:14
  46.3 0.9 copy.126
  47.1 1.0 constant_dynamic-update-slice_fusion.1
  48.1 0.8 copy-done.17
  48.9 0.7 all-to-all-done.2
  49.6 0.7 copy.118
  50.4 2.5 %collective-permute-done.1 = bf16[1024,1,128]{2,0,1:T(8,128)(2,1)S(1)} collective-permute-done((bf16[1024,1,128]{2,0,1:T(8,128)(2,1)S(1)}, bf16[1024,1,128]{2,0,1:T(8,128)(2,1)S(1)}, u32[]{:S(2)}, u32[]{:S(2)}) %collective-permute-start.1) | collective-permute-done | bytes 262176 | tf_op jit(solution)/shard_map/ppermute | solution.py:14
  52.9 1.8 %fusion.12 = (f32[4,256]{1,0:T(4,128)S(1)}, f32[1024,256,4]{1,0,2:T(8,128)S(1)}) fusion(pred[256,1024]{0,1:T(8,128)(4,1)} %fusion.132, bf16[256,4,128]{2,0,1:T(8,128)(2,1)S(1)} %bitcast.542, bf16[1024,1,128]{2,0,1:T(8,128)(2,1)S(1)} %collective-permute-done.1, bf16[1024,1,128]{2,0,1:T(8,128)(2,1)S(1)} %bitcast.524), kind=kOutput, calls=%fused_computation.28 | convolution fusion | flops 272104448 | bytes 5246976 | tf_op jit(solution)/shard_map/tgrd,ngd->grtn/dot_general | solution.py:20
  54.7 0.9 exponential_reduce_fusion.3
  55.7 0.8 fusion.13
  56.5 0.9 exponential_reduce_fusion.2
  57.4 0.8 fusion.14
  58.2 0.9 exponential_reduce_fusion.1
  59.2 1.1 convolution_bitcast_fusion.3
  60.2 1.1 scatter-add.25
  61.3 3.0 %fusion.49 = f32[2048,1,128]{2,0,1:T(8,128)} fusion(f32[2048,1,128]{2,0,1:T(8,128)} %scatter-add.25, bf16[256,4,128]{0,2,1:T(8,128)(2,1)S(1)} %bitcast.552, f32[1024,256,4]{1,0,2:T(8,128)S(1)} %get-tuple-element.213, f32[4,256]{1,0:T(4,128)S(1)} %log_add_fusion.2, pred[256,1024]{0,1:T(8,128)(4,1)S(1)} %copy-done.6), kind=kOutput, calls=%fused_computation.61 | convolution fusion | flops 272760832 | bytes 5771264 | tf_op jit(solution)/shard_map/grtn,tgrd->ngd/dot_general | solution.py:46
  64.3 3.0 %fusion.51 = f32[2048,1,128]{2,0,1:T(8,128)} fusion(f32[2048,1,128]{2,0,1:T(8,128)} %fusion.49, bf16[256,4,128]{0,2,1:T(8,128)(2,1)S(1)} %bitcast.549, f32[1024,256,4]{1,0,2:T(8,128)S(1)} %get-tuple-element.211, f32[4,256]{1,0:T(4,128)S(1)} %log_add_fusion.1, pred[256,1024]{0,1:T(8,128)(4,1)S(1)} %compare_and_fusion.1), kind=kOutput, calls=%fused_computation.63 | convolution fusion | flops 272760832 | bytes 5771264 | tf_op jit(solution)/shard_map/grtn,tgrd->ngd/dot_general | solution.py:46
  67.3 1.8 %slice.473 = bf16[1024,1,128]{2,0,1:T(8,128)(2,1)} slice(f32[2048,1,128]{2,0,1:T(8,128)} %fusion.51), slice={[0:1024], [0:1], [0:128]} | slice | bytes 524288 | tf_op jit(solution)/shard_map/slice | solution.py:116
  69.1 6.0 %collective-permute-start.3 = (bf16[1024,1,128]{2,0,1:T(8,128)(2,1)}, bf16[1024,1,128]{2,0,1:T(8,128)(2,1)}, u32[]{:S(2)}, u32[]{:S(2)}) collective-permute-start(bf16[1024,1,128]{2,0,1:T(8,128)(2,1)} %slice.473), channel_id=1, source_target_pairs={{8,0},{16,8},{24,16},{32,24},{40,32},{48,40},{56,48},{64,56},{72,6... | collective-permute-start | bytes 786440 | tf_op jit(solution)/shard_map/ppermute | solution.py:14
  75.1 0.8 fusion.15
  75.9 0.9 exponential_reduce_fusion
  76.8 2.0 %fusion.136 = (f32[256,4]{0,1:T(4,128)S(1)}, bf16[256,1,4,128]{0,3,2,1:T(8,128)(2,1)}) fusion(bf16[256,1,4,128]{0,3,2,1:T(8,128)(2,1)S(1)} %bitcast.556, f32[1024,256,4]{1,0,2:T(8,128)S(1)} %get-tuple-element.215, f32[4,256]{1,0:T(4,128)S(1)} %log_add_fusion.3, pred[256,1024]{0,1:T(8,128)(4,1)S(1)} %copy-done.7, bf16[2048,1,128]{0,2,1:T(8,128)(2,1)S(1)} %copy-done.18), kind=kOutput, calls=%fused_computation.118 | convolution fusion | flops 273284096 | bytes 5251072 | tf_op jit(solution)/shard_map/grtn,ngd->tgrd/dot_general | solution.py:29
  78.8 1.4 %fusion.7 = bf16[1,4,256,1024]{2,3,1,0:T(8,128)(2,1)S(1)} fusion(f32[1024,256,4]{1,0,2:T(8,128)S(1)} %get-tuple-element.215, bf16[256,4,128]{0,2,1:T(8,128)(2,1)S(1)} %bitcast.557, f32[4,256]{1,0:T(4,128)S(1)} %bitcast.560, f32[4,256]{1,0:T(4,128)S(1)} %log_add_fusion.3, pred[256,1024]{0,1:T(8,128)(4,1)S(1)} %copy-done.7, ...), kind=kOutput, calls=%fused_computation.11 | convolution fusion | flops 274726912 | bytes 7086080 | tf_op jit(solution)/shard_map/tgrd,ngd->grtn/dot_general | solution.py:34
  80.2 0.7 fusion.86
  81.0 1.9 %fusion.135 = (f32[256,4]{0,1:T(4,128)S(1)}, bf16[256,1,4,128]{0,3,2,1:T(8,128)(2,1)}) fusion(bf16[256,1,4,128]{0,3,2,1:T(8,128)(2,1)S(1)} %bitcast.553, f32[1024,256,4]{1,0,2:T(8,128)S(1)} %get-tuple-element.213, f32[4,256]{1,0:T(4,128)S(1)} %log_add_fusion.2, pred[256,1024]{0,1:T(8,128)(4,1)S(1)} %copy-done.6, bf16[2048,1,128]{0,2,1:T(8,128)(2,1)S(1)} %copy-done.18), kind=kOutput, calls=%fused_computation.116 | convolution fusion | flops 273284096 | bytes 5251072 | tf_op jit(solution)/shard_map/grtn,ngd->tgrd/dot_general | solution.py:29
  82.9 1.4 %fusion.5 = bf16[1,4,256,1024]{2,3,1,0:T(8,128)(2,1)S(1)} fusion(f32[1024,256,4]{1,0,2:T(8,128)S(1)} %get-tuple-element.213, bf16[256,4,128]{0,2,1:T(8,128)(2,1)S(1)} %bitcast.554, f32[4,256]{1,0:T(4,128)S(1)} %bitcast.561, f32[4,256]{1,0:T(4,128)S(1)} %log_add_fusion.2, pred[256,1024]{0,1:T(8,128)(4,1)S(1)} %copy-done.6, ...), kind=kOutput, calls=%fused_computation.8 | convolution fusion | flops 274726912 | bytes 7086080 | tf_op jit(solution)/shard_map/tgrd,ngd->grtn/dot_general | solution.py:34
  84.3 1.9 %fusion.134 = (f32[256,4]{0,1:T(4,128)S(1)}, bf16[256,1,4,128]{0,3,2,1:T(8,128)(2,1)}) fusion(bf16[256,1,4,128]{0,3,2,1:T(8,128)(2,1)S(1)} %bitcast.550, f32[1024,256,4]{1,0,2:T(8,128)S(1)} %get-tuple-element.211, f32[4,256]{1,0:T(4,128)S(1)} %log_add_fusion.1, pred[256,1024]{0,1:T(8,128)(4,1)S(1)} %compare_and_fusion.1, ...), kind=kOutput, calls=%fused_computation.114 | convolution fusion | flops 273284096 | bytes 5251072 | tf_op jit(solution)/shard_map/grtn,ngd->tgrd/dot_general | solution.py:29
  86.2 1.4 %fusion.3 = bf16[1,4,256,1024]{2,3,1,0:T(8,128)(2,1)S(1)} fusion(f32[1024,256,4]{1,0,2:T(8,128)S(1)} %get-tuple-element.211, bf16[256,4,128]{0,2,1:T(8,128)(2,1)S(1)} %bitcast.551, f32[4,256]{1,0:T(4,128)S(1)} %bitcast.559, f32[4,256]{1,0:T(4,128)S(1)} %log_add_fusion.1, pred[256,1024]{0,1:T(8,128)(4,1)S(1)} %compare_and_fusion.1, ...), kind=kOutput, calls=%fused_computation.5 | convolution fusion | flops 274726912 | bytes 7086080 | tf_op jit(solution)/shard_map/tgrd,ngd->grtn/dot_general | solution.py:34
  87.7 0.7 fusion.92
  88.4 0.7 fusion.98
  89.2 0.8 slice.474
  89.9 2.7 %collective-permute-start.2 = (bf16[1024,1,128]{2,0,1:T(8,128)(2,1)}, bf16[1024,1,128]{2,0,1:T(8,128)(2,1)}, u32[]{:S(2)}, u32[]{:S(2)}) collective-permute-start(bf16[1024,1,128]{2,0,1:T(8,128)(2,1)} %slice.474), channel_id=1, source_target_pairs={{8,0},{16,8},{24,16},{32,24},{40,32},{48,40},{56,48},{64,56},{72,6... | collective-permute-start | bytes 786440 | tf_op jit(solution)/shard_map/ppermute | solution.py:14
  92.6 1.8 %fusion.133 = (f32[256,4]{0,1:T(4,128)S(1)}, bf16[256,1,4,128]{0,3,2,1:T(8,128)(2,1)}) fusion(bf16[256,1,4,128]{0,3,2,1:T(8,128)(2,1)S(1)} %bitcast.544, bf16[1024,128,1]{1,0,2:T(8,128)(2,1)S(1)} %bitcast.547, f32[1024,256,4]{1,0,2:T(8,128)S(1)} %get-tuple-element.209, f32[4,256]{1,0:T(4,128)S(1)} %log_add_fusion, pred[256,1024]{0,1:T(8,128)(4,1)S(1)} %compare_and_fusion), kind=kOutput, calls=%fused_computation.112 | convolution fusion | flops 273284096 | bytes 5251072 | tf_op jit(solution)/shard_map/grtn,ngd->tgrd/dot_general | solution.py:29
  94.5 1.3 %fusion.1 = bf16[1,4,256,1024]{2,3,1,0:T(8,128)(2,1)S(1)} fusion(f32[1024,256,4]{1,0,2:T(8,128)S(1)} %get-tuple-element.209, bf16[1024,128,1]{1,0,2:T(8,128)(2,1)S(1)} %bitcast.548, bf16[256,4,128]{0,2,1:T(8,128)(2,1)S(1)} %bitcast.545, f32[4,256]{1,0:T(4,128)S(1)} %bitcast.562, f32[4,256]{1,0:T(4,128)S(1)} %log_add_fusion, ...), kind=kOutput, calls=%fused_computation.2 | convolution fusion | flops 274726912 | bytes 7086080 | tf_op jit(solution)/shard_map/tgrd,ngd->grtn/dot_general | solution.py:34
  95.8 0.5 fusion.125
  96.3 0.5 fusion.116
  96.8 0.5 fusion.119
  97.3 0.5 fusion.122
  98.0 1.3 %copy.153 = bf16[1024,512]{1,0:T(8,128)(2,1)} copy(bf16[1024,512]{0,1:T(8,128)(2,1)S(1)} %bitcast.533) | data formatting | bytes 2097152
  99.3 1.2 %pad_maximum_fusion = bf16[1024,1,4,128]{0,3,2,1:T(8,128)(2,1)S(1)} fusion(bf16[256,1,4,128]{0,3,2,1:T(8,128)(2,1)} %get-tuple-element.217, bf16[256,1,4,128]{0,3,2,1:T(8,128)(2,1)} %get-tuple-element.219, bf16[256,1,4,128]{0,3,2,1:T(8,128)(2,1)S(1)} %copy-done.16, bf16[256,1,4,128]{0,3,2,1:T(8,128)(2,1)S(1)} %copy-done.15), kind=kLoop, calls=%fused_computation.98 | loop fusion | flops 4194304 | bytes 2097152 | tf_op jit(solution)/shard_map/concatenate | solution.py:122
  100.5 1.3 %copy.152 = bf16[1024,512]{1,0:T(8,128)(2,1)} copy(bf16[1024,512]{0,1:T(8,128)(2,1)S(1)} %bitcast.534) | data formatting | bytes 2097152
  101.8 4.3 %fusion.138 = bf16[1024,128]{1,0:T(8,128)(2,1)} fusion(bf16[1024,1,128]{2,0,1:T(8,128)(2,1)} %collective-permute-done.3, bf16[256,4,128]{0,2,1:T(8,128)(2,1)S(1)} %bitcast.546, f32[1024,256,4]{1,0,2:T(8,128)} %copy-done.1, f32[4,256]{1,0:T(4,128)S(1)} %log_add_fusion, pred[256,1024]{0,1:T(8,128)(4,1)S(1)} %compare_and_fusion, f32[2048,1,128]{2,0,1:T(8,128)} %fusion.51), kind=kOutput, calls=%fused_computation.122 | convolution fusion | flops 273154048 | bytes 5771264 | tf_op jit(solution)/shard_map/grtn,tgrd->ngd/dot_general | solution.py:46
  106.1 2.4 %fusion.137 = bf16[1024,128]{1,0:T(8,128)(2,1)} fusion(bf16[1024,1,128]{2,0,1:T(8,128)(2,1)} %collective-permute-done.2, bf16[256,4,128]{2,0,1:T(8,128)(2,1)S(1)} %bitcast.537, bf16[1,4,256,1024]{2,3,1,0:T(8,128)(2,1)S(1)} %copy-done.5, f32[2048,1,128]{2,0,1:T(8,128)S(1)} %fusion.98), kind=kOutput, calls=%fused_computation.121 | convolution fusion | flops 269090816 | bytes 3407872 | tf_op jit(solution)/shard_map/grtn,tgrd->ngd/dot_general | solution.py:43
  (62 shorter events, 1.0 us)
Async XLA Ops:
  0.6 1.0 copy-start
  0.6 16.4 %copy-start.8 = (bf16[1024,512]{1,0:T(8,128)(2,1)S(1)}, bf16[1024,512]{1,0:T(8,128)(2,1)}, u32[]{:S(2)}) copy-start(bf16[1024,512]{1,0:T(8,128)(2,1)} %param.38) | copy-start | bytes 3145732
  1.6 15.5 %copy-start.9 = (bf16[128,1024]{1,0:T(8,128)(2,1)S(1)}, bf16[128,1024]{1,0:T(8,128)(2,1)}, u32[]{:S(2)}) copy-start(bf16[128,1024]{1,0:T(8,128)(2,1)} %param.37) | copy-start | bytes 786436
  2.3 17.0 %all-to-all-start.1 = ((bf16[128,8,128]{2,0,1:T(8,128)(2,1)}), bf16[128,8,128]{2,0,1:T(8,128)(2,1)S(1)}, u32[]{:S(2)}, u32[]{:S(2)}) async-start(bf16[128,8,128]{2,0,1:T(8,128)(2,1)} %copy_bitcast_fusion.1), calls=%async_computation.1 | async-start | bytes 524288 | tf_op jit(solution)/shard_map/all_to_all | solution.py:59
  19.3 10.9 %all-to-all-start = ((bf16[128,8,128]{0,2,1:T(8,128)(2,1)}), bf16[128,8,128]{0,2,1:T(8,128)(2,1)S(1)}, u32[]{:S(2)}, u32[]{:S(2)}) async-start(bf16[128,8,128]{0,2,1:T(8,128)(2,1)} %bitcast), calls=%async_computation | async-start | bytes 524288 | tf_op jit(solution)/shard_map/all_to_all | solution.py:60
  30.2 19.4 %all-to-all-start.2 = ((bf16[128,32,128]{0,2,1:T(8,128)(2,1)}), bf16[128,32,128]{0,2,1:T(8,128)(2,1)S(1)}, u32[]{:S(2)}, u32[]{:S(2)}) async-start(bf16[128,32,128]{0,2,1:T(8,128)(2,1)} %bitcast.19), calls=%async_computation.2 | async-start | bytes 2097152 | tf_op jit(solution)/shard_map/all_to_all | solution.py:58
  35.9 11.3 %collective-permute-start = (bf16[1024,1,128]{0,2,1:T(8,128)(2,1)}, bf16[1024,1,128]{0,2,1:T(8,128)(2,1)}, u32[]{:S(2)}, u32[]{:S(2)}) collective-permute-start(bf16[1024,1,128]{0,2,1:T(8,128)(2,1)} %copy_bitcast_fusion), channel_id=1, source_target_pairs={{0,8},{8,16},{16,24},{24,32},{32,40},{40,48},{48,56},{56,64},{64,7... | collective-permute-start | bytes 786440 | tf_op jit(solution)/shard_map/ppermute | solution.py:14
  43.0 9.9 %collective-permute-start.1 = (bf16[1024,1,128]{2,0,1:T(8,128)(2,1)S(1)}, bf16[1024,1,128]{2,0,1:T(8,128)(2,1)S(1)}, u32[]{:S(2)}, u32[]{:S(2)}) collective-permute-start(bf16[1024,1,128]{2,0,1:T(8,128)(2,1)S(1)} %bitcast.523), channel_id=1, source_target_pairs={{0,8},{8,16},{16,24},{24,32},{32,40},{40,48},{48,56},{56,64},{64,7... | collective-permute-start | bytes 786440 | tf_op jit(solution)/shard_map/ppermute | solution.py:14
  48.1 0.8 copy-start.17
  50.3 4.4 %copy-start.7 = (pred[256,1024]{0,1:T(8,128)(4,1)S(1)}, pred[256,1024]{0,1:T(8,128)(4,1)}, u32[]{:S(2)}) copy-start(pred[256,1024]{0,1:T(8,128)(4,1)} %fusion.132) | copy-start | bytes 786436
  52.9 2.7 %copy-start.6 = (pred[256,1024]{0,1:T(8,128)(4,1)S(1)}, pred[256,1024]{0,1:T(8,128)(4,1)}, u32[]{:S(2)}) copy-start(pred[256,1024]{0,1:T(8,128)(4,1)} %compare_and_fusion.2) | copy-start | bytes 786436
  57.4 1.7 %copy-start.14 = (bf16[256,512]{0,1:T(8,128)(2,1)S(1)}, bf16[256,512]{0,1:T(8,128)(2,1)}, u32[]{:S(2)}) copy-start(bf16[256,512]{0,1:T(8,128)(2,1)} %copy.184) | copy-start | bytes 786436
  59.1 2.2 %copy-start.13 = (bf16[256,512]{0,1:T(8,128)(2,1)S(1)}, bf16[256,512]{0,1:T(8,128)(2,1)}, u32[]{:S(2)}) copy-start(bf16[256,512]{0,1:T(8,128)(2,1)} %copy.185) | copy-start | bytes 786436
  60.2 4.1 %copy-start.12 = (bf16[256,512]{0,1:T(8,128)(2,1)S(1)}, bf16[256,512]{0,1:T(8,128)(2,1)}, u32[]{:S(2)}) copy-start(bf16[256,512]{0,1:T(8,128)(2,1)} %copy.186) | copy-start | bytes 786436
  69.1 32.7 %collective-permute-start.3 = (bf16[1024,1,128]{2,0,1:T(8,128)(2,1)}, bf16[1024,1,128]{2,0,1:T(8,128)(2,1)}, u32[]{:S(2)}, u32[]{:S(2)}) collective-permute-start(bf16[1024,1,128]{2,0,1:T(8,128)(2,1)} %slice.473), channel_id=1, source_target_pairs={{8,0},{16,8},{24,16},{32,24},{40,32},{48,40},{56,48},{64,56},{72,6... | collective-permute-start | bytes 786440 | tf_op jit(solution)/shard_map/ppermute | solution.py:14
  75.1 1.7 %copy-start.2 = (bf16[2,128,4,128]{3,1,0,2:T(8,128)(2,1)}, bf16[2,128,4,128]{3,1,0,2:T(8,128)(2,1)S(1)}, u32[]{:S(2)}) copy-start(bf16[2,128,4,128]{3,1,0,2:T(8,128)(2,1)S(1)} %copy.125) | copy-start | bytes 786436
  75.1 1.7 %copy-start.18 = (bf16[2048,1,128]{0,2,1:T(8,128)(2,1)S(1)}, bf16[2048,1,128]{0,2,1:T(8,128)(2,1)}, u32[]{:S(2)}) copy-start(bf16[2048,1,128]{0,2,1:T(8,128)(2,1)} %copy-done.17) | copy-start | bytes 1572868
  75.9 18.6 %copy-start.1 = (f32[1024,256,4]{1,0,2:T(8,128)}, f32[1024,256,4]{1,0,2:T(8,128)S(1)}, u32[]{:S(2)}) copy-start(f32[1024,256,4]{1,0,2:T(8,128)S(1)} %get-tuple-element.209) | copy-start | bytes 12582916
  87.6 5.0 %copy-start.10 = (bf16[256,512]{0,1:T(8,128)(2,1)S(1)}, bf16[256,512]{0,1:T(8,128)(2,1)}, u32[]{:S(2)}) copy-start(bf16[256,512]{0,1:T(8,128)(2,1)} %copy.187) | copy-start | bytes 786436
  87.7 5.0 %copy-start.11 = (bf16[8,128,1,128]{3,1,0,2:T(8,128)(2,1)S(1)}, bf16[8,128,1,128]{3,1,0,2:T(8,128)(2,1)}, u32[]{:S(2)}) copy-start(bf16[8,128,1,128]{3,1,0,2:T(8,128)(2,1)} %copy.126) | copy-start | bytes 786436
  89.9 16.2 %collective-permute-start.2 = (bf16[1024,1,128]{2,0,1:T(8,128)(2,1)}, bf16[1024,1,128]{2,0,1:T(8,128)(2,1)}, u32[]{:S(2)}, u32[]{:S(2)}) collective-permute-start(bf16[1024,1,128]{2,0,1:T(8,128)(2,1)} %slice.474), channel_id=1, source_target_pairs={{8,0},{16,8},{24,16},{32,24},{40,32},{48,40},{56,48},{64,56},{72,6... | collective-permute-start | bytes 786440 | tf_op jit(solution)/shard_map/ppermute | solution.py:14
  95.8 1.5 %copy-start.4 = (bf16[1,4,256,1024]{2,3,1,0:T(8,128)(2,1)}, bf16[1,4,256,1024]{2,3,1,0:T(8,128)(2,1)S(1)}, u32[]{:S(2)}) copy-start(bf16[1,4,256,1024]{2,3,1,0:T(8,128)(2,1)S(1)} %fusion.1) | copy-start | bytes 6291460
  97.8 1.5 %copy-start.15 = (bf16[256,1,4,128]{0,3,2,1:T(8,128)(2,1)S(1)}, bf16[256,1,4,128]{0,3,2,1:T(8,128)(2,1)}, u32[]{:S(2)}) copy-start(bf16[256,1,4,128]{0,3,2,1:T(8,128)(2,1)} %get-tuple-element.223) | copy-start | bytes 786436
  97.8 1.5 %copy-start.16 = (bf16[256,1,4,128]{0,3,2,1:T(8,128)(2,1)S(1)}, bf16[256,1,4,128]{0,3,2,1:T(8,128)(2,1)}, u32[]{:S(2)}) copy-start(bf16[256,1,4,128]{0,3,2,1:T(8,128)(2,1)} %get-tuple-element.221) | copy-start | bytes 786436
  101.8 4.3 %copy-start.3 = (bf16[2,128,4,128]{3,1,0,2:T(8,128)(2,1)S(1)}, bf16[2,128,4,128]{3,1,0,2:T(8,128)(2,1)}, u32[]{:S(2)}) copy-start(bf16[2,128,4,128]{3,1,0,2:T(8,128)(2,1)} %copy-done.2) | copy-start | bytes 786436
  101.8 4.3 %copy-start.5 = (bf16[1,4,256,1024]{2,3,1,0:T(8,128)(2,1)S(1)}, bf16[1,4,256,1024]{2,3,1,0:T(8,128)(2,1)}, u32[]{:S(2)}) copy-start(bf16[1,4,256,1024]{2,3,1,0:T(8,128)(2,1)} %copy-done.4) | copy-start | bytes 6291460
where the time goes:
time: 109 us
  matrix products  35.2 us (32%)
  starting transfers between devices  30 us (28%)
  local copies, waits for them, and re-layouts  20.3 us (19%)
  other arithmetic  13.8 us (13%)
  waiting for transfers between devices  8.2 us (8%)
  between operations  1.13 us (1%)
    ppermute x4, starting transfers between devices, from_behind(): return lax.ppermute(block, axis, route)  15.3 us
    unnamed x47, local copies, waits for them, and re-layouts  11.9 us
    dot_general x4, matrix products, tile_grads(): jnp.einsum('grtn,tgrd->ngd', weights_low, grad_tile, preferred_element_ty...  11.3 us
    dot_general x4, matrix products, tile_grads(): jnp.einsum('grtn,ngd->tgrd', weights_low, value_rows, preferred_element_t...  7.66 us
    gather x1, other arithmetic, local(): jnp.repeat(prior_units, unit_rows, total_repeat_length=ctx_rows)  5.7 us
    dot_general x4, matrix products, tile_grads(): jnp.einsum('tgrd,ngd->grtn', grad_tile, value_rows, preferred_element_typ...  5.49 us
    all_to_all x1, waiting for transfers between devices, local(): lax.all_to_all(heads_of_values, 'head', split_axis=1, concat_axis=0, tile...  5 us
    all_to_all x1, starting transfers between devices, local(): lax.all_to_all(query_heads, 'head', split_axis=1, concat_axis=0, tiled=True)  4.93 us
  transfers between devices with their start and end apart: 7, of which 3 were waited for; matrix products, arithmetic and copies ran while one was open for 44% of the time, Pallas kernels for 0%

commit v1 on v0

--- a/solution.py
+++ b/solution.py
@@ -51,20 +51,30 @@
 
 def local(query_matrix, key_matrix, value_matrix, output_gradient, doc_start):
     token_per_shard = query_matrix.shape[0]
-    query_heads = query_matrix.reshape(token_per_shard, QUERY_HEADS, HEAD_SIZE)
-    heads_of_keys = key_matrix.reshape(token_per_shard, KEY_VALUE_HEADS, HEAD_SIZE)
-    heads_of_values = value_matrix.reshape(token_per_shard, KEY_VALUE_HEADS, HEAD_SIZE)
-    query_array, own_keys, own_values = (
-        lax.all_to_all(query_heads, "head", split_axis=1, concat_axis=0, tiled=True),
-        lax.all_to_all(heads_of_keys, "head", split_axis=1, concat_axis=0, tiled=True),
-        lax.all_to_all(heads_of_values, "head", split_axis=1, concat_axis=0, tiled=True),
+    head_groups = lax.axis_size("head")
+    q_cols = query_matrix.shape[1] // head_groups
+    k_cols = key_matrix.shape[1] // head_groups
+    packed = jnp.concatenate(
+        [
+            query_matrix.reshape(token_per_shard, head_groups, q_cols),
+            key_matrix.reshape(token_per_shard, head_groups, k_cols),
+            value_matrix.reshape(token_per_shard, head_groups, k_cols),
+        ],
+        axis=2,
     )
-    ctx_rows = own_keys.shape[0]
+    packed = lax.all_to_all(packed, "head", split_axis=1, concat_axis=0, tiled=True)
+    ctx_rows = packed.shape[0]
+    packed = packed.reshape(ctx_rows, q_cols + 2 * k_cols)
+    kv_local = k_cols // HEAD_SIZE
+    heads_per_group = q_cols // k_cols
+    query_array = packed[:, :q_cols].reshape(ctx_rows, kv_local, heads_per_group, HEAD_SIZE)
+    own_kv = packed[:, q_cols:]
+    own_keys = own_kv[:, :k_cols].reshape(ctx_rows, kv_local, HEAD_SIZE)
+    own_values = own_kv[:, k_cols:].reshape(ctx_rows, kv_local, HEAD_SIZE)
     unit_rows = 2 * token_per_shard
-    earlier_keys, earlier_values = from_behind((own_keys, own_values), "ctx", 1)
-    kv_local = own_keys.shape[1]
-    heads_per_group = query_array.shape[1] // kv_local
-    query_array = query_array.reshape(ctx_rows, kv_local, heads_per_group, HEAD_SIZE)
+    earlier_kv = from_behind(own_kv, "ctx", 1)
+    earlier_keys = earlier_kv[:, :k_cols].reshape(ctx_rows, kv_local, HEAD_SIZE)
+    earlier_values = earlier_kv[:, k_cols:].reshape(ctx_rows, kv_local, HEAD_SIZE)
     gradient_per_head = output_gradient.reshape(ctx_rows, kv_local, heads_per_group, HEAD_SIZE)
     per_shard = ctx_rows // unit_rows
     ctx_index = lax.axis_index("ctx")
@@ -75,9 +85,7 @@
     )
     prior_units = jnp.where(ctx_index > 0, prior_units, -1)
     own_doc = jnp.repeat(own_units, unit_rows, total_repeat_length=ctx_rows)
-    prior_doc = jnp.repeat(prior_units, unit_rows, total_repeat_length=ctx_rows)[
-        ctx_rows - ctx_rows :
-    ]
+    prior_doc = jnp.repeat(prior_units, unit_rows, total_repeat_length=ctx_rows)
     joined_keys = jnp.concatenate([earlier_keys, own_keys], axis=0)
     joined_values = jnp.concatenate([earlier_values, own_values], axis=0)
     joined_doc = jnp.concatenate([prior_doc, own_doc], axis=0)
@@ -111,14 +119,18 @@
         query_grads.append(grad_query)
         key_grad = key_grad.at[window_start:window_end].add(grad_key)
         value_grad = value_grad.at[window_start:window_end].add(grad_value)
-    later_keys, later_values = (
-        from_behind(key_grad[:ctx_rows].astype(jnp.bfloat16), "ctx", -1).astype(jnp.float32),
-        from_behind(value_grad[:ctx_rows].astype(jnp.bfloat16), "ctx", -1).astype(jnp.float32),
+    prior_grads = jnp.concatenate(
+        [
+            key_grad[:ctx_rows].astype(jnp.bfloat16).reshape(ctx_rows, k_cols),
+            value_grad[:ctx_rows].astype(jnp.bfloat16).reshape(ctx_rows, k_cols),
+        ],
+        axis=1,
     )
-    key_own = key_grad[ctx_rows:].at[ctx_rows - ctx_rows :].add(later_keys)
-    value_own = value_grad[ctx_rows:].at[ctx_rows - ctx_rows :].add(later_values)
-    summed_keys = key_own.astype(jnp.bfloat16).reshape(ctx_rows, kv_local * HEAD_SIZE)
-    summed_values = value_own.astype(jnp.bfloat16).reshape(ctx_rows, kv_local * HEAD_SIZE)
+    later = from_behind(prior_grads, "ctx", -1).astype(jnp.float32)
+    key_own = key_grad[ctx_rows:].reshape(ctx_rows, k_cols) + later[:, :k_cols]
+    value_own = value_grad[ctx_rows:].reshape(ctx_rows, k_cols) + later[:, k_cols:]
+    summed_keys = key_own.astype(jnp.bfloat16)
+    summed_values = value_own.astype(jnp.bfloat16)
     attended_all = jnp.concatenate(pieces, axis=0).reshape(
         ctx_rows, kv_local * heads_per_group * HEAD_SIZE
     )

time: 109 us -> 102 us (0.936)
  the two profiles are of different devices: /device:TPU:138 before, /device:TPU:102 now
where the time goes in v1:
time: 102 us; the launch traced here: 101 us
  matrix products  32 us (31%)
  local copies, waits for them, and re-layouts  21.8 us (21%)
  waiting for transfers between devices  19.1 us (19%)
  other arithmetic  15.4 us (15%)
  starting transfers between devices  11.8 us (12%)
  between operations  1.19 us (1%)
    ppermute x2, waiting for transfers between devices, from_behind(): return lax.ppermute(block, axis, route)  11.4 us
    unnamed x40, local copies, waits for them, and re-layouts  9.71 us
    all_to_all x1, waiting for transfers between devices, local(): lax.all_to_all(packed, 'head', split_axis=1, concat_axis=0, tiled=True)  7.72 us
    dot_general x4, matrix products, tile_grads(): jnp.einsum('grtn,ngd->tgrd', weights_low, value_rows, preferred_element_t...  7.66 us
    dot_general x4, matrix products, tile_grads(): jnp.einsum('grtn,tgrd->ngd', weights_low, grad_tile, preferred_element_ty...  7.63 us
    ppermute x2, starting transfers between devices, from_behind(): return lax.ppermute(block, axis, route)  7.29 us
    dot_general x4, matrix products, tile_grads(): jnp.einsum('tgrd,ngd->grtn', grad_tile, value_rows, preferred_element_typ...  6.65 us
    gather x1, other arithmetic, local(): prior_doc = jnp.repeat(prior_units, unit_rows, total_repeat_length=ctx_rows)  5.04 us
  transfers between devices with their start and end apart: 3, of which 2 were waited for; matrix products, arithmetic and copies ran while one was open for 32% of the time, Pallas kernels for 0%

profile of v1, /device:TPU:102, one launch (start us, length us, event | category | flops | bytes accessed | tf_op | source)
XLA Modules:
  0.0 101.2 jit_solution(3459865520196995552)
XLA Ops:
  0.6 1.4 %copy.156 = bf16[16,8,8,512]{3,2,0,1:T(8,128)(2,1)S(1)} copy(bf16[16,8,8,512]{3,2,1,0:T(8,128)(2,1)} %bitcast.542) | data formatting | bytes 2097152 | tf_op jit(solution)/shard_map/reshape | solution.py:59
  2.0 1.2 %copy_bitcast_fusion.1 = (bf16[128,8,128]{2,0,1:T(8,128)(2,1)S(1)}, bf16[128,8,128]{2,0,1:T(8,128)(2,1)S(1)}) fusion(bf16[128,1024]{1,0:T(8,128)(2,1)S(1)} %copy-done, bf16[128,1024]{1,0:T(8,128)(2,1)} %param.29), kind=kLoop, calls=%fused_computation.142 | loop fusion | bytes 1048576 | tf_op jit(solution)/shard_map/reshape | solution.py:61
  3.3 1.3 %pad_maximum_fusion = bf16[128,8,768]{2,0,1:T(8,128)(2,1)} fusion(bf16[128,8,128]{2,0,1:T(8,128)(2,1)S(1)} %get-tuple-element.184, bf16[128,8,128]{2,0,1:T(8,128)(2,1)S(1)} %get-tuple-element.185, bf16[128,8,512]{2,0,1:T(8,128)(2,1)S(1)} %bitcast.535), kind=kLoop, calls=%fused_computation.52 | loop fusion | flops 4718592 | bytes 3145728 | tf_op jit(solution)/shard_map/concatenate | solution.py:57
  4.5 4.5 %all-to-all-start = ((bf16[128,8,768]{2,0,1:T(8,128)(2,1)}), bf16[128,8,768]{2,0,1:T(8,128)(2,1)S(1)}, u32[]{:S(2)}, u32[]{:S(2)}) async-start(bf16[128,8,768]{2,0,1:T(8,128)(2,1)} %pad_maximum_fusion), calls=%async_computation | async-start | bytes 3145728 | tf_op jit(solution)/shard_map/all_to_all | solution.py:65
  9.2 0.2 reduce-window.9
  9.3 0.9 fusion.196
  10.2 0.1 select_reduce_fusion
  10.4 0.7 fusion.199
  11.1 5.0 %select_select_fusion.1 = (s32[1024]{0:T(1024)S(1)}, s32[1024]{0:T(1024)S(1)}) fusion(pred[1024]{0:T(1024)(128)(4,1)S(1)} %copy-done.12, pred[1024]{0:T(1024)(128)(4,1)S(1)} %copy-done.13, pred[1024]{0:T(1024)(128)(4,1)S(1)} %copy-done.14, s32[]{:T(128)} %bitcast.13, s32[]{:T(128)} %bitcast.12, s32[]{:T(128)} %bitcast.11, s32[]{:T(128)} %bitcast.10, ...), kind=kLoop, calls=%fused_computation.171 | loop fusion | flops 6144 | bytes 11296 | tf_op jit(solution)/shard_map/jit(_take)/gather | solution.py:88
  16.1 1.8 %copy.143 = bf16[256,512]{0,1:T(8,128)(2,1)} copy(bf16[256,512]{1,0:T(8,128)(2,1)} %get-tuple-element.137) | data formatting | bytes 524288
  17.9 1.8 %copy.144 = bf16[256,512]{0,1:T(8,128)(2,1)} copy(bf16[256,512]{1,0:T(8,128)(2,1)} %get-tuple-element.139) | data formatting | bytes 524288
  19.7 0.9 copy.145
  20.6 0.8 copy.146
  21.5 0.3 fusion.136
  21.8 0.3 compare_and_fusion
  22.1 0.3 compare_and_fusion.2
  22.5 0.3 compare_and_fusion.1
  22.8 7.7 %all-to-all-done = bf16[128,8,768]{2,0,1:T(8,128)(2,1)S(1)} async-done(((bf16[128,8,768]{2,0,1:T(8,128)(2,1)}), bf16[128,8,768]{2,0,1:T(8,128)(2,1)S(1)}, u32[]{:S(2)}, u32[]{:S(2)}) %all-to-all-start) | async-done | bytes 1572896 | tf_op jit(solution)/shard_map/all_to_all | solution.py:65
  30.6 0.8 slice.388
  31.4 0.9 fusion.195
  32.3 5.1 %collective-permute-start = (bf16[1024,256]{1,0:T(8,128)(2,1)}, bf16[1024,256]{1,0:T(8,128)(2,1)}, u32[]{:S(2)}, u32[]{:S(2)}) collective-permute-start(bf16[1024,256]{1,0:T(8,128)(2,1)} %slice.388), channel_id=1, source_target_pairs={{0,8},{8,16},{16,24},{24,32},{32,40},{40,48},{48,56},{56,64},{64,7... | collective-permute-start | bytes 1572872 | tf_op jit(solution)/shard_map/ppermute | solution.py:14
  37.4 1.1 %copy.149 = bf16[256,512]{0,1:T(8,128)(2,1)S(1)} copy(bf16[256,512]{1,0:T(8,128)(2,1)} %get-tuple-element.132) | data formatting | bytes 524288 | tf_op jit(solution)/shard_map/reshape.306
  38.5 0.8 fusion.15
  39.3 0.9 exponential_reduce_fusion
  40.2 1.9 %fusion.141 = (f32[256,4]{0,1:T(4,128)S(1)}, bf16[256,1,4,128]{0,3,2,1:T(8,128)(2,1)}) fusion(bf16[256,1,4,128]{0,3,2,1:T(8,128)(2,1)S(1)} %bitcast.547, f32[1024,256,4]{1,0,2:T(8,128)S(1)} %get-tuple-element.165, f32[4,256]{1,0:T(4,128)S(1)} %log_add_fusion, pred[256,1024]{0,1:T(8,128)(4,1)S(1)} %compare_and_fusion, bf16[1024,768]{1,0:T(8,128)(2,1)S(1)} %bitcast.531), kind=kOutput, calls=%fused_computation.125 | convolution fusion | flops 273284096 | bytes 5251072 | tf_op jit(solution)/shard_map/grtn,ngd->tgrd/dot_general | solution.py:29
  42.2 2.7 %fusion.1 = bf16[1,4,256,1024]{2,3,1,0:T(8,128)(2,1)} fusion(f32[1024,256,4]{1,0,2:T(8,128)S(1)} %get-tuple-element.165, bf16[256,4,128]{0,2,1:T(8,128)(2,1)S(1)} %bitcast.548, f32[4,256]{1,0:T(4,128)S(1)} %bitcast.562, f32[4,256]{1,0:T(4,128)S(1)} %log_add_fusion, pred[256,1024]{0,1:T(8,128)(4,1)S(1)} %compare_and_fusion, bf16[1024,768]{1,0:T(8,128)(2,1)S(1)} %bitcast.532), kind=kOutput, calls=%fused_computation.2 | convolution fusion | flops 274726912 | bytes 7086080 | tf_op jit(solution)/shard_map/tgrd,ngd->grtn/dot_general | solution.py:34
  44.8 1.8 %copy.59 = bf16[256,512]{0,1:T(8,128)(2,1)} copy(bf16[256,512]{1,0:T(8,128)(2,1)} %get-tuple-element.131) | data formatting | bytes 524288 | tf_op jit(solution)/shard_map/slice | solution.py:103
  46.6 0.8 copy.147
  47.4 1.1 %copy.148 = bf16[256,512]{0,1:T(8,128)(2,1)S(1)} copy(bf16[256,512]{1,0:T(8,128)(2,1)} %get-tuple-element.133) | data formatting | bytes 524288 | tf_op jit(solution)/shard_map/reshape.297
  48.5 2.1 %fusion.129 = bf16[256,1,4,128]{0,3,2,1:T(8,128)(2,1)S(1)} fusion(bf16[1,4,256,1024]{2,3,1,0:T(8,128)(2,1)} %fusion.1, bf16[1024,768]{1,0:T(8,128)(2,1)S(1)} %bitcast.533), kind=kOutput, calls=%fused_computation.96 | convolution fusion | flops 268697600 | bytes 2621440 | tf_op jit(solution)/shard_map/grtn,ngd->tgrd/dot_general | solution.py:39
  50.7 1.1 %slice_bitcast_fusion = (bf16[1024,1,128]{2,0,1:T(8,128)(2,1)S(1)}, bf16[1024,1,128]{2,0,1:T(8,128)(2,1)S(1)}) fusion(bf16[1024,256]{1,0:T(8,128)(2,1)} %collective-permute-done), kind=kLoop, calls=%fused_computation.148 | loop fusion | bytes 1048576 | tf_op jit(solution)/shard_map/reshape | solution.py:76
  51.8 0.8 fusion.12
  52.6 0.9 exponential_reduce_fusion.3
  53.5 1.3 %convolution_bitcast_fusion.3 = f32[1024,1,128]{0,2,1:T(8,128)S(1)} fusion(bf16[256,4,128]{0,2,1:T(8,128)(2,1)S(1)} %bitcast.556, f32[1024,256,4]{1,0,2:T(8,128)S(1)} %get-tuple-element.171, f32[4,256]{1,0:T(4,128)S(1)} %log_add_fusion.3, pred[256,1024]{0,1:T(8,128)(4,1)S(1)} %fusion.136), kind=kOutput, calls=%fused_computation.60 | convolution fusion | flops 272629760 | bytes 5246976 | tf_op jit(solution)/shard_map/grtn,tgrd->ngd/dot_general | solution.py:46
  54.8 1.9 %fusion.144 = (f32[256,4]{0,1:T(4,128)S(1)}, bf16[256,1,4,128]{0,3,2,1:T(8,128)(2,1)}) fusion(bf16[256,1,4,128]{0,3,2,1:T(8,128)(2,1)S(1)} %bitcast.557, f32[1024,256,4]{1,0,2:T(8,128)S(1)} %get-tuple-element.171, f32[4,256]{1,0:T(4,128)S(1)} %log_add_fusion.3, pred[256,1024]{0,1:T(8,128)(4,1)S(1)} %fusion.136, ...), kind=kOutput, calls=%fused_computation.131 | convolution fusion | flops 273808384 | bytes 5513216 | tf_op jit(solution)/shard_map/grtn,ngd->tgrd/dot_general | solution.py:29
  56.7 1.3 %fusion.7 = bf16[1,4,256,1024]{2,3,1,0:T(8,128)(2,1)S(1)} fusion(f32[1024,256,4]{1,0,2:T(8,128)S(1)} %get-tuple-element.171, bf16[256,4,128]{0,2,1:T(8,128)(2,1)S(1)} %bitcast.558, f32[4,256]{1,0:T(4,128)S(1)} %bitcast.560, f32[4,256]{1,0:T(4,128)S(1)} %log_add_fusion.3, pred[256,1024]{0,1:T(8,128)(4,1)S(1)} %fusion.136, ...), kind=kOutput, calls=%fused_computation.11 | convolution fusion | flops 275251200 | bytes 7348224 | tf_op jit(solution)/shard_map/tgrd,ngd->grtn/dot_general | solution.py:34
  58.1 0.8 fusion.87
  58.9 0.5 fusion.120
  59.4 0.8 fusion.13
  60.2 1.1 %exponential_reduce_fusion.2 = f32[4,256]{1,0:T(4,128)S(1)} fusion(f32[1024,256,4]{1,0,2:T(8,128)S(1)} %get-tuple-element.169, f32[4,256]{1,0:T(4,128)S(1)} %get-tuple-element.168, pred[256,1024]{0,1:T(8,128)(4,1)S(1)} %compare_and_fusion.2), kind=kLoop, calls=%fused_computation.21 | loop fusion | flops 4193280 | bytes 4464640 | tf_op jit(solution)/shard_map/reduce_sum | solution.py:26
  61.3 0.8 fusion.14
  62.1 0.9 exponential_reduce_fusion.1
  63.2 1.9 %fusion.143 = (f32[256,4]{0,1:T(4,128)S(1)}, bf16[256,1,4,128]{0,3,2,1:T(8,128)(2,1)}) fusion(bf16[256,1,4,128]{0,3,2,1:T(8,128)(2,1)S(1)} %bitcast.553, f32[1024,256,4]{1,0,2:T(8,128)S(1)} %get-tuple-element.169, f32[4,256]{1,0:T(4,128)S(1)} %log_add_fusion.2, pred[256,1024]{0,1:T(8,128)(4,1)S(1)} %compare_and_fusion.2, ...), kind=kOutput, calls=%fused_computation.129 | convolution fusion | flops 273808384 | bytes 5513216 | tf_op jit(solution)/shard_map/grtn,ngd->tgrd/dot_general | solution.py:29
  65.1 1.3 %fusion.5 = bf16[1,4,256,1024]{2,3,1,0:T(8,128)(2,1)S(1)} fusion(f32[1024,256,4]{1,0,2:T(8,128)S(1)} %get-tuple-element.169, bf16[256,4,128]{0,2,1:T(8,128)(2,1)S(1)} %bitcast.554, f32[4,256]{1,0:T(4,128)S(1)} %bitcast.563, f32[4,256]{1,0:T(4,128)S(1)} %log_add_fusion.2, pred[256,1024]{0,1:T(8,128)(4,1)S(1)} %compare_and_fusion.2, ...), kind=kOutput, calls=%fused_computation.8 | convolution fusion | flops 275251200 | bytes 7348224 | tf_op jit(solution)/shard_map/tgrd,ngd->grtn/dot_general | solution.py:34
  66.4 0.9 fusion.93
  67.3 1.9 %fusion.142 = (f32[256,4]{0,1:T(4,128)S(1)}, bf16[256,1,4,128]{0,3,2,1:T(8,128)(2,1)}) fusion(bf16[256,1,4,128]{0,3,2,1:T(8,128)(2,1)S(1)} %bitcast.550, f32[1024,256,4]{1,0,2:T(8,128)S(1)} %get-tuple-element.167, f32[4,256]{1,0:T(4,128)S(1)} %log_add_fusion.1, pred[256,1024]{0,1:T(8,128)(4,1)S(1)} %compare_and_fusion.1, ...), kind=kOutput, calls=%fused_computation.127 | convolution fusion | flops 273808384 | bytes 5513216 | tf_op jit(solution)/shard_map/grtn,ngd->tgrd/dot_general | solution.py:29
  69.2 1.3 %fusion.3 = bf16[1,4,256,1024]{2,3,1,0:T(8,128)(2,1)S(1)} fusion(f32[1024,256,4]{1,0,2:T(8,128)S(1)} %get-tuple-element.167, bf16[256,4,128]{0,2,1:T(8,128)(2,1)S(1)} %bitcast.551, f32[4,256]{1,0:T(4,128)S(1)} %bitcast.561, f32[4,256]{1,0:T(4,128)S(1)} %log_add_fusion.1, pred[256,1024]{0,1:T(8,128)(4,1)S(1)} %compare_and_fusion.1, ...), kind=kOutput, calls=%fused_computation.5 | convolution fusion | flops 275251200 | bytes 7348224 | tf_op jit(solution)/shard_map/tgrd,ngd->grtn/dot_general | solution.py:34
  70.5 0.9 fusion.99
  71.5 1.4 %fusion.49 = f32[2048,1,128]{0,2,1:T(8,128)S(1)} fusion(f32[2048,1,128]{0,2,1:T(8,128)S(1)} %scatter-add.25, bf16[256,4,128]{0,2,1:T(8,128)(2,1)S(1)} %bitcast.555, f32[1024,256,4]{1,0,2:T(8,128)S(1)} %get-tuple-element.169, f32[4,256]{1,0:T(4,128)S(1)} %log_add_fusion.2, pred[256,1024]{0,1:T(8,128)(4,1)S(1)} %compare_and_fusion.2), kind=kOutput, calls=%fused_computation.62 | convolution fusion | flops 272760832 | bytes 5771264 | tf_op jit(solution)/shard_map/grtn,tgrd->ngd/dot_general | solution.py:46
  72.9 1.4 %fusion.51 = f32[2048,1,128]{0,2,1:T(8,128)S(1)} fusion(f32[2048,1,128]{0,2,1:T(8,128)S(1)} %fusion.49, bf16[256,4,128]{0,2,1:T(8,128)(2,1)S(1)} %bitcast.552, f32[1024,256,4]{1,0,2:T(8,128)S(1)} %get-tuple-element.167, f32[4,256]{1,0:T(4,128)S(1)} %log_add_fusion.1, pred[256,1024]{0,1:T(8,128)(4,1)S(1)} %compare_and_fusion.1), kind=kOutput, calls=%fused_computation.64 | convolution fusion | flops 272760832 | bytes 5771264 | tf_op jit(solution)/shard_map/grtn,tgrd->ngd/dot_general | solution.py:46
  74.3 0.9 pad_maximum_fusion.3
  75.3 2.2 %collective-permute-start.1 = (bf16[1024,256]{0,1:T(8,128)(2,1)}, bf16[1024,256]{0,1:T(8,128)(2,1)}, u32[]{:S(2)}, u32[]{:S(2)}) collective-permute-start(bf16[1024,256]{0,1:T(8,128)(2,1)} %pad_maximum_fusion.3), channel_id=1, source_target_pairs={{8,0},{16,8},{24,16},{32,24},{40,32},{48,40},{56,48},{64,56},{72,6... | collective-permute-start | bytes 1572872 | tf_op jit(solution)/shard_map/ppermute | solution.py:14
  77.5 0.5 fusion.126
  77.9 0.5 fusion.123
  78.4 0.1 pad_maximum_fusion.2
  78.6 1.3 %copy.101 = bf16[1024,512]{1,0:T(8,128)(2,1)} copy(bf16[1024,512]{0,1:T(8,128)(2,1)S(1)} %bitcast.536) | data formatting | bytes 2097152
  79.9 1.3 %pad_maximum_fusion.1 = bf16[1024,1,4,128]{0,3,2,1:T(8,128)(2,1)S(1)} fusion(bf16[256,1,4,128]{0,3,2,1:T(8,128)(2,1)} %get-tuple-element.173, bf16[256,1,4,128]{0,3,2,1:T(8,128)(2,1)} %get-tuple-element.175, bf16[256,1,4,128]{0,3,2,1:T(8,128)(2,1)} %get-tuple-element.177, bf16[256,1,4,128]{0,3,2,1:T(8,128)(2,1)} %get-tuple-element.179), kind=kLoop, calls=%fused_computation.102 | loop fusion | flops 4194304 | bytes 2097152 | tf_op jit(solution)/shard_map/concatenate | solution.py:134
  81.2 1.3 %copy.100 = bf16[1024,512]{1,0:T(8,128)(2,1)} copy(bf16[1024,512]{0,1:T(8,128)(2,1)S(1)} %bitcast.537) | data formatting | bytes 2097152
  82.6 11.4 %collective-permute-done.1 = bf16[1024,256]{0,1:T(8,128)(2,1)} collective-permute-done((bf16[1024,256]{0,1:T(8,128)(2,1)}, bf16[1024,256]{0,1:T(8,128)(2,1)}, u32[]{:S(2)}, u32[]{:S(2)}) %collective-permute-start.1) | collective-permute-done | bytes 524320 | tf_op jit(solution)/shard_map/ppermute | solution.py:14
  93.9 1.1 %convert_element_type.219 = f32[1024,256]{0,1:T(8,128)S(1)} convert(bf16[1024,256]{0,1:T(8,128)(2,1)} %collective-permute-done.1) | non-fusion elementwise | flops 262144 | bytes 1572864 | tf_op jit(solution)/shard_map/convert_element_type | solution.py:129
  95.1 3.6 %fusion.137 = bf16[1024,128]{0,1:T(8,128)(2,1)S(1)} fusion(f32[1024,256]{0,1:T(8,128)S(1)} %convert_element_type.219, bf16[256,4,128]{0,2,1:T(8,128)(2,1)S(1)} %bitcast.549, f32[2048,1,128]{0,2,1:T(8,128)} %copy-done.3, f32[1024,256,4]{1,0,2:T(8,128)} %copy-done.1, f32[4,256]{1,0:T(4,128)S(1)} %log_add_fusion, pred[256,1024]{0,1:T(8,128)(4,1)S(1)} %compare_and_fusion), kind=kOutput, calls=%fused_computation.118 | convolution fusion | flops 273022976 | bytes 6033408 | tf_op jit(solution)/shard_map/grtn,tgrd->ngd/dot_general | solution.py:46
  98.7 0.8 fusion.138
  99.5 0.8 copy.103
  100.4 0.8 copy.102
  (50 shorter events, 0.6 us)
Async XLA Ops:
  0.6 1.4 %copy-start = (bf16[128,1024]{1,0:T(8,128)(2,1)S(1)}, bf16[128,1024]{1,0:T(8,128)(2,1)}, u32[]{:S(2)}) copy-start(bf16[128,1024]{1,0:T(8,128)(2,1)} %param.28) | copy-start | bytes 786436
  2.0 7.0 %copy-start.15 = (s32[128]{0:T(128)S(1)}, s32[128]{0:T(128)}, u32[]{:S(2)}) copy-start(s32[128]{0:T(128)} %param.31) | copy-start | bytes 1540
  2.0 7.3 %copy-start.4 = (bf16[1024,512]{1,0:T(8,128)(2,1)S(1)}, bf16[1024,512]{1,0:T(8,128)(2,1)}, u32[]{:S(2)}) copy-start(bf16[1024,512]{1,0:T(8,128)(2,1)} %param.30) | copy-start | bytes 3145732
  3.2 7.9 %copy-start.12 = (pred[1024]{0:T(1024)(128)(4,1)S(1)}, pred[1024]{0:T(1024)(128)(4,1)}, u32[]{:S(2)}) copy-start(pred[1024]{0:T(1024)(128)(4,1)} %constant.343) | copy-start | bytes 3076
  3.2 7.8 %copy-start.13 = (pred[1024]{0:T(1024)(128)(4,1)S(1)}, pred[1024]{0:T(1024)(128)(4,1)}, u32[]{:S(2)}) copy-start(pred[1024]{0:T(1024)(128)(4,1)} %constant.344) | copy-start | bytes 3076
  3.2 7.8 %copy-start.14 = (pred[1024]{0:T(1024)(128)(4,1)S(1)}, pred[1024]{0:T(1024)(128)(4,1)}, u32[]{:S(2)}) copy-start(pred[1024]{0:T(1024)(128)(4,1)} %constant.345) | copy-start | bytes 3076
  4.5 26.0 %all-to-all-start = ((bf16[128,8,768]{2,0,1:T(8,128)(2,1)}), bf16[128,8,768]{2,0,1:T(8,128)(2,1)S(1)}, u32[]{:S(2)}, u32[]{:S(2)}) async-start(bf16[128,8,768]{2,0,1:T(8,128)(2,1)} %pad_maximum_fusion), calls=%async_computation | async-start | bytes 3145728 | tf_op jit(solution)/shard_map/all_to_all | solution.py:65
  32.3 18.4 %collective-permute-start = (bf16[1024,256]{1,0:T(8,128)(2,1)}, bf16[1024,256]{1,0:T(8,128)(2,1)}, u32[]{:S(2)}, u32[]{:S(2)}) collective-permute-start(bf16[1024,256]{1,0:T(8,128)(2,1)} %slice.388), channel_id=1, source_target_pairs={{0,8},{8,16},{16,24},{24,32},{32,40},{40,48},{48,56},{56,64},{64,7... | collective-permute-start | bytes 1572872 | tf_op jit(solution)/shard_map/ppermute | solution.py:14
  38.5 1.7 %copy-start.7 = (bf16[256,512]{0,1:T(8,128)(2,1)S(1)}, bf16[256,512]{0,1:T(8,128)(2,1)}, u32[]{:S(2)}) copy-start(bf16[256,512]{0,1:T(8,128)(2,1)} %copy.146) | copy-start | bytes 786436
  39.3 2.9 %copy-start.1 = (f32[1024,256,4]{1,0,2:T(8,128)}, f32[1024,256,4]{1,0,2:T(8,128)S(1)}, u32[]{:S(2)}) copy-start(f32[1024,256,4]{1,0,2:T(8,128)S(1)} %get-tuple-element.165) | copy-start | bytes 12582916
  48.5 3.2 %copy-start.6 = (bf16[256,512]{0,1:T(8,128)(2,1)S(1)}, bf16[256,512]{0,1:T(8,128)(2,1)}, u32[]{:S(2)}) copy-start(bf16[256,512]{0,1:T(8,128)(2,1)} %copy.59) | copy-start | bytes 786436
  51.8 1.7 %copy-start.11 = (bf16[256,512]{0,1:T(8,128)(2,1)S(1)}, bf16[256,512]{0,1:T(8,128)(2,1)}, u32[]{:S(2)}) copy-start(bf16[256,512]{0,1:T(8,128)(2,1)} %copy.143) | copy-start | bytes 786436
  58.1 1.3 %copy-start.5 = (bf16[256,512]{0,1:T(8,128)(2,1)S(1)}, bf16[256,512]{0,1:T(8,128)(2,1)}, u32[]{:S(2)}) copy-start(bf16[256,512]{0,1:T(8,128)(2,1)} %copy.147) | copy-start | bytes 786436
  62.1 1.0 %copy-start.10 = (bf16[256,512]{0,1:T(8,128)(2,1)S(1)}, bf16[256,512]{0,1:T(8,128)(2,1)}, u32[]{:S(2)}) copy-start(bf16[256,512]{0,1:T(8,128)(2,1)} %copy.144) | copy-start | bytes 786436
  65.1 2.2 %copy-start.9 = (bf16[256,512]{0,1:T(8,128)(2,1)S(1)}, bf16[256,512]{0,1:T(8,128)(2,1)}, u32[]{:S(2)}) copy-start(bf16[256,512]{0,1:T(8,128)(2,1)} %copy.145) | copy-start | bytes 786436
  74.3 4.3 %copy-start.3 = (f32[2048,1,128]{0,2,1:T(8,128)}, f32[2048,1,128]{0,2,1:T(8,128)S(1)}, u32[]{:S(2)}) copy-start(f32[2048,1,128]{0,2,1:T(8,128)S(1)} %fusion.51) | copy-start | bytes 3145732
  75.3 18.6 %collective-permute-start.1 = (bf16[1024,256]{0,1:T(8,128)(2,1)}, bf16[1024,256]{0,1:T(8,128)(2,1)}, u32[]{:S(2)}, u32[]{:S(2)}) collective-permute-start(bf16[1024,256]{0,1:T(8,128)(2,1)} %pad_maximum_fusion.3), channel_id=1, source_target_pairs={{8,0},{16,8},{24,16},{32,24},{40,32},{48,40},{56,48},{64,56},{72,6... | collective-permute-start | bytes 1572872 | tf_op jit(solution)/shard_map/ppermute | solution.py:14
  78.6 16.5 %copy-start.8 = (bf16[256,512]{0,1:T(8,128)(2,1)S(1)}, bf16[256,512]{0,1:T(8,128)(2,1)}, u32[]{:S(2)}) copy-start(bf16[256,512]{0,1:T(8,128)(2,1)} %copy.146) | copy-start | bytes 786436
  82.6 16.1 %copy-start.2 = (bf16[1,4,256,1024]{2,3,1,0:T(8,128)(2,1)S(1)}, bf16[1,4,256,1024]{2,3,1,0:T(8,128)(2,1)}, u32[]{:S(2)}) copy-start(bf16[1,4,256,1024]{2,3,1,0:T(8,128)(2,1)} %fusion.1) | copy-start | bytes 6291460

commit v2 on v1

v2 whole, which is shorter than its diff:
```python
import jax
import jax.numpy as jnp
from jax import lax
from jax.sharding import PartitionSpec as P
import functools
from jax.experimental import pallas as pl
from jax.experimental.pallas import tpu as pltpu

QUERY_HEADS = 32
KEY_VALUE_HEADS = 8
HEAD_SIZE = 128
BLOCK = 256
INTERPRET = False


def from_behind(block, axis, distance):
    devices = range(lax.axis_size(axis))
    route = [(i - distance, i) for i in devices if i - distance in devices]
    return lax.ppermute(block, axis, route)


def _nt(a, b):
    return lax.dot_general(a, b, (((1,), (1,)), ((), ())), preferred_element_type=jnp.float32)


def _tn(a, b):
    return lax.dot_general(a, b, (((0,), (0,)), ((), ())), preferred_element_type=jnp.float32)


def _nn(a, b):
    return lax.dot_general(a, b, (((1,), (0,)), ((), ())), preferred_element_type=jnp.float32)


def attention_kernel(lo_ref, packed_ref, earlier_ref, grad_ref,
                     att_ref, dq_ref, prior_ref, own_ref,
                     s_scr, att_scr, dq_scr, *, units, heads, q_cols):
    scale = HEAD_SIZE ** (-0.5)
    prior_ref[...] = jnp.zeros(prior_ref.shape, prior_ref.dtype)
    own_ref[...] = jnp.zeros(own_ref.shape, own_ref.dtype)
    rows = heads * BLOCK
    causal = (lax.broadcasted_iota(jnp.int32, (rows, BLOCK), 0) % BLOCK
              >= lax.broadcasted_iota(jnp.int32, (rows, BLOCK), 1))

    def load_kv(ref, col0, blk):
        start = pl.multiple_of(blk * BLOCK, BLOCK)
        return (ref[pl.ds(start, BLOCK), col0:col0 + HEAD_SIZE],
                ref[pl.ds(start, BLOCK), col0 + HEAD_SIZE:col0 + 2 * HEAD_SIZE])

    for u in range(units):
        r0 = u * BLOCK
        qs = jnp.concatenate(
            [packed_ref[r0:r0 + BLOCK, h * HEAD_SIZE:(h + 1) * HEAD_SIZE] for h in range(heads)], axis=0)
        dos = jnp.concatenate(
            [grad_ref[r0:r0 + BLOCK, h * HEAD_SIZE:(h + 1) * HEAD_SIZE] for h in range(heads)], axis=0)
        lo = lo_ref[u]
        diag = units + u
        first_own = jnp.maximum(lo, units)
        segments = ((earlier_ref, 0, prior_ref, lo, units, 0),
                    (packed_ref, q_cols, own_ref, first_own, diag, units))

        def pass1(b, carry, ref, col0, off):
            m, l = carry
            k, _ = load_kv(ref, col0, b - off)
            s = _nt(qs, k) * scale
            s_scr[b - (u + 1)] = s
            m_new = jnp.maximum(m, jnp.max(s, axis=1, keepdims=True))
            l = l * jnp.exp(m - m_new) + jnp.sum(jnp.exp(s - m_new), axis=1, keepdims=True)
            return m_new, l

        carry = (jnp.full((rows, 1), -jnp.inf, jnp.float32), jnp.zeros((rows, 1), jnp.float32))
        for ref, col0, _, start, stop, off in segments:
            carry = lax.fori_loop(start, stop, functools.partial(pass1, ref=ref, col0=col0, off=off), carry)
        m, l = carry
        k_d, v_d = load_kv(packed_ref, q_cols, u)
        s = jnp.where(causal, _nt(qs, k_d) * scale, -jnp.inf)
        s_scr[units - 1] = s
        m_new = jnp.maximum(m, jnp.max(s, axis=1, keepdims=True))
        l = l * jnp.exp(m - m_new) + jnp.sum(jnp.exp(s - m_new), axis=1, keepdims=True)
        lse = m_new + jnp.log(l)

        def pass2(b, _, ref, col0, off):
            _, v = load_kv(ref, col0, b - off)
            p = jnp.exp(s_scr[b - (u + 1)] - lse)
            s_scr[b - (u + 1)] = p
            att_scr[...] += _nn(p.astype(jnp.bfloat16), v)
            return 0

        p = jnp.exp(s - lse)
        s_scr[units - 1] = p
        att_scr[...] = _nn(p.astype(jnp.bfloat16), v_d)
        for ref, col0, _, start, stop, off in segments:
            lax.fori_loop(start, stop, functools.partial(pass2, ref=ref, col0=col0, off=off), 0)
        att = att_scr[...].astype(jnp.bfloat16)
        delta = jnp.sum(dos.astype(jnp.float32) * att.astype(jnp.float32), axis=1, keepdims=True)

        def pass3(b, _, ref, col0, gref, off):
            k, v = load_kv(ref, col0, b - off)
            p = s_scr[b - (u + 1)]
            ds = (p * (_nt(dos, v) - delta)).astype(jnp.bfloat16)
            dq_scr[...] += _nn(ds, k)
            start = pl.multiple_of((b - off) * BLOCK, BLOCK)
            gref[pl.ds(start, BLOCK), 0:HEAD_SIZE] += _tn(ds, qs)
            gref[pl.ds(start, BLOCK), HEAD_SIZE:2 * HEAD_SIZE] += _tn(p.astype(jnp.bfloat16), dos)
            return 0

        ds = (p * (_nt(dos, v_d) - delta)).astype(jnp.bfloat16)
        dq_scr[...] = _nn(ds, k_d)
        own_ref[r0:r0 + BLOCK, 0:HEAD_SIZE] += _tn(ds, qs)
        own_ref[r0:r0 + BLOCK, HEAD_SIZE:2 * HEAD_SIZE] += _tn(p.astype(jnp.bfloat16), dos)
        for ref, col0, gref, start, stop, off in segments:
            lax.fori_loop(start, stop, functools.partial(pass3, ref=ref, col0=col0, gref=gref, off=off), 0)
        dq = (dq_scr[...] * scale).astype(jnp.bfloat16)
        for h in range(heads):
            att_ref[r0:r0 + BLOCK, h * HEAD_SIZE:(h + 1) * HEAD_SIZE] = att[h * BLOCK:(h + 1) * BLOCK]
            dq_ref[r0:r0 + BLOCK, h * HEAD_SIZE:(h + 1) * HEAD_SIZE] = dq[h * BLOCK:(h + 1) * BLOCK]


def attention_call(lo, packed, earlier, grad, *, heads, interpret=False):
    ctx_rows = packed.shape[0]
    units = ctx_rows // BLOCK
    q_cols = heads * HEAD_SIZE
    kv_cols = 2 * HEAD_SIZE
    vmem = pltpu.MemorySpace.VMEM
    kernel = functools.partial(attention_kernel, units=units, heads=heads, q_cols=q_cols)
    rows = heads * BLOCK
    visible_blocks = units * (units + 1) // 2 + units
    flops = 12 * rows * BLOCK * HEAD_SIZE * visible_blocks
    return pl.pallas_call(
        kernel,
        out_shape=(
            jax.ShapeDtypeStruct((ctx_rows, q_cols), jnp.bfloat16),
            jax.ShapeDtypeStruct((ctx_rows, q_cols), jnp.bfloat16),
            jax.ShapeDtypeStruct((ctx_rows, kv_cols), jnp.float32),
            jax.ShapeDtypeStruct((ctx_rows, kv_cols), jnp.float32),
        ),
        in_specs=[pl.BlockSpec(memory_space=pltpu.SMEM)] + [pl.BlockSpec(memory_space=vmem)] * 3,
        out_specs=tuple(pl.BlockSpec(memory_space=vmem) for _ in range(4)),
        scratch_shapes=[
            pltpu.VMEM((units, rows, BLOCK), jnp.float32),
            pltpu.VMEM((rows, HEAD_SIZE), jnp.float32),
            pltpu.VMEM((rows, HEAD_SIZE), jnp.float32),
        ],
        compiler_params=pltpu.CompilerParams(vmem_limit_bytes=48 * 1024 * 1024),
        cost_estimate=pl.CostEstimate(flops=flops, transcendentals=2 * rows * BLOCK * visible_blocks,
                                      bytes_accessed=8 * 1024 * 1024),
        interpret=interpret,
    )(lo, packed, earlier, grad)


def local(query_matrix, key_matrix, value_matrix, output_gradient, doc_start):
    token_per_shard = query_matrix.shape[0]
    head_groups = lax.axis_size("head")
    q_cols = query_matrix.shape[1] // head_groups
    k_cols = key_matrix.shape[1] // head_groups
    assert k_cols == HEAD_SIZE and 2 * token_per_shard == BLOCK
    packed = jnp.concatenate(
        [
            query_matrix.reshape(token_per_shard, head_groups, q_cols),
            key_matrix.reshape(token_per_shard, head_groups, k_cols),
            value_matrix.reshape(token_per_shard, head_groups, k_cols),
        ],
        axis=2,
    )
    packed = lax.all_to_all(packed, "head", split_axis=1, concat_axis=0, tiled=True)
    ctx_rows = packed.shape[0]
    packed = packed.reshape(ctx_rows, q_cols + 2 * k_cols)
    earlier_kv = from_behind(packed[:, q_cols:], "ctx", 1)
    units = ctx_rows // BLOCK
    ctx_index = lax.axis_index("ctx")
    unit_doc = jnp.cumsum(doc_start)
    own_units = lax.dynamic_slice_in_dim(unit_doc, ctx_index * units, units)
    prior_units = lax.dynamic_slice_in_dim(unit_doc, jnp.maximum(ctx_index - 1, 0) * units, units)
    prior_units = jnp.where(ctx_index > 0, prior_units, -1)
    joined_units = jnp.concatenate([prior_units, own_units])
    unit_ids = jnp.arange(units, dtype=jnp.int32)
    window = unit_ids[:, None] + 1 + unit_ids[None, :]
    same = (joined_units[window] == own_units[:, None]).astype(jnp.int32)
    lo = (unit_ids + units + 1 - jnp.sum(same, axis=1)).astype(jnp.int32)
    attended_all, query_total, prior_grads, own_grads = attention_call(
        lo, packed, earlier_kv, output_gradient, heads=q_cols // HEAD_SIZE, interpret=INTERPRET
    )
    score_scale = HEAD_SIZE ** (-0.5)
    prior_grads = jnp.concatenate(
        [(prior_grads[:, :k_cols] * score_scale).astype(jnp.bfloat16),
         prior_grads[:, k_cols:].astype(jnp.bfloat16)],
        axis=1,
    )
    later = from_behind(prior_grads, "ctx", -1).astype(jnp.float32)
    summed_keys = (own_grads[:, :k_cols] * score_scale + later[:, :k_cols]).astype(jnp.bfloat16)
    summed_values = (own_grads[:, k_cols:] + later[:, k_cols:]).astype(jnp.bfloat16)
    return (attended_all, query_total, summed_keys, summed_values)


def solution(mesh):
    placed = (
        P(("ctx", "head"), None),
        P(("ctx", "head"), None),
        P(("ctx", "head"), None),
        P("ctx", "head"),
        P(),
    )
    return jax.shard_map(
        local,
        mesh=mesh,
        in_specs=placed,
        out_specs=(P("ctx", "head"), P("ctx", "head"), P("ctx", "head"), P("ctx", "head")),
        check_vma=False,
    )
```

time: 102 us -> 88.5 us (0.87)
  matrix products: 32 us -> 0 us
  waiting for transfers between devices: 19.1 us -> 51.1 us
  local copies, waits for them, and re-layouts: 21.8 us -> 3.3 us
  Pallas kernels: 0 us -> 14.6 us
  other arithmetic: 15.4 us -> 3.05 us
  starting transfers between devices: 11.8 us -> 15.5 us
    dot_general x24 -> x0, matrix products: 32 us -> none  [the longest x4 7.66 us: tile_grads(): jnp.einsum('grtn,ngd->tgrd', weights_low, value_rows, preferred_element_t...]
    ppermute x2, waiting for transfers between devices: 11.4 us -> 30.1 us  [from_behind(): return lax.ppermute(block, axis, route)]
    pallas_call x0 -> x1, Pallas kernels: none -> 14.6 us  [attention_call(): pl.pallas_call(kernel, out_shape=(jax.ShapeDtypeStruct((ctx_rows, q_cols)...]
    all_to_all x1, waiting for transfers between devices: 7.72 us -> 20.9 us  [local(): lax.all_to_all(packed, 'head', split_axis=1, concat_axis=0, tiled=True)]
    unnamed x40 -> x8, local copies, waits for them, and re-layouts: 9.71 us -> 0.02 us
    gather x1, other arithmetic: 5.04 us -> 0.01 us  [local(): same = (joined_units[window] == own_units[:, None]).astype(jnp.int32)]
    reduce_sum x4 -> x1, other arithmetic: 3.84 us -> 0.18 us  [local(): lo = (unit_ids + units + 1 - jnp.sum(same, axis=1)).astype(jnp.int32)]
    ppermute x2, starting transfers between devices: 7.29 us -> 10.9 us  [from_behind(): return lax.ppermute(block, axis, route)]
  transfers between devices with their start and end apart: 3 -> 3, of which waited for: 2 -> 3; matrix products, arithmetic and copies ran while one was open for 32% -> 2% of each run, Pallas kernels for 0% -> 0%
where the time goes in v2:
time: 88.5 us; the launch traced here: 88.3 us
  waiting for transfers between devices  51.1 us (58%)
  starting transfers between devices  15.5 us (18%)
  Pallas kernels  14.6 us (16%)
  local copies, waits for them, and re-layouts  3.3 us (4%)
  other arithmetic  3.05 us (3%)
    ppermute x2, waiting for transfers between devices, from_behind(): return lax.ppermute(block, axis, route)  30.1 us
    all_to_all x1, waiting for transfers between devices, local(): lax.all_to_all(packed, 'head', split_axis=1, concat_axis=0, tiled=True)  20.9 us
    pallas_call x1, Pallas kernels, attention_call(): pl.pallas_call(kernel, out_shape=(jax.ShapeDtypeStruct((ctx_rows, q_cols)...  14.6 us
    ppermute x2, starting transfers between devices, from_behind(): return lax.ppermute(block, axis, route)  10.9 us
    all_to_all x1, starting transfers between devices, local(): lax.all_to_all(packed, 'head', split_axis=1, concat_axis=0, tiled=True)  4.6 us
  transfers between devices with their start and end apart: 3, of which 3 were waited for; matrix products, arithmetic and copies ran while one was open for 2% of the time, Pallas kernels for 0%

profile of v2, /device:TPU:102, one launch (start us, length us, event | category | flops | bytes accessed | tf_op | source)
XLA Modules:
  0.0 88.3 jit_solution(6436596115532170516)
XLA Ops:
  0.6 0.0 copy-start
  0.6 0.0 copy-start.2
  0.7 1.4 %copy.23 = bf16[16,8,8,512]{3,2,0,1:T(8,128)(2,1)S(1)} copy(bf16[16,8,8,512]{3,2,1,0:T(8,128)(2,1)} %bitcast.25) | data formatting | bytes 2097152 | tf_op jit(solution)/shard_map/reshape | solution.py:158
  2.0 0.0 copy-done
  2.0 0.0 copy-done.2
  2.0 0.1 copy_bitcast_fusion.1
  2.2 1.3 %pad_maximum_fusion = bf16[128,8,768]{2,0,1:T(8,128)(2,1)} fusion(bf16[128,8,128]{2,0,1:T(8,128)(2,1)S(1)} %get-tuple-element.16, bf16[128,8,128]{2,0,1:T(8,128)(2,1)S(1)} %get-tuple-element.17, bf16[128,8,512]{2,0,1:T(8,128)(2,1)S(1)} %bitcast.24), kind=kLoop, calls=%fused_computation.1 | loop fusion | flops 4718592 | bytes 3145728 | tf_op jit(solution)/shard_map/concatenate | solution.py:156
  3.5 0.0 copy-start.3
  3.5 4.6 %all-to-all-start = ((bf16[128,8,768]{2,0,1:T(8,128)(2,1)}), bf16[128,8,768]{2,0,1:T(8,128)(2,1)S(1)}, u32[]{:S(2)}, u32[]{:S(2)}) async-start(bf16[128,8,768]{2,0,1:T(8,128)(2,1)} %pad_maximum_fusion), calls=%async_computation | async-start | bytes 3145728 | tf_op jit(solution)/shard_map/all_to_all | solution.py:164
  8.1 0.1 compare_select_fusion
  8.1 0.1 reshape.82
  8.2 0.0 copy-done.3
  8.2 0.1 copy.13
  8.3 0.2 reduce-window.4
  8.5 0.1 select_reduce_fusion
  8.7 20.9 %all-to-all-done = bf16[128,8,768]{2,0,1:T(8,128)(2,1)S(1)} async-done(((bf16[128,8,768]{2,0,1:T(8,128)(2,1)}), bf16[128,8,768]{2,0,1:T(8,128)(2,1)S(1)}, u32[]{:S(2)}, u32[]{:S(2)}) %all-to-all-start) | async-done | bytes 1572896 | tf_op jit(solution)/shard_map/all_to_all | solution.py:164
  29.6 0.0 copy-start.1
  29.6 0.8 slice.31
  30.4 4.9 %collective-permute-start = (bf16[1024,256]{1,0:T(8,128)(2,1)}, bf16[1024,256]{1,0:T(8,128)(2,1)S(1)}, u32[]{:S(2)}, u32[]{:S(2)}) collective-permute-start(bf16[1024,256]{1,0:T(8,128)(2,1)} %slice.31), channel_id=1, source_target_pairs={{0,8},{8,16},{16,24},{24,32},{32,40},{40,48},{48,56},{56,64},{64,7... | collective-permute-start | bytes 1572872 | tf_op jit(solution)/shard_map/ppermute | solution.py:19
  35.4 0.1 pad_add_fusion
  35.5 0.7 gather_fusion
  36.1 0.1 reshape.81
  36.2 0.2 convert_reduce_fusion
  36.4 10.2 %collective-permute-done.earlier_ref = bf16[1024,256]{1,0:T(8,128)(2,1)S(1)} collective-permute-done((bf16[1024,256]{1,0:T(8,128)(2,1)}, bf16[1024,256]{1,0:T(8,128)(2,1)S(1)}, u32[]{:S(2)}, u32[]{:S(2)}) %collective-permute-start) | collective-permute-done | bytes 524320 | tf_op jit(solution)/shard_map/ppermute | solution.py:19
  46.6 0.0 copy-done.1
  46.6 14.6 %shard_map.84 = (bf16[1024,512]{1,0:T(8,128)(2,1)}, bf16[1024,512]{1,0:T(8,128)(2,1)}, f32[1024,256]{1,0:T(8,128)S(1)}, f32[1024,256]{1,0:T(8,128)S(1)}) custom-call(s32[4]{0:T(128)S(1)} %add_subtract_fusion.lo_ref, bf16[1024,768]{1,0:T(8,128)(2,1)S(1)} %bitcast.23, bf16[1024,256]{1,0:T(8,128)(2,1)S(1)} %collective-permute-done.earlier_ref, ...), custom_call_target="tpu_custom_call" | custom-call | flops 5637144576 | bytes 8388608 | tf_op jit(solution)/shard_map/pallas_call | solution.py:128
  61.2 0.1 pad_maximum_fusion.1
  61.3 6.0 %collective-permute-start.1 = (bf16[1024,256]{1,0:T(8,128)(2,1)S(1)}, bf16[1024,256]{1,0:T(8,128)(2,1)S(1)}, u32[]{:S(2)}, u32[]{:S(2)}) collective-permute-start(bf16[1024,256]{1,0:T(8,128)(2,1)S(1)} %pad_maximum_fusion.1), channel_id=1, source_target_pairs={{8,0},{16,8},{24,16},{32,24},{40,32},{48,40},{56,48},{64,56},{72,6... | collective-permute-start | bytes 1572872 | tf_op jit(solution)/shard_map/ppermute | solution.py:19
  67.3 20.0 %collective-permute-done.1 = bf16[1024,256]{1,0:T(8,128)(2,1)S(1)} collective-permute-done((bf16[1024,256]{1,0:T(8,128)(2,1)S(1)}, bf16[1024,256]{1,0:T(8,128)(2,1)S(1)}, u32[]{:S(2)}, u32[]{:S(2)}) %collective-permute-start.1) | collective-permute-done | bytes 524320 | tf_op jit(solution)/shard_map/ppermute | solution.py:19
  87.3 0.1 convert_element_type.18
  87.3 0.9 %fusion = (bf16[1024,128]{1,0:T(8,128)(2,1)}, bf16[1024,128]{1,0:T(8,128)(2,1)}) fusion(f32[1024,256]{1,0:T(8,128)S(1)} %convert_element_type.18, f32[1024,256]{1,0:T(8,128)S(1)} %get-tuple-element.10), kind=kLoop, calls=%fused_computation.4 | loop fusion | flops 655360 | bytes 2621440 | tf_op jit(solution)/shard_map/convert_element_type | solution.py:190
  (5 shorter events, 0.1 us)
Async XLA Ops:
  0.6 1.4 %copy-start = (bf16[128,1024]{1,0:T(8,128)(2,1)S(1)}, bf16[128,1024]{1,0:T(8,128)(2,1)}, u32[]{:S(2)}) copy-start(bf16[128,1024]{1,0:T(8,128)(2,1)} %param.6) | copy-start | bytes 786436
  0.6 1.4 %copy-start.2 = (bf16[128,1024]{1,0:T(8,128)(2,1)S(1)}, bf16[128,1024]{1,0:T(8,128)(2,1)}, u32[]{:S(2)}) copy-start(bf16[128,1024]{1,0:T(8,128)(2,1)} %param.7) | copy-start | bytes 786436
  3.5 4.8 %copy-start.3 = (s32[128]{0:T(128)S(1)}, s32[128]{0:T(128)}, u32[]{:S(2)}) copy-start(s32[128]{0:T(128)} %param.9) | copy-start | bytes 1540
  3.5 26.2 %all-to-all-start = ((bf16[128,8,768]{2,0,1:T(8,128)(2,1)}), bf16[128,8,768]{2,0,1:T(8,128)(2,1)S(1)}, u32[]{:S(2)}, u32[]{:S(2)}) async-start(bf16[128,8,768]{2,0,1:T(8,128)(2,1)} %pad_maximum_fusion), calls=%async_computation | async-start | bytes 3145728 | tf_op jit(solution)/shard_map/all_to_all | solution.py:164
  29.6 17.0 %copy-start.1 = (bf16[1024,512]{1,0:T(8,128)(2,1)S(1)}, bf16[1024,512]{1,0:T(8,128)(2,1)}, u32[]{:S(2)}) copy-start(bf16[1024,512]{1,0:T(8,128)(2,1)} %grad_ref.1) | copy-start | bytes 3145732
  30.4 16.1 %collective-permute-start = (bf16[1024,256]{1,0:T(8,128)(2,1)}, bf16[1024,256]{1,0:T(8,128)(2,1)S(1)}, u32[]{:S(2)}, u32[]{:S(2)}) collective-permute-start(bf16[1024,256]{1,0:T(8,128)(2,1)} %slice.31), channel_id=1, source_target_pairs={{0,8},{8,16},{16,24},{24,32},{32,40},{40,48},{48,56},{56,64},{64,7... | collective-permute-start | bytes 1572872 | tf_op jit(solution)/shard_map/ppermute | solution.py:19
  61.3 26.0 %collective-permute-start.1 = (bf16[1024,256]{1,0:T(8,128)(2,1)S(1)}, bf16[1024,256]{1,0:T(8,128)(2,1)S(1)}, u32[]{:S(2)}, u32[]{:S(2)}) collective-permute-start(bf16[1024,256]{1,0:T(8,128)(2,1)S(1)} %pad_maximum_fusion.1), channel_id=1, source_target_pairs={{8,0},{16,8},{24,16},{32,24},{40,32},{48,40},{56,48},{64,56},{72,6... | collective-permute-start | bytes 1572872 | tf_op jit(solution)/shard_map/ppermute | solution.py:19

commit v3 on v2

--- a/solution.py
+++ b/solution.py
@@ -31,7 +31,7 @@
     return lax.dot_general(a, b, (((1,), (0,)), ((), ())), preferred_element_type=jnp.float32)
 
 
-def attention_kernel(lo_ref, packed_ref, earlier_ref, grad_ref,
+def attention_kernel(lo_ref, packed_ref, kv_ref, earlier_ref, grad_ref,
                      att_ref, dq_ref, prior_ref, own_ref,
                      s_scr, att_scr, dq_scr, *, units, heads, q_cols):
     scale = HEAD_SIZE ** (-0.5)
@@ -55,8 +55,8 @@
         lo = lo_ref[u]
         diag = units + u
         first_own = jnp.maximum(lo, units)
-        segments = ((earlier_ref, 0, prior_ref, lo, units, 0),
-                    (packed_ref, q_cols, own_ref, first_own, diag, units))
+        segments = ((earlier_ref, 0, prior_ref, lo, units, 1),
+                    (kv_ref, 0, own_ref, first_own, diag, units))
 
         def pass1(b, carry, ref, col0, off):
             m, l = carry
@@ -71,7 +71,7 @@
         for ref, col0, _, start, stop, off in segments:
             carry = lax.fori_loop(start, stop, functools.partial(pass1, ref=ref, col0=col0, off=off), carry)
         m, l = carry
-        k_d, v_d = load_kv(packed_ref, q_cols, u)
+        k_d, v_d = load_kv(kv_ref, 0, u)
         s = jnp.where(causal, _nt(qs, k_d) * scale, -jnp.inf)
         s_scr[units - 1] = s
         m_new = jnp.maximum(m, jnp.max(s, axis=1, keepdims=True))
@@ -115,7 +115,7 @@
             dq_ref[r0:r0 + BLOCK, h * HEAD_SIZE:(h + 1) * HEAD_SIZE] = dq[h * BLOCK:(h + 1) * BLOCK]
 
 
-def attention_call(lo, packed, earlier, grad, *, heads, interpret=False):
+def attention_call(lo, packed, kv, earlier, grad, *, heads, interpret=False):
     ctx_rows = packed.shape[0]
     units = ctx_rows // BLOCK
     q_cols = heads * HEAD_SIZE
@@ -130,10 +130,10 @@
         out_shape=(
             jax.ShapeDtypeStruct((ctx_rows, q_cols), jnp.bfloat16),
             jax.ShapeDtypeStruct((ctx_rows, q_cols), jnp.bfloat16),
-            jax.ShapeDtypeStruct((ctx_rows, kv_cols), jnp.float32),
+            jax.ShapeDtypeStruct(earlier.shape, jnp.float32),
             jax.ShapeDtypeStruct((ctx_rows, kv_cols), jnp.float32),
         ),
-        in_specs=[pl.BlockSpec(memory_space=pltpu.SMEM)] + [pl.BlockSpec(memory_space=vmem)] * 3,
+        in_specs=[pl.BlockSpec(memory_space=pltpu.SMEM)] + [pl.BlockSpec(memory_space=vmem)] * 4,
         out_specs=tuple(pl.BlockSpec(memory_space=vmem) for _ in range(4)),
         scratch_shapes=[
             pltpu.VMEM((units, rows, BLOCK), jnp.float32),
@@ -144,7 +144,7 @@
         cost_estimate=pl.CostEstimate(flops=flops, transcendentals=2 * rows * BLOCK * visible_blocks,
                                       bytes_accessed=8 * 1024 * 1024),
         interpret=interpret,
-    )(lo, packed, earlier, grad)
+    )(lo, packed, kv, earlier, grad)
 
 
 def local(query_matrix, key_matrix, value_matrix, output_gradient, doc_start):
@@ -153,18 +153,21 @@
     q_cols = query_matrix.shape[1] // head_groups
     k_cols = key_matrix.shape[1] // head_groups
     assert k_cols == HEAD_SIZE and 2 * token_per_shard == BLOCK
-    packed = jnp.concatenate(
+    kv_packed = jnp.concatenate(
         [
-            query_matrix.reshape(token_per_shard, head_groups, q_cols),
             key_matrix.reshape(token_per_shard, head_groups, k_cols),
             value_matrix.reshape(token_per_shard, head_groups, k_cols),
         ],
         axis=2,
     )
-    packed = lax.all_to_all(packed, "head", split_axis=1, concat_axis=0, tiled=True)
-    ctx_rows = packed.shape[0]
-    packed = packed.reshape(ctx_rows, q_cols + 2 * k_cols)
-    earlier_kv = from_behind(packed[:, q_cols:], "ctx", 1)
+    kv = lax.all_to_all(kv_packed, "head", split_axis=1, concat_axis=0, tiled=True)
+    ctx_rows = kv.shape[0]
+    kv = kv.reshape(ctx_rows, 2 * k_cols)
+    earlier_kv = from_behind(kv[BLOCK:], "ctx", 1)
+    packed = lax.all_to_all(
+        query_matrix.reshape(token_per_shard, head_groups, q_cols),
+        "head", split_axis=1, concat_axis=0, tiled=True,
+    ).reshape(ctx_rows, q_cols)
     units = ctx_rows // BLOCK
     ctx_index = lax.axis_index("ctx")
     unit_doc = jnp.cumsum(doc_start)
@@ -177,7 +180,7 @@
     same = (joined_units[window] == own_units[:, None]).astype(jnp.int32)
     lo = (unit_ids + units + 1 - jnp.sum(same, axis=1)).astype(jnp.int32)
     attended_all, query_total, prior_grads, own_grads = attention_call(
-        lo, packed, earlier_kv, output_gradient, heads=q_cols // HEAD_SIZE, interpret=INTERPRET
+        lo, packed, kv, earlier_kv, output_gradient, heads=q_cols // HEAD_SIZE, interpret=INTERPRET
     )
     score_scale = HEAD_SIZE ** (-0.5)
     prior_grads = jnp.concatenate(
@@ -186,6 +189,7 @@
         axis=1,
     )
     later = from_behind(prior_grads, "ctx", -1).astype(jnp.float32)
+    later = jnp.concatenate([jnp.zeros((BLOCK, 2 * k_cols), jnp.float32), later], axis=0)
     summed_keys = (own_grads[:, :k_cols] * score_scale + later[:, :k_cols]).astype(jnp.bfloat16)
     summed_values = (own_grads[:, k_cols:] + later[:, k_cols:]).astype(jnp.bfloat16)
     return (attended_all, query_total, summed_keys, summed_values)

time: 88.5 us -> 78.1 us (0.88)
  waiting for transfers between devices: 51.1 us -> 31.9 us
  Pallas kernels: 14.6 us -> 22.1 us
  local copies, waits for them, and re-layouts: 3.3 us -> 5.49 us
    all_to_all x1 -> x2, waiting for transfers between devices: 20.9 us -> 9.24 us  [the longest x1 9.24 us: local(): lax.all_to_all(kv_packed, 'head', split_axis=1, concat_axis=0, tiled=True)]
    pallas_call x1, Pallas kernels: 14.6 us -> 22.1 us  [attention_call(): pl.pallas_call(kernel, out_shape=(jax.ShapeDtypeStruct((ctx_rows, q_cols)...]
    ppermute x2, waiting for transfers between devices: 30.1 us -> 22.7 us  [from_behind(): return lax.ppermute(block, axis, route)]
    ppermute x2, starting transfers between devices: 10.9 us -> 6.86 us  [from_behind(): return lax.ppermute(block, axis, route)]
    all_to_all x1 -> x2, starting transfers between devices: 4.6 us -> 8.03 us  [the longest x1 4.47 us: local(): lax.all_to_all(kv_packed, 'head', split_axis=1, concat_axis=0, tiled=True)]
    unnamed x8, local copies, waits for them, and re-layouts: 0.02 us -> 1.62 us
    reshape x1, local copies, waits for them, and re-layouts: 0.12 us -> 1.07 us  [local(): value_matrix.reshape(token_per_shard, head_groups, k_cols)]
  transfers between devices with their start and end apart: 3 -> 4, of which waited for: 3 -> 3; matrix products, arithmetic and copies ran while one was open for 2% -> 4% of each run, Pallas kernels for 0% -> 0%
where the time goes in v3:
time: 78.1 us; the launch traced here: 77.8 us
  waiting for transfers between devices  31.9 us (41%)
  Pallas kernels  22.1 us (28%)
  starting transfers between devices  14.9 us (19%)
  local copies, waits for them, and re-layouts  5.49 us (7%)
  other arithmetic  2.58 us (3%)
    ppermute x2, waiting for transfers between devices, from_behind(): return lax.ppermute(block, axis, route)  22.7 us
    pallas_call x1, Pallas kernels, attention_call(): pl.pallas_call(kernel, out_shape=(jax.ShapeDtypeStruct((ctx_rows, q_cols)...  22.1 us
    all_to_all x1, waiting for transfers between devices, local(): lax.all_to_all(kv_packed, 'head', split_axis=1, concat_axis=0, tiled=True)  9.24 us
    ppermute x2, starting transfers between devices, from_behind(): return lax.ppermute(block, axis, route)  6.86 us
    all_to_all x1, starting transfers between devices, local(): lax.all_to_all(kv_packed, 'head', split_axis=1, concat_axis=0, tiled=True)  4.47 us
    all_to_all x1, starting transfers between devices, local(): lax.all_to_all(query_matrix.reshape(token_per_shard, head_groups, q_cols)...  3.56 us
    unnamed x8, local copies, waits for them, and re-layouts  1.62 us
  transfers between devices with their start and end apart: 4, of which 3 were waited for; matrix products, arithmetic and copies ran while one was open for 4% of the time, Pallas kernels for 0%

profile of v3, /device:TPU:102, one launch (start us, length us, event | category | flops | bytes accessed | tf_op | source)
XLA Modules:
  0.0 77.8 jit_solution(6617264018969528513)
XLA Ops:
  0.6 0.0 copy-start
  0.6 0.9 %copy-done = bf16[128,1024]{1,0:T(8,128)(2,1)S(1)} copy-done((bf16[128,1024]{1,0:T(8,128)(2,1)S(1)}, bf16[128,1024]{1,0:T(8,128)(2,1)}, u32[]{:S(2)}) %copy-start) | copy-done | bytes 262168
  1.6 1.1 %copy_bitcast_fusion.1 = (bf16[128,8,128]{2,0,1:T(8,128)(2,1)S(1)}, bf16[128,8,128]{2,0,1:T(8,128)(2,1)S(1)}) fusion(bf16[128,1024]{1,0:T(8,128)(2,1)S(1)} %copy-done, bf16[128,1024]{1,0:T(8,128)(2,1)} %param.7), kind=kLoop, calls=%fused_computation.11 | loop fusion | bytes 1048576 | tf_op jit(solution)/shard_map/reshape | solution.py:159
  2.7 0.0 copy-start.2
  2.7 0.9 %pad_maximum_fusion = bf16[128,8,256]{2,0,1:T(8,128)(2,1)} fusion(bf16[128,8,128]{2,0,1:T(8,128)(2,1)S(1)} %get-tuple-element.16, bf16[128,8,128]{2,0,1:T(8,128)(2,1)S(1)} %get-tuple-element.17), kind=kLoop, calls=%fused_computation.6 | loop fusion | flops 1048576 | bytes 1048576 | tf_op jit(solution)/shard_map/concatenate | solution.py:156
  3.5 4.5 %all-to-all-start.1 = ((bf16[128,8,256]{2,0,1:T(8,128)(2,1)}), bf16[128,8,256]{2,0,1:T(8,128)(2,1)S(1)}, u32[]{:S(2)}, u32[]{:S(2)}) async-start(bf16[128,8,256]{2,0,1:T(8,128)(2,1)} %pad_maximum_fusion), calls=%async_computation.1 | async-start | bytes 1048576 | tf_op jit(solution)/shard_map/all_to_all | solution.py:163
  8.0 0.0 copy-done.2
  8.0 1.1 %copy.23 = bf16[16,8,8,512]{3,2,0,1:T(8,128)(2,1)} copy(bf16[16,8,8,512]{3,2,1,0:T(8,128)(2,1)S(1)} %bitcast.31) | data formatting | bytes 2097152 | tf_op jit(solution)/shard_map/reshape | solution.py:168
  9.1 9.2 %all-to-all-done.1 = bf16[128,8,256]{2,0,1:T(8,128)(2,1)S(1)} async-done(((bf16[128,8,256]{2,0,1:T(8,128)(2,1)}), bf16[128,8,256]{2,0,1:T(8,128)(2,1)S(1)}, u32[]{:S(2)}, u32[]{:S(2)}) %all-to-all-start.1) | async-done | bytes 524320 | tf_op jit(solution)/shard_map/all_to_all | solution.py:163
  18.3 3.6 %all-to-all-start = ((bf16[128,8,512]{2,0,1:T(8,128)(2,1)}), bf16[128,8,512]{2,0,1:T(8,128)(2,1)S(1)}, u32[]{:S(2)}, u32[]{:S(2)}) async-start(bf16[128,8,512]{2,0,1:T(8,128)(2,1)} %bitcast.27), calls=%async_computation | async-start | bytes 2097152 | tf_op jit(solution)/shard_map/all_to_all | solution.py:167
  21.9 0.1 compare_select_fusion
  22.0 0.1 reshape.88
  22.1 0.0 copy-start.3
  22.1 0.7 copy-done.3
  22.7 0.1 copy.13
  22.8 0.2 reduce-window.4
  23.0 0.1 select_reduce_fusion
  23.2 0.8 slice.35
  23.9 4.9 %collective-permute-start = (bf16[768,256]{1,0:T(8,128)(2,1)}, bf16[768,256]{1,0:T(8,128)(2,1)S(1)}, u32[]{:S(2)}, u32[]{:S(2)}) collective-permute-start(bf16[768,256]{1,0:T(8,128)(2,1)} %bitcast.8), channel_id=1, source_target_pairs={{0,8},{8,16},{16,24},{24,32},{32,40},{40,48},{48,56},{56,64},{64,7... | collective-permute-start | bytes 1179656 | tf_op jit(solution)/shard_map/ppermute | solution.py:19
  28.9 0.1 pad_add_fusion
  29.0 0.0 copy-start.1
  29.0 0.7 gather_fusion
  29.6 0.1 reshape.87
  29.7 0.2 convert_reduce_fusion
  29.9 8.2 %collective-permute-done.earlier_ref = bf16[768,256]{1,0:T(8,128)(2,1)S(1)} collective-permute-done((bf16[768,256]{1,0:T(8,128)(2,1)}, bf16[768,256]{1,0:T(8,128)(2,1)S(1)}, u32[]{:S(2)}, u32[]{:S(2)}) %collective-permute-start) | collective-permute-done | bytes 393248 | tf_op jit(solution)/shard_map/ppermute | solution.py:19
  38.1 0.0 all-to-all-done
  38.1 0.0 copy-done.1
  38.1 22.1 %shard_map.84 = (bf16[1024,512]{1,0:T(8,128)(2,1)}, bf16[1024,512]{1,0:T(8,128)(2,1)}, f32[768,256]{1,0:T(8,128)S(1)}, f32[1024,256]{1,0:T(8,128)S(1)}) custom-call(s32[4]{0:T(128)S(1)} %add_subtract_fusion.lo_ref, bf16[1024,512]{1,0:T(8,128)(2,1)S(1)} %bitcast.30, bf16[1024,256]{1,0:T(8,128)(2,1)S(1)} %bitcast.29, ...), custom_call_target="tpu_custom_call" | custom-call | flops 5637144576 | bytes 8388608 | tf_op jit(solution)/shard_map/pallas_call | solution.py:128
  60.4 1.9 %collective-permute-start.1 = (bf16[768,256]{1,0:T(8,128)(2,1)S(1)}, bf16[768,256]{1,0:T(8,128)(2,1)S(1)}, u32[]{:S(2)}, u32[]{:S(2)}) collective-permute-start(bf16[768,256]{1,0:T(8,128)(2,1)S(1)} %pad_maximum_fusion.1), channel_id=1, source_target_pairs={{8,0},{16,8},{24,16},{32,24},{40,32},{48,40},{56,48},{64,56},{72,6... | collective-permute-start | bytes 1179656 | tf_op jit(solution)/shard_map/ppermute | solution.py:19
  62.3 14.5 %collective-permute-done.1 = bf16[768,256]{1,0:T(8,128)(2,1)S(1)} collective-permute-done((bf16[768,256]{1,0:T(8,128)(2,1)S(1)}, bf16[768,256]{1,0:T(8,128)(2,1)S(1)}, u32[]{:S(2)}, u32[]{:S(2)}) %collective-permute-start.1) | collective-permute-done | bytes 393248 | tf_op jit(solution)/shard_map/ppermute | solution.py:19
  76.8 0.1 pad_convert_fusion
  76.9 0.9 %fusion = (bf16[1024,128]{1,0:T(8,128)(2,1)}, bf16[1024,128]{1,0:T(8,128)(2,1)}) fusion(f32[1024,256]{1,0:T(8,128)S(1)} %pad_convert_fusion, f32[1024,256]{1,0:T(8,128)S(1)} %get-tuple-element.10), kind=kLoop, calls=%fused_computation.3 | loop fusion | flops 655360 | bytes 2621440 | tf_op jit(solution)/shard_map/convert_element_type | solution.py:194
  (6 shorter events, 0.1 us)
Async XLA Ops:
  0.6 1.0 %copy-start = (bf16[128,1024]{1,0:T(8,128)(2,1)S(1)}, bf16[128,1024]{1,0:T(8,128)(2,1)}, u32[]{:S(2)}) copy-start(bf16[128,1024]{1,0:T(8,128)(2,1)} %param.6) | copy-start | bytes 786436
  2.7 5.3 %copy-start.2 = (bf16[128,4096]{1,0:T(8,128)(2,1)S(1)}, bf16[128,4096]{1,0:T(8,128)(2,1)}, u32[]{:S(2)}) copy-start(bf16[128,4096]{1,0:T(8,128)(2,1)} %param.5) | copy-start | bytes 3145732
  3.5 14.8 %all-to-all-start.1 = ((bf16[128,8,256]{2,0,1:T(8,128)(2,1)}), bf16[128,8,256]{2,0,1:T(8,128)(2,1)S(1)}, u32[]{:S(2)}, u32[]{:S(2)}) async-start(bf16[128,8,256]{2,0,1:T(8,128)(2,1)} %pad_maximum_fusion), calls=%async_computation.1 | async-start | bytes 1048576 | tf_op jit(solution)/shard_map/all_to_all | solution.py:163
  18.3 19.8 %all-to-all-start = ((bf16[128,8,512]{2,0,1:T(8,128)(2,1)}), bf16[128,8,512]{2,0,1:T(8,128)(2,1)S(1)}, u32[]{:S(2)}, u32[]{:S(2)}) async-start(bf16[128,8,512]{2,0,1:T(8,128)(2,1)} %bitcast.27), calls=%async_computation | async-start | bytes 2097152 | tf_op jit(solution)/shard_map/all_to_all | solution.py:167
  22.1 0.7 copy-start.3
  23.9 14.2 %collective-permute-start = (bf16[768,256]{1,0:T(8,128)(2,1)}, bf16[768,256]{1,0:T(8,128)(2,1)S(1)}, u32[]{:S(2)}, u32[]{:S(2)}) collective-permute-start(bf16[768,256]{1,0:T(8,128)(2,1)} %bitcast.8), channel_id=1, source_target_pairs={{0,8},{8,16},{16,24},{24,32},{32,40},{40,48},{48,56},{56,64},{64,7... | collective-permute-start | bytes 1179656 | tf_op jit(solution)/shard_map/ppermute | solution.py:19
  29.0 9.2 %copy-start.1 = (bf16[1024,512]{1,0:T(8,128)(2,1)S(1)}, bf16[1024,512]{1,0:T(8,128)(2,1)}, u32[]{:S(2)}) copy-start(bf16[1024,512]{1,0:T(8,128)(2,1)} %grad_ref.1) | copy-start | bytes 3145732
  60.4 16.4 %collective-permute-start.1 = (bf16[768,256]{1,0:T(8,128)(2,1)S(1)}, bf16[768,256]{1,0:T(8,128)(2,1)S(1)}, u32[]{:S(2)}, u32[]{:S(2)}) collective-permute-start(bf16[768,256]{1,0:T(8,128)(2,1)S(1)} %pad_maximum_fusion.1), channel_id=1, source_target_pairs={{8,0},{16,8},{24,16},{32,24},{40,32},{48,40},{56,48},{64,56},{72,6... | collective-permute-start | bytes 1179656 | tf_op jit(solution)/shard_map/ppermute | solution.py:19

commit v4 on v3

--- a/solution.py
+++ b/solution.py
@@ -31,11 +31,20 @@
     return lax.dot_general(a, b, (((1,), (0,)), ((), ())), preferred_element_type=jnp.float32)
 
 
-def attention_kernel(lo_ref, packed_ref, kv_ref, earlier_ref, grad_ref,
-                     att_ref, dq_ref, prior_ref, own_ref,
-                     s_scr, att_scr, dq_scr, *, units, heads, q_cols):
+def attention_kernel(*refs, unit_list, units, heads, with_prior, aliased):
+    refs = list(refs)
+    lo_ref, q_ref, kv_ref = refs[:3]
+    refs = refs[3:]
+    earlier_ref = refs.pop(0) if with_prior else None
+    grad_ref = refs.pop(0)
+    refs = refs[aliased:]
+    att_ref, dq_ref = refs[:2]
+    refs = refs[2:]
+    prior_ref = refs.pop(0) if with_prior else None
+    own_ref, s_scr, att_scr, dq_scr = refs
     scale = HEAD_SIZE ** (-0.5)
-    prior_ref[...] = jnp.zeros(prior_ref.shape, prior_ref.dtype)
+    if with_prior:
+        prior_ref[...] = jnp.zeros(prior_ref.shape, prior_ref.dtype)
     own_ref[...] = jnp.zeros(own_ref.shape, own_ref.dtype)
     rows = heads * BLOCK
     causal = (lax.broadcasted_iota(jnp.int32, (rows, BLOCK), 0) % BLOCK
@@ -46,17 +55,19 @@
         return (ref[pl.ds(start, BLOCK), col0:col0 + HEAD_SIZE],
                 ref[pl.ds(start, BLOCK), col0 + HEAD_SIZE:col0 + 2 * HEAD_SIZE])
 
-    for u in range(units):
+    for u in unit_list:
         r0 = u * BLOCK
+        w0 = (u - unit_list[0]) * BLOCK
         qs = jnp.concatenate(
-            [packed_ref[r0:r0 + BLOCK, h * HEAD_SIZE:(h + 1) * HEAD_SIZE] for h in range(heads)], axis=0)
+            [q_ref[r0:r0 + BLOCK, h * HEAD_SIZE:(h + 1) * HEAD_SIZE] for h in range(heads)], axis=0)
         dos = jnp.concatenate(
             [grad_ref[r0:r0 + BLOCK, h * HEAD_SIZE:(h + 1) * HEAD_SIZE] for h in range(heads)], axis=0)
         lo = lo_ref[u]
         diag = units + u
         first_own = jnp.maximum(lo, units)
-        segments = ((earlier_ref, 0, prior_ref, lo, units, 1),
-                    (kv_ref, 0, own_ref, first_own, diag, units))
+        segments = ((kv_ref, 0, own_ref, first_own, diag, units),)
+        if with_prior:
+            segments = ((earlier_ref, 0, prior_ref, lo, units, 1),) + segments
 
         def pass1(b, carry, ref, col0, off):
             m, l = carry
@@ -73,7 +84,6 @@
         m, l = carry
         k_d, v_d = load_kv(kv_ref, 0, u)
         s = jnp.where(causal, _nt(qs, k_d) * scale, -jnp.inf)
-        s_scr[units - 1] = s
         m_new = jnp.maximum(m, jnp.max(s, axis=1, keepdims=True))
         l = l * jnp.exp(m - m_new) + jnp.sum(jnp.exp(s - m_new), axis=1, keepdims=True)
         lse = m_new + jnp.log(l)
@@ -86,7 +96,6 @@
             return 0
 
         p = jnp.exp(s - lse)
-        s_scr[units - 1] = p
         att_scr[...] = _nn(p.astype(jnp.bfloat16), v_d)
         for ref, col0, _, start, stop, off in segments:
             lax.fori_loop(start, stop, functools.partial(pass2, ref=ref, col0=col0, off=off), 0)
@@ -111,40 +120,59 @@
             lax.fori_loop(start, stop, functools.partial(pass3, ref=ref, col0=col0, gref=gref, off=off), 0)
         dq = (dq_scr[...] * scale).astype(jnp.bfloat16)
         for h in range(heads):
-            att_ref[r0:r0 + BLOCK, h * HEAD_SIZE:(h + 1) * HEAD_SIZE] = att[h * BLOCK:(h + 1) * BLOCK]
-            dq_ref[r0:r0 + BLOCK, h * HEAD_SIZE:(h + 1) * HEAD_SIZE] = dq[h * BLOCK:(h + 1) * BLOCK]
-
-
-def attention_call(lo, packed, kv, earlier, grad, *, heads, interpret=False):
+            att_ref[w0:w0 + BLOCK, h * HEAD_SIZE:(h + 1) * HEAD_SIZE] = att[h * BLOCK:(h + 1) * BLOCK]
+            dq_ref[w0:w0 + BLOCK, h * HEAD_SIZE:(h + 1) * HEAD_SIZE] = dq[h * BLOCK:(h + 1) * BLOCK]
+
+
+def attention_call(lo, packed, kv, earlier, grad, unit_list, out_alias=None, *, heads, interpret=False):
     ctx_rows = packed.shape[0]
     units = ctx_rows // BLOCK
     q_cols = heads * HEAD_SIZE
     kv_cols = 2 * HEAD_SIZE
-    vmem = pltpu.MemorySpace.VMEM
-    kernel = functools.partial(attention_kernel, units=units, heads=heads, q_cols=q_cols)
+    with_prior = earlier is not None
+    aliased = 0 if out_alias is None else 2
+    kernel = functools.partial(attention_kernel, unit_list=tuple(unit_list), units=units, heads=heads,
+                               with_prior=with_prior, aliased=aliased)
     rows = heads * BLOCK
-    visible_blocks = units * (units + 1) // 2 + units
+    n_rows = len(unit_list) * BLOCK
+    block_index = unit_list[0] // len(unit_list)
+    assert block_index * len(unit_list) == unit_list[0]
+
+    def whole(x):
+        return pl.BlockSpec(x.shape, lambda i: (0,) * len(x.shape))
+
+    operands = [lo, packed, kv] + ([earlier] if with_prior else []) + [grad]
+    in_specs = [pl.BlockSpec(memory_space=pltpu.SMEM)] + [whole(x) for x in operands[1:]]
+    if out_alias is not None:
+        operands += list(out_alias)
+        in_specs += [pl.BlockSpec(memory_space=pl.ANY)] * 2
+    out_shape = [jax.ShapeDtypeStruct((ctx_rows, q_cols), jnp.bfloat16)] * 2
+    out_specs = [pl.BlockSpec((n_rows, q_cols), lambda i: (block_index, 0))] * 2
+    if with_prior:
+        out_shape.append(jax.ShapeDtypeStruct(earlier.shape, jnp.float32))
+        out_specs.append(pl.BlockSpec(earlier.shape, lambda i: (0, 0)))
+    out_shape.append(jax.ShapeDtypeStruct((ctx_rows, kv_cols), jnp.float32))
+    out_specs.append(pl.BlockSpec((ctx_rows, kv_cols), lambda i: (0, 0)))
+    visible_blocks = 4 * len(unit_list)
     flops = 12 * rows * BLOCK * HEAD_SIZE * visible_blocks
+    aliases = {} if out_alias is None else {len(operands) - 2: 0, len(operands) - 1: 1}
     return pl.pallas_call(
         kernel,
-        out_shape=(
-            jax.ShapeDtypeStruct((ctx_rows, q_cols), jnp.bfloat16),
-            jax.ShapeDtypeStruct((ctx_rows, q_cols), jnp.bfloat16),
-            jax.ShapeDtypeStruct(earlier.shape, jnp.float32),
-            jax.ShapeDtypeStruct((ctx_rows, kv_cols), jnp.float32),
-        ),
-        in_specs=[pl.BlockSpec(memory_space=pltpu.SMEM)] + [pl.BlockSpec(memory_space=vmem)] * 4,
-        out_specs=tuple(pl.BlockSpec(memory_space=vmem) for _ in range(4)),
+        grid=(1,),
+        out_shape=tuple(out_shape),
+        in_specs=in_specs,
+        out_specs=tuple(out_specs),
         scratch_shapes=[
             pltpu.VMEM((units, rows, BLOCK), jnp.float32),
             pltpu.VMEM((rows, HEAD_SIZE), jnp.float32),
             pltpu.VMEM((rows, HEAD_SIZE), jnp.float32),
         ],
+        input_output_aliases=aliases,
         compiler_params=pltpu.CompilerParams(vmem_limit_bytes=48 * 1024 * 1024),
         cost_estimate=pl.CostEstimate(flops=flops, transcendentals=2 * rows * BLOCK * visible_blocks,
-                                      bytes_accessed=8 * 1024 * 1024),
+                                      bytes_accessed=6 * 1024 * 1024),
         interpret=interpret,
-    )(lo, packed, kv, earlier, grad)
+    )(*operands)
 
 
 def local(query_matrix, key_matrix, value_matrix, output_gradient, doc_start):
@@ -179,9 +207,14 @@
     window = unit_ids[:, None] + 1 + unit_ids[None, :]
     same = (joined_units[window] == own_units[:, None]).astype(jnp.int32)
     lo = (unit_ids + units + 1 - jnp.sum(same, axis=1)).astype(jnp.int32)
-    attended_all, query_total, prior_grads, own_grads = attention_call(
-        lo, packed, kv, earlier_kv, output_gradient, heads=q_cols // HEAD_SIZE, interpret=INTERPRET
-    )
+    heads = q_cols // HEAD_SIZE
+    first = attention_call(lo, packed, kv, earlier_kv, output_gradient, range(units - 1),
+                           heads=heads, interpret=INTERPRET)
+    attended_all, query_total, prior_grads, own_first = first
+    last = attention_call(lo, packed, kv, None, output_gradient, [units - 1],
+                          (attended_all, query_total), heads=heads, interpret=INTERPRET)
+    attended_all, query_total, own_last = last
+    own_grads = own_first + own_last
     score_scale = HEAD_SIZE ** (-0.5)
     prior_grads = jnp.concatenate(
         [(prior_grads[:, :k_cols] * score_scale).astype(jnp.bfloat16),

time: 78.1 us -> 73.8 us (0.945)
  starting transfers between devices: 14.9 us -> 25 us
  waiting for transfers between devices: 31.9 us -> 23.9 us
  Pallas kernels: 22.1 us -> 15.6 us
    ppermute x2, starting transfers between devices: 6.86 us -> 17 us  [from_behind(): return lax.ppermute(block, axis, route)]
    ppermute x2, waiting for transfers between devices: 22.7 us -> 14.6 us  [from_behind(): return lax.ppermute(block, axis, route)]
    pallas_call x1 -> x2, Pallas kernels: 22.1 us -> 15.6 us  [attention_call(): pl.pallas_call(kernel, grid=(1,), out_shape=tuple(out_shape), in_specs=in...]
  transfers between devices with their start and end apart: 4 -> 4, of which waited for: 3 -> 3; matrix products, arithmetic and copies ran while one was open for 4% -> 5% of each run, Pallas kernels for 0% -> 7%
where the time goes in v4:
time: 73.8 us; the launch traced here: 73.5 us
  starting transfers between devices  25 us (34%)
  waiting for transfers between devices  23.9 us (32%)
  Pallas kernels  15.6 us (21%)
  local copies, waits for them, and re-layouts  5.49 us (7%)
  other arithmetic  2.71 us (4%)
  between operations  0.76 us (1%)
    ppermute x2, starting transfers between devices, from_behind(): return lax.ppermute(block, axis, route)  17 us
    pallas_call x2, Pallas kernels, attention_call(): pl.pallas_call(kernel, grid=(1,), out_shape=tuple(out_shape), in_specs=in...  15.6 us
    ppermute x2, waiting for transfers between devices, from_behind(): return lax.ppermute(block, axis, route)  14.6 us
    all_to_all x1, waiting for transfers between devices, local(): lax.all_to_all(kv_packed, 'head', split_axis=1, concat_axis=0, tiled=True)  9.24 us
    all_to_all x1, starting transfers between devices, local(): lax.all_to_all(kv_packed, 'head', split_axis=1, concat_axis=0, tiled=True)  4.47 us
    all_to_all x1, starting transfers between devices, local(): lax.all_to_all(query_matrix.reshape(token_per_shard, head_groups, q_cols)...  3.56 us
    unnamed x8, local copies, waits for them, and re-layouts  1.62 us
  transfers between devices with their start and end apart: 4, of which 3 were waited for; matrix products, arithmetic and copies ran while one was open for 5% of the time, Pallas kernels for 7%

profile of v4, /device:TPU:102, one launch (start us, length us, event | category | flops | bytes accessed | tf_op | source)
XLA Modules:
  0.0 73.5 jit_solution(7527188729516233200)
XLA Ops:
  0.6 0.0 copy-start
  0.6 0.9 %copy-done = bf16[128,1024]{1,0:T(8,128)(2,1)S(1)} copy-done((bf16[128,1024]{1,0:T(8,128)(2,1)S(1)}, bf16[128,1024]{1,0:T(8,128)(2,1)}, u32[]{:S(2)}) %copy-start) | copy-done | bytes 262168
  1.6 1.1 %copy_bitcast_fusion.1 = (bf16[128,8,128]{2,0,1:T(8,128)(2,1)S(1)}, bf16[128,8,128]{2,0,1:T(8,128)(2,1)S(1)}) fusion(bf16[128,1024]{1,0:T(8,128)(2,1)S(1)} %copy-done, bf16[128,1024]{1,0:T(8,128)(2,1)} %param.7), kind=kLoop, calls=%fused_computation.12 | loop fusion | bytes 1048576 | tf_op jit(solution)/shard_map/reshape | solution.py:187
  2.7 0.0 copy-start.2
  2.7 0.9 %pad_maximum_fusion = bf16[128,8,256]{2,0,1:T(8,128)(2,1)} fusion(bf16[128,8,128]{2,0,1:T(8,128)(2,1)S(1)} %get-tuple-element.22, bf16[128,8,128]{2,0,1:T(8,128)(2,1)S(1)} %get-tuple-element.23), kind=kLoop, calls=%fused_computation.7 | loop fusion | flops 1048576 | bytes 1048576 | tf_op jit(solution)/shard_map/concatenate | solution.py:184
  3.5 4.5 %all-to-all-start.1 = ((bf16[128,8,256]{2,0,1:T(8,128)(2,1)}), bf16[128,8,256]{2,0,1:T(8,128)(2,1)S(1)}, u32[]{:S(2)}, u32[]{:S(2)}) async-start(bf16[128,8,256]{2,0,1:T(8,128)(2,1)} %pad_maximum_fusion), calls=%async_computation.1 | async-start | bytes 1048576 | tf_op jit(solution)/shard_map/all_to_all | solution.py:191
  8.0 0.0 copy-done.2
  8.0 1.1 %copy.25 = bf16[16,8,8,512]{3,2,0,1:T(8,128)(2,1)} copy(bf16[16,8,8,512]{3,2,1,0:T(8,128)(2,1)S(1)} %bitcast.33) | data formatting | bytes 2097152 | tf_op jit(solution)/shard_map/reshape | solution.py:196
  9.1 9.2 %all-to-all-done.1 = bf16[128,8,256]{2,0,1:T(8,128)(2,1)S(1)} async-done(((bf16[128,8,256]{2,0,1:T(8,128)(2,1)}), bf16[128,8,256]{2,0,1:T(8,128)(2,1)S(1)}, u32[]{:S(2)}, u32[]{:S(2)}) %all-to-all-start.1) | async-done | bytes 524320 | tf_op jit(solution)/shard_map/all_to_all | solution.py:191
  18.3 3.6 %all-to-all-start = ((bf16[128,8,512]{2,0,1:T(8,128)(2,1)}), bf16[128,8,512]{2,0,1:T(8,128)(2,1)S(1)}, u32[]{:S(2)}, u32[]{:S(2)}) async-start(bf16[128,8,512]{2,0,1:T(8,128)(2,1)} %bitcast.27), calls=%async_computation | async-start | bytes 2097152 | tf_op jit(solution)/shard_map/all_to_all | solution.py:195
  21.9 0.1 compare_select_fusion
  22.0 0.1 reshape.88
  22.1 0.0 copy-start.3
  22.1 0.7 copy-done.3
  22.7 0.1 copy.15
  22.8 0.2 reduce-window.4
  23.0 0.1 select_reduce_fusion
  23.2 0.8 %slice.35 = bf16[6,128,1,256]{3,1,0,2:T(8,128)(2,1)} slice(bf16[8,128,1,256]{3,1,0,2:T(8,128)(2,1)S(1)} %bitcast.28), slice={[2:8], [0:128], [0:1], [0:256]} | slice | bytes 786432 | tf_op jit(solution)/shard_map/slice | solution.py:194
  23.9 4.9 %collective-permute-start = (bf16[768,256]{1,0:T(8,128)(2,1)}, bf16[768,256]{1,0:T(8,128)(2,1)S(1)}, u32[]{:S(2)}, u32[]{:S(2)}) collective-permute-start(bf16[768,256]{1,0:T(8,128)(2,1)} %bitcast.11), channel_id=1, source_target_pairs={{0,8},{8,16},{16,24},{24,32},{32,40},{40,48},{48,56},{56,64},{64,7... | collective-permute-start | bytes 1179656 | tf_op jit(solution)/shard_map/ppermute | solution.py:19
  28.9 0.1 pad_add_fusion
  29.0 0.0 copy-start.1
  29.0 0.7 gather_fusion
  29.6 0.1 reshape.87
  29.7 0.2 convert_reduce_fusion
  29.9 8.2 %collective-permute-done.refs_3_ = bf16[768,256]{1,0:T(8,128)(2,1)S(1)} collective-permute-done((bf16[768,256]{1,0:T(8,128)(2,1)}, bf16[768,256]{1,0:T(8,128)(2,1)S(1)}, u32[]{:S(2)}, u32[]{:S(2)}) %collective-permute-start) | collective-permute-done | bytes 393248 | tf_op jit(solution)/shard_map/ppermute | solution.py:19
  38.1 0.0 all-to-all-done
  38.1 0.0 copy-done.1
  38.1 10.2 %shard_map.84 = (bf16[1024,512]{1,0:T(8,128)(2,1)}, bf16[1024,512]{1,0:T(8,128)(2,1)}, f32[768,256]{1,0:T(8,128)S(1)}, f32[1024,256]{1,0:T(8,128)S(1)}) custom-call(s32[4]{0:T(128)S(1)} %add_subtract_fusion.refs_0_, bf16[1024,512]{1,0:T(8,128)(2,1)S(1)} %bitcast.31, bf16[1024,256]{1,0:T(8,128)(2,1)S(1)} %bitcast.29, ...), custom_call_target="tpu_custom_call" | custom-call | flops 4831838208 | bytes 6291456 | tf_op jit(solution)/shard_map/pallas_call | solution.py:159
  48.5 12.1 %collective-permute-start.1 = (bf16[768,256]{1,0:T(8,128)(2,1)S(1)}, bf16[768,256]{1,0:T(8,128)(2,1)S(1)}, u32[]{:S(2)}, u32[]{:S(2)}) collective-permute-start(bf16[768,256]{1,0:T(8,128)(2,1)S(1)} %pad_maximum_fusion.1), channel_id=1, source_target_pairs={{8,0},{16,8},{24,16},{32,24},{40,32},{48,40},{56,48},{64,56},{72,6... | collective-permute-start | bytes 1179656 | tf_op jit(solution)/shard_map/ppermute | solution.py:19
  60.5 5.4 %shard_map.85 = (bf16[1024,512]{1,0:T(8,128)(2,1)}, bf16[1024,512]{1,0:T(8,128)(2,1)}, f32[1024,256]{1,0:T(8,128)S(1)}) custom-call(s32[4]{0:T(128)S(1)} %add_subtract_fusion.refs_0_, bf16[1024,512]{1,0:T(8,128)(2,1)S(1)} %bitcast.32, bf16[1024,256]{1,0:T(8,128)(2,1)S(1)} %bitcast.30, ...), custom_call_target="tpu_custom_call", output_to_operand_aliasing={{0}: (4, {}), {1}: (5, {})} | custom-call | flops 1610612736 | bytes 6291456 | tf_op jit(solution)/shard_map/pallas_call | solution.py:159
  65.9 0.1 add.73
  66.1 6.4 %collective-permute-done.1 = bf16[768,256]{1,0:T(8,128)(2,1)S(1)} collective-permute-done((bf16[768,256]{1,0:T(8,128)(2,1)S(1)}, bf16[768,256]{1,0:T(8,128)(2,1)S(1)}, u32[]{:S(2)}, u32[]{:S(2)}) %collective-permute-start.1) | collective-permute-done | bytes 393248 | tf_op jit(solution)/shard_map/ppermute | solution.py:19
  72.5 0.1 pad_convert_fusion
  72.6 0.9 %fusion = (bf16[1024,128]{1,0:T(8,128)(2,1)}, bf16[1024,128]{1,0:T(8,128)(2,1)}) fusion(f32[1024,256]{1,0:T(8,128)S(1)} %pad_convert_fusion, f32[1024,256]{1,0:T(8,128)S(1)} %add.73), kind=kLoop, calls=%fused_computation.3 | loop fusion | flops 655360 | bytes 2621440 | tf_op jit(solution)/shard_map/convert_element_type | solution.py:227
  (6 shorter events, 0.1 us)
Async XLA Ops:
  0.6 1.0 %copy-start = (bf16[128,1024]{1,0:T(8,128)(2,1)S(1)}, bf16[128,1024]{1,0:T(8,128)(2,1)}, u32[]{:S(2)}) copy-start(bf16[128,1024]{1,0:T(8,128)(2,1)} %param.6) | copy-start | bytes 786436
  2.7 5.3 %copy-start.2 = (bf16[128,4096]{1,0:T(8,128)(2,1)S(1)}, bf16[128,4096]{1,0:T(8,128)(2,1)}, u32[]{:S(2)}) copy-start(bf16[128,4096]{1,0:T(8,128)(2,1)} %param.5) | copy-start | bytes 3145732
  3.5 14.8 %all-to-all-start.1 = ((bf16[128,8,256]{2,0,1:T(8,128)(2,1)}), bf16[128,8,256]{2,0,1:T(8,128)(2,1)S(1)}, u32[]{:S(2)}, u32[]{:S(2)}) async-start(bf16[128,8,256]{2,0,1:T(8,128)(2,1)} %pad_maximum_fusion), calls=%async_computation.1 | async-start | bytes 1048576 | tf_op jit(solution)/shard_map/all_to_all | solution.py:191
  18.3 19.8 %all-to-all-start = ((bf16[128,8,512]{2,0,1:T(8,128)(2,1)}), bf16[128,8,512]{2,0,1:T(8,128)(2,1)S(1)}, u32[]{:S(2)}, u32[]{:S(2)}) async-start(bf16[128,8,512]{2,0,1:T(8,128)(2,1)} %bitcast.27), calls=%async_computation | async-start | bytes 2097152 | tf_op jit(solution)/shard_map/all_to_all | solution.py:195
  22.1 0.7 copy-start.3
  23.9 14.2 %collective-permute-start = (bf16[768,256]{1,0:T(8,128)(2,1)}, bf16[768,256]{1,0:T(8,128)(2,1)S(1)}, u32[]{:S(2)}, u32[]{:S(2)}) collective-permute-start(bf16[768,256]{1,0:T(8,128)(2,1)} %bitcast.11), channel_id=1, source_target_pairs={{0,8},{8,16},{16,24},{24,32},{32,40},{40,48},{48,56},{56,64},{64,7... | collective-permute-start | bytes 1179656 | tf_op jit(solution)/shard_map/ppermute | solution.py:19
  29.0 9.2 %copy-start.1 = (bf16[1024,512]{1,0:T(8,128)(2,1)S(1)}, bf16[1024,512]{1,0:T(8,128)(2,1)}, u32[]{:S(2)}) copy-start(bf16[1024,512]{1,0:T(8,128)(2,1)} %refs_3_.1) | copy-start | bytes 3145732
  48.5 24.0 %collective-permute-start.1 = (bf16[768,256]{1,0:T(8,128)(2,1)S(1)}, bf16[768,256]{1,0:T(8,128)(2,1)S(1)}, u32[]{:S(2)}, u32[]{:S(2)}) collective-permute-start(bf16[768,256]{1,0:T(8,128)(2,1)S(1)} %pad_maximum_fusion.1), channel_id=1, source_target_pairs={{8,0},{16,8},{24,16},{32,24},{40,32},{48,40},{56,48},{64,56},{72,6... | collective-permute-start | bytes 1179656 | tf_op jit(solution)/shard_map/ppermute | solution.py:19

commit v5 on v4

--- a/solution.py
+++ b/solution.py
@@ -31,7 +31,7 @@
     return lax.dot_general(a, b, (((1,), (0,)), ((), ())), preferred_element_type=jnp.float32)
 
 
-def attention_kernel(*refs, unit_list, units, heads, with_prior, aliased):
+def attention_kernel(*refs, first_unit, units, heads, with_prior, aliased):
     refs = list(refs)
     lo_ref, q_ref, kv_ref = refs[:3]
     refs = refs[3:]
@@ -43,9 +43,14 @@
     prior_ref = refs.pop(0) if with_prior else None
     own_ref, s_scr, att_scr, dq_scr = refs
     scale = HEAD_SIZE ** (-0.5)
-    if with_prior:
-        prior_ref[...] = jnp.zeros(prior_ref.shape, prior_ref.dtype)
-    own_ref[...] = jnp.zeros(own_ref.shape, own_ref.dtype)
+    step = pl.program_id(0)
+
+    @pl.when(step == 0)
+    def _():
+        if with_prior:
+            prior_ref[...] = jnp.zeros(prior_ref.shape, prior_ref.dtype)
+        own_ref[...] = jnp.zeros(own_ref.shape, own_ref.dtype)
+
     rows = heads * BLOCK
     causal = (lax.broadcasted_iota(jnp.int32, (rows, BLOCK), 0) % BLOCK
               >= lax.broadcasted_iota(jnp.int32, (rows, BLOCK), 1))
@@ -55,13 +60,12 @@
         return (ref[pl.ds(start, BLOCK), col0:col0 + HEAD_SIZE],
                 ref[pl.ds(start, BLOCK), col0 + HEAD_SIZE:col0 + 2 * HEAD_SIZE])
 
-    for u in unit_list:
-        r0 = u * BLOCK
-        w0 = (u - unit_list[0]) * BLOCK
+    if True:
+        u = first_unit + step
         qs = jnp.concatenate(
-            [q_ref[r0:r0 + BLOCK, h * HEAD_SIZE:(h + 1) * HEAD_SIZE] for h in range(heads)], axis=0)
+            [q_ref[:, h * HEAD_SIZE:(h + 1) * HEAD_SIZE] for h in range(heads)], axis=0)
         dos = jnp.concatenate(
-            [grad_ref[r0:r0 + BLOCK, h * HEAD_SIZE:(h + 1) * HEAD_SIZE] for h in range(heads)], axis=0)
+            [grad_ref[:, h * HEAD_SIZE:(h + 1) * HEAD_SIZE] for h in range(heads)], axis=0)
         lo = lo_ref[u]
         diag = units + u
         first_own = jnp.maximum(lo, units)
@@ -114,14 +118,15 @@
 
         ds = (p * (_nt(dos, v_d) - delta)).astype(jnp.bfloat16)
         dq_scr[...] = _nn(ds, k_d)
-        own_ref[r0:r0 + BLOCK, 0:HEAD_SIZE] += _tn(ds, qs)
-        own_ref[r0:r0 + BLOCK, HEAD_SIZE:2 * HEAD_SIZE] += _tn(p.astype(jnp.bfloat16), dos)
+        r0 = pl.multiple_of(u * BLOCK, BLOCK)
+        own_ref[pl.ds(r0, BLOCK), 0:HEAD_SIZE] += _tn(ds, qs)
+        own_ref[pl.ds(r0, BLOCK), HEAD_SIZE:2 * HEAD_SIZE] += _tn(p.astype(jnp.bfloat16), dos)
         for ref, col0, gref, start, stop, off in segments:
             lax.fori_loop(start, stop, functools.partial(pass3, ref=ref, col0=col0, gref=gref, off=off), 0)
         dq = (dq_scr[...] * scale).astype(jnp.bfloat16)
         for h in range(heads):
-            att_ref[w0:w0 + BLOCK, h * HEAD_SIZE:(h + 1) * HEAD_SIZE] = att[h * BLOCK:(h + 1) * BLOCK]
-            dq_ref[w0:w0 + BLOCK, h * HEAD_SIZE:(h + 1) * HEAD_SIZE] = dq[h * BLOCK:(h + 1) * BLOCK]
+            att_ref[:, h * HEAD_SIZE:(h + 1) * HEAD_SIZE] = att[h * BLOCK:(h + 1) * BLOCK]
+            dq_ref[:, h * HEAD_SIZE:(h + 1) * HEAD_SIZE] = dq[h * BLOCK:(h + 1) * BLOCK]
 
 
 def attention_call(lo, packed, kv, earlier, grad, unit_list, out_alias=None, *, heads, interpret=False):
@@ -131,23 +136,24 @@
     kv_cols = 2 * HEAD_SIZE
     with_prior = earlier is not None
     aliased = 0 if out_alias is None else 2
-    kernel = functools.partial(attention_kernel, unit_list=tuple(unit_list), units=units, heads=heads,
+    first_unit = unit_list[0]
+    steps = len(unit_list)
+    kernel = functools.partial(attention_kernel, first_unit=first_unit, units=units, heads=heads,
                                with_prior=with_prior, aliased=aliased)
     rows = heads * BLOCK
-    n_rows = len(unit_list) * BLOCK
-    block_index = unit_list[0] // len(unit_list)
-    assert block_index * len(unit_list) == unit_list[0]
 
     def whole(x):
         return pl.BlockSpec(x.shape, lambda i: (0,) * len(x.shape))
 
     operands = [lo, packed, kv] + ([earlier] if with_prior else []) + [grad]
-    in_specs = [pl.BlockSpec(memory_space=pltpu.SMEM)] + [whole(x) for x in operands[1:]]
+    unit_block = pl.BlockSpec((BLOCK, q_cols), lambda i: (first_unit + i, 0))
+    in_specs = [pl.BlockSpec(memory_space=pltpu.SMEM), unit_block]
+    in_specs += [whole(x) for x in operands[2:-1]] + [unit_block]
     if out_alias is not None:
         operands += list(out_alias)
         in_specs += [pl.BlockSpec(memory_space=pl.ANY)] * 2
     out_shape = [jax.ShapeDtypeStruct((ctx_rows, q_cols), jnp.bfloat16)] * 2
-    out_specs = [pl.BlockSpec((n_rows, q_cols), lambda i: (block_index, 0))] * 2
+    out_specs = [unit_block] * 2
     if with_prior:
         out_shape.append(jax.ShapeDtypeStruct(earlier.shape, jnp.float32))
         out_specs.append(pl.BlockSpec(earlier.shape, lambda i: (0, 0)))
@@ -158,7 +164,7 @@
     aliases = {} if out_alias is None else {len(operands) - 2: 0, len(operands) - 1: 1}
     return pl.pallas_call(
         kernel,
-        grid=(1,),
+        grid=(steps,),
         out_shape=tuple(out_shape),
         in_specs=in_specs,
         out_specs=tuple(out_specs),
@@ -168,7 +174,8 @@
             pltpu.VMEM((rows, HEAD_SIZE), jnp.float32),
         ],
         input_output_aliases=aliases,
-        compiler_params=pltpu.CompilerParams(vmem_limit_bytes=48 * 1024 * 1024),
+        compiler_params=pltpu.CompilerParams(
+            dimension_semantics=("arbitrary",), vmem_limit_bytes=48 * 1024 * 1024),
         cost_estimate=pl.CostEstimate(flops=flops, transcendentals=2 * rows * BLOCK * visible_blocks,
                                       bytes_accessed=6 * 1024 * 1024),
         interpret=interpret,

time: 73.8 us -> 73.6 us (level)
  waiting for transfers between devices: 23.9 us -> 34 us
  starting transfers between devices: 25 us -> 14.9 us
    ppermute x2, starting transfers between devices: 17 us -> 6.86 us  [from_behind(): return lax.ppermute(block, axis, route)]
    ppermute x2, waiting for transfers between devices: 14.6 us -> 24.7 us  [from_behind(): return lax.ppermute(block, axis, route)]
where the time goes in v5:
time: 73.6 us; the launch traced here: 73.2 us
  waiting for transfers between devices  34 us (46%)
  Pallas kernels  15.4 us (21%)
  starting transfers between devices  14.9 us (20%)
  local copies, waits for them, and re-layouts  5.49 us (7%)
  other arithmetic  2.71 us (4%)
  between operations  0.76 us (1%)
    ppermute x2, waiting for transfers between devices, from_behind(): return lax.ppermute(block, axis, route)  24.7 us
    pallas_call x2, Pallas kernels, attention_call(): pl.pallas_call(kernel, grid=(steps,), out_shape=tuple(out_shape), in_spec...  15.4 us
    all_to_all x1, waiting for transfers between devices, local(): lax.all_to_all(kv_packed, 'head', split_axis=1, concat_axis=0, tiled=True)  9.24 us
    ppermute x2, starting transfers between devices, from_behind(): return lax.ppermute(block, axis, route)  6.86 us
    all_to_all x1, starting transfers between devices, local(): lax.all_to_all(kv_packed, 'head', split_axis=1, concat_axis=0, tiled=True)  4.47 us
    all_to_all x1, starting transfers between devices, local(): lax.all_to_all(query_matrix.reshape(token_per_shard, head_groups, q_cols)...  3.56 us
    unnamed x8, local copies, waits for them, and re-layouts  1.62 us
  transfers between devices with their start and end apart: 4, of which 3 were waited for; matrix products, arithmetic and copies ran while one was open for 5% of the time, Pallas kernels for 7%

profile of v5, /device:TPU:102, one launch (start us, length us, event | category | flops | bytes accessed | tf_op | source)
XLA Modules:
  0.0 73.2 jit_solution(9877357790142664646)
XLA Ops:
  0.6 0.0 copy-start
  0.6 0.9 %copy-done = bf16[128,1024]{1,0:T(8,128)(2,1)S(1)} copy-done((bf16[128,1024]{1,0:T(8,128)(2,1)S(1)}, bf16[128,1024]{1,0:T(8,128)(2,1)}, u32[]{:S(2)}) %copy-start) | copy-done | bytes 262168
  1.6 1.1 %copy_bitcast_fusion.1 = (bf16[128,8,128]{2,0,1:T(8,128)(2,1)S(1)}, bf16[128,8,128]{2,0,1:T(8,128)(2,1)S(1)}) fusion(bf16[128,1024]{1,0:T(8,128)(2,1)S(1)} %copy-done, bf16[128,1024]{1,0:T(8,128)(2,1)} %param.7), kind=kLoop, calls=%fused_computation.12 | loop fusion | bytes 1048576 | tf_op jit(solution)/shard_map/reshape | solution.py:194
  2.7 0.0 copy-start.2
  2.7 0.9 %pad_maximum_fusion = bf16[128,8,256]{2,0,1:T(8,128)(2,1)} fusion(bf16[128,8,128]{2,0,1:T(8,128)(2,1)S(1)} %get-tuple-element.22, bf16[128,8,128]{2,0,1:T(8,128)(2,1)S(1)} %get-tuple-element.23), kind=kLoop, calls=%fused_computation.7 | loop fusion | flops 1048576 | bytes 1048576 | tf_op jit(solution)/shard_map/concatenate | solution.py:191
  3.5 4.5 %all-to-all-start.1 = ((bf16[128,8,256]{2,0,1:T(8,128)(2,1)}), bf16[128,8,256]{2,0,1:T(8,128)(2,1)S(1)}, u32[]{:S(2)}, u32[]{:S(2)}) async-start(bf16[128,8,256]{2,0,1:T(8,128)(2,1)} %pad_maximum_fusion), calls=%async_computation.1 | async-start | bytes 1048576 | tf_op jit(solution)/shard_map/all_to_all | solution.py:198
  8.0 0.0 copy-done.2
  8.0 1.1 %copy.25 = bf16[16,8,8,512]{3,2,0,1:T(8,128)(2,1)} copy(bf16[16,8,8,512]{3,2,1,0:T(8,128)(2,1)S(1)} %bitcast.33) | data formatting | bytes 2097152 | tf_op jit(solution)/shard_map/reshape | solution.py:203
  9.1 9.2 %all-to-all-done.1 = bf16[128,8,256]{2,0,1:T(8,128)(2,1)S(1)} async-done(((bf16[128,8,256]{2,0,1:T(8,128)(2,1)}), bf16[128,8,256]{2,0,1:T(8,128)(2,1)S(1)}, u32[]{:S(2)}, u32[]{:S(2)}) %all-to-all-start.1) | async-done | bytes 524320 | tf_op jit(solution)/shard_map/all_to_all | solution.py:198
  18.3 3.6 %all-to-all-start = ((bf16[128,8,512]{2,0,1:T(8,128)(2,1)}), bf16[128,8,512]{2,0,1:T(8,128)(2,1)S(1)}, u32[]{:S(2)}, u32[]{:S(2)}) async-start(bf16[128,8,512]{2,0,1:T(8,128)(2,1)} %bitcast.27), calls=%async_computation | async-start | bytes 2097152 | tf_op jit(solution)/shard_map/all_to_all | solution.py:202
  21.9 0.1 compare_select_fusion
  22.0 0.1 reshape.88
  22.1 0.0 copy-start.3
  22.1 0.7 copy-done.3
  22.7 0.1 copy.15
  22.8 0.2 reduce-window.4
  23.0 0.1 select_reduce_fusion
  23.2 0.8 %slice.35 = bf16[6,128,1,256]{3,1,0,2:T(8,128)(2,1)} slice(bf16[8,128,1,256]{3,1,0,2:T(8,128)(2,1)S(1)} %bitcast.28), slice={[2:8], [0:128], [0:1], [0:256]} | slice | bytes 786432 | tf_op jit(solution)/shard_map/slice | solution.py:201
  23.9 4.9 %collective-permute-start = (bf16[768,256]{1,0:T(8,128)(2,1)}, bf16[768,256]{1,0:T(8,128)(2,1)S(1)}, u32[]{:S(2)}, u32[]{:S(2)}) collective-permute-start(bf16[768,256]{1,0:T(8,128)(2,1)} %bitcast.11), channel_id=1, source_target_pairs={{0,8},{8,16},{16,24},{24,32},{32,40},{40,48},{48,56},{56,64},{64,7... | collective-permute-start | bytes 1179656 | tf_op jit(solution)/shard_map/ppermute | solution.py:19
  28.9 0.1 pad_add_fusion
  29.0 0.0 copy-start.1
  29.0 0.7 gather_fusion
  29.6 0.1 reshape.87
  29.7 0.2 convert_reduce_fusion
  29.9 8.2 %collective-permute-done.refs_3_ = bf16[768,256]{1,0:T(8,128)(2,1)S(1)} collective-permute-done((bf16[768,256]{1,0:T(8,128)(2,1)}, bf16[768,256]{1,0:T(8,128)(2,1)S(1)}, u32[]{:S(2)}, u32[]{:S(2)}) %collective-permute-start) | collective-permute-done | bytes 393248 | tf_op jit(solution)/shard_map/ppermute | solution.py:19
  38.1 0.0 all-to-all-done
  38.1 0.0 copy-done.1
  38.1 10.0 %shard_map.84 = (bf16[1024,512]{1,0:T(8,128)(2,1)}, bf16[1024,512]{1,0:T(8,128)(2,1)}, f32[768,256]{1,0:T(8,128)S(1)}, f32[1024,256]{1,0:T(8,128)S(1)}) custom-call(s32[4]{0:T(128)S(1)} %add_subtract_fusion.refs_0_, bf16[1024,512]{1,0:T(8,128)(2,1)S(1)} %bitcast.31, bf16[1024,256]{1,0:T(8,128)(2,1)S(1)} %bitcast.29, ...), custom_call_target="tpu_custom_call" | custom-call | flops 4831838208 | bytes 6291456 | tf_op jit(solution)/shard_map/pallas_call | solution.py:165
  48.3 1.9 %collective-permute-start.1 = (bf16[768,256]{1,0:T(8,128)(2,1)S(1)}, bf16[768,256]{1,0:T(8,128)(2,1)S(1)}, u32[]{:S(2)}, u32[]{:S(2)}) collective-permute-start(bf16[768,256]{1,0:T(8,128)(2,1)S(1)} %pad_maximum_fusion.1), channel_id=1, source_target_pairs={{8,0},{16,8},{24,16},{32,24},{40,32},{48,40},{56,48},{64,56},{72,6... | collective-permute-start | bytes 1179656 | tf_op jit(solution)/shard_map/ppermute | solution.py:19
  50.2 5.4 %shard_map.85 = (bf16[1024,512]{1,0:T(8,128)(2,1)}, bf16[1024,512]{1,0:T(8,128)(2,1)}, f32[1024,256]{1,0:T(8,128)S(1)}) custom-call(s32[4]{0:T(128)S(1)} %add_subtract_fusion.refs_0_, bf16[1024,512]{1,0:T(8,128)(2,1)S(1)} %bitcast.32, bf16[1024,256]{1,0:T(8,128)(2,1)S(1)} %bitcast.30, ...), custom_call_target="tpu_custom_call", output_to_operand_aliasing={{0}: (4, {}), {1}: (5, {})} | custom-call | flops 1610612736 | bytes 6291456 | tf_op jit(solution)/shard_map/pallas_call | solution.py:165
  55.6 0.1 add.73
  55.7 16.5 %collective-permute-done.1 = bf16[768,256]{1,0:T(8,128)(2,1)S(1)} collective-permute-done((bf16[768,256]{1,0:T(8,128)(2,1)S(1)}, bf16[768,256]{1,0:T(8,128)(2,1)S(1)}, u32[]{:S(2)}, u32[]{:S(2)}) %collective-permute-start.1) | collective-permute-done | bytes 393248 | tf_op jit(solution)/shard_map/ppermute | solution.py:19
  72.3 0.1 pad_convert_fusion
  72.3 0.9 %fusion = (bf16[1024,128]{1,0:T(8,128)(2,1)}, bf16[1024,128]{1,0:T(8,128)(2,1)}) fusion(f32[1024,256]{1,0:T(8,128)S(1)} %pad_convert_fusion, f32[1024,256]{1,0:T(8,128)S(1)} %add.73), kind=kLoop, calls=%fused_computation.3 | loop fusion | flops 655360 | bytes 2621440 | tf_op jit(solution)/shard_map/convert_element_type | solution.py:234
  (6 shorter events, 0.1 us)
Async XLA Ops:
  0.6 1.0 %copy-start = (bf16[128,1024]{1,0:T(8,128)(2,1)S(1)}, bf16[128,1024]{1,0:T(8,128)(2,1)}, u32[]{:S(2)}) copy-start(bf16[128,1024]{1,0:T(8,128)(2,1)} %param.6) | copy-start | bytes 786436
  2.7 5.3 %copy-start.2 = (bf16[128,4096]{1,0:T(8,128)(2,1)S(1)}, bf16[128,4096]{1,0:T(8,128)(2,1)}, u32[]{:S(2)}) copy-start(bf16[128,4096]{1,0:T(8,128)(2,1)} %param.5) | copy-start | bytes 3145732
  3.5 14.8 %all-to-all-start.1 = ((bf16[128,8,256]{2,0,1:T(8,128)(2,1)}), bf16[128,8,256]{2,0,1:T(8,128)(2,1)S(1)}, u32[]{:S(2)}, u32[]{:S(2)}) async-start(bf16[128,8,256]{2,0,1:T(8,128)(2,1)} %pad_maximum_fusion), calls=%async_computation.1 | async-start | bytes 1048576 | tf_op jit(solution)/shard_map/all_to_all | solution.py:198
  18.3 19.8 %all-to-all-start = ((bf16[128,8,512]{2,0,1:T(8,128)(2,1)}), bf16[128,8,512]{2,0,1:T(8,128)(2,1)S(1)}, u32[]{:S(2)}, u32[]{:S(2)}) async-start(bf16[128,8,512]{2,0,1:T(8,128)(2,1)} %bitcast.27), calls=%async_computation | async-start | bytes 2097152 | tf_op jit(solution)/shard_map/all_to_all | solution.py:202
  22.1 0.7 copy-start.3
  23.9 14.2 %collective-permute-start = (bf16[768,256]{1,0:T(8,128)(2,1)}, bf16[768,256]{1,0:T(8,128)(2,1)S(1)}, u32[]{:S(2)}, u32[]{:S(2)}) collective-permute-start(bf16[768,256]{1,0:T(8,128)(2,1)} %bitcast.11), channel_id=1, source_target_pairs={{0,8},{8,16},{16,24},{24,32},{32,40},{40,48},{48,56},{56,64},{64,7... | collective-permute-start | bytes 1179656 | tf_op jit(solution)/shard_map/ppermute | solution.py:19
  29.0 9.2 %copy-start.1 = (bf16[1024,512]{1,0:T(8,128)(2,1)S(1)}, bf16[1024,512]{1,0:T(8,128)(2,1)}, u32[]{:S(2)}) copy-start(bf16[1024,512]{1,0:T(8,128)(2,1)} %refs_3_.1) | copy-start | bytes 3145732
  48.3 24.0 %collective-permute-start.1 = (bf16[768,256]{1,0:T(8,128)(2,1)S(1)}, bf16[768,256]{1,0:T(8,128)(2,1)S(1)}, u32[]{:S(2)}, u32[]{:S(2)}) collective-permute-start(bf16[768,256]{1,0:T(8,128)(2,1)S(1)} %pad_maximum_fusion.1), channel_id=1, source_target_pairs={{8,0},{16,8},{24,16},{32,24},{40,32},{48,40},{56,48},{64,56},{72,6... | collective-permute-start | bytes 1179656 | tf_op jit(solution)/shard_map/ppermute | solution.py:19

commit v6 on v5

v6 whole, which is shorter than its diff:
```python
import jax
import jax.numpy as jnp
from jax import lax
from jax.sharding import PartitionSpec as P
import functools
from jax.experimental import pallas as pl
from jax.experimental.pallas import tpu as pltpu

QUERY_HEADS = 32
KEY_VALUE_HEADS = 8
HEAD_SIZE = 128
BLOCK = 256
INTERPRET = False


def from_behind(block, axis, distance):
    devices = range(lax.axis_size(axis))
    route = [(i - distance, i) for i in devices if i - distance in devices]
    return lax.ppermute(block, axis, route)


def _nt(a, b):
    return lax.dot_general(a, b, (((1,), (1,)), ((), ())), preferred_element_type=jnp.float32)


def _tn(a, b):
    return lax.dot_general(a, b, (((0,), (0,)), ((), ())), preferred_element_type=jnp.float32)


def _nn(a, b):
    return lax.dot_general(a, b, (((1,), (0,)), ((), ())), preferred_element_type=jnp.float32)


def attention_kernel(*refs, first_unit, units, heads, with_prior, has_att, init_prior, init_own):
    refs = list(refs)
    lo_ref, q_ref, kv_ref = refs[:3]
    refs = refs[3:]
    earlier_ref = refs.pop(0) if with_prior else None
    grad_ref = refs.pop(0)
    if has_att:
        refs = refs[2:]
    prior_in = refs.pop(0) if with_prior and not init_prior else None
    own_in = None if init_own else refs.pop(0)
    att_ref, dq_ref = refs[:2]
    refs = refs[2:]
    prior_ref = refs.pop(0) if with_prior else None
    own_ref, s_scr, att_scr, dq_scr = refs
    scale = HEAD_SIZE ** (-0.5)
    step = pl.program_id(0)

    @pl.when(step == 0)
    def _():
        if with_prior:
            prior_ref[...] = (jnp.zeros(prior_ref.shape, prior_ref.dtype) if init_prior
                              else prior_in[...])
        own_ref[...] = jnp.zeros(own_ref.shape, own_ref.dtype) if init_own else own_in[...]

    rows = heads * BLOCK
    causal = (lax.broadcasted_iota(jnp.int32, (rows, BLOCK), 0) % BLOCK
              >= lax.broadcasted_iota(jnp.int32, (rows, BLOCK), 1))

    def load_kv(ref, col0, blk):
        start = pl.multiple_of(blk * BLOCK, BLOCK)
        return (ref[pl.ds(start, BLOCK), col0:col0 + HEAD_SIZE],
                ref[pl.ds(start, BLOCK), col0 + HEAD_SIZE:col0 + 2 * HEAD_SIZE])

    u = first_unit + step
    qs = jnp.concatenate(
        [q_ref[:, h * HEAD_SIZE:(h + 1) * HEAD_SIZE] for h in range(heads)], axis=0)
    dos = jnp.concatenate(
        [grad_ref[:, h * HEAD_SIZE:(h + 1) * HEAD_SIZE] for h in range(heads)], axis=0)
    lo = lo_ref[u]
    diag = units + u
    first_own = jnp.maximum(lo, units)
    segments = ((kv_ref, 0, own_ref, first_own, diag, units),)
    if with_prior:
        segments = ((earlier_ref, 0, prior_ref, lo, units, 1),) + segments

    def pass1(b, carry, ref, col0, off):
        m, l = carry
        k, _ = load_kv(ref, col0, b - off)
        s = _nt(qs, k) * scale
        s_scr[b - (u + 1)] = s
        m_new = jnp.maximum(m, jnp.max(s, axis=1, keepdims=True))
        l = l * jnp.exp(m - m_new) + jnp.sum(jnp.exp(s - m_new), axis=1, keepdims=True)
        return m_new, l

    carry = (jnp.full((rows, 1), -jnp.inf, jnp.float32), jnp.zeros((rows, 1), jnp.float32))
    for ref, col0, _, start, stop, off in segments:
        carry = lax.fori_loop(start, stop, functools.partial(pass1, ref=ref, col0=col0, off=off), carry)
    m, l = carry
    k_d, v_d = load_kv(kv_ref, 0, u)
    s = jnp.where(causal, _nt(qs, k_d) * scale, -jnp.inf)
    m_new = jnp.maximum(m, jnp.max(s, axis=1, keepdims=True))
    l = l * jnp.exp(m - m_new) + jnp.sum(jnp.exp(s - m_new), axis=1, keepdims=True)
    lse = m_new + jnp.log(l)

    def pass2(b, _, ref, col0, off):
        _, v = load_kv(ref, col0, b - off)
        p = jnp.exp(s_scr[b - (u + 1)] - lse)
        s_scr[b - (u + 1)] = p
        att_scr[...] += _nn(p.astype(jnp.bfloat16), v)
        return 0

    p = jnp.exp(s - lse)
    att_scr[...] = _nn(p.astype(jnp.bfloat16), v_d)
    for ref, col0, _, start, stop, off in segments:
        lax.fori_loop(start, stop, functools.partial(pass2, ref=ref, col0=col0, off=off), 0)
    att = att_scr[...].astype(jnp.bfloat16)
    delta = jnp.sum(dos.astype(jnp.float32) * att.astype(jnp.float32), axis=1, keepdims=True)

    def pass3(b, _, ref, col0, gref, off):
        k, v = load_kv(ref, col0, b - off)
        p = s_scr[b - (u + 1)]
        ds = (p * (_nt(dos, v) - delta)).astype(jnp.bfloat16)
        dq_scr[...] += _nn(ds, k)
        start = pl.multiple_of((b - off) * BLOCK, BLOCK)
        gref[pl.ds(start, BLOCK), 0:HEAD_SIZE] += _tn(ds, qs)
        gref[pl.ds(start, BLOCK), HEAD_SIZE:2 * HEAD_SIZE] += _tn(p.astype(jnp.bfloat16), dos)
        return 0

    ds = (p * (_nt(dos, v_d) - delta)).astype(jnp.bfloat16)
    dq_scr[...] = _nn(ds, k_d)
    r0 = pl.multiple_of(u * BLOCK, BLOCK)
    own_ref[pl.ds(r0, BLOCK), 0:HEAD_SIZE] += _tn(ds, qs)
    own_ref[pl.ds(r0, BLOCK), HEAD_SIZE:2 * HEAD_SIZE] += _tn(p.astype(jnp.bfloat16), dos)
    for ref, col0, gref, start, stop, off in segments:
        lax.fori_loop(start, stop, functools.partial(pass3, ref=ref, col0=col0, gref=gref, off=off), 0)
    dq = (dq_scr[...] * scale).astype(jnp.bfloat16)
    for h in range(heads):
        att_ref[:, h * HEAD_SIZE:(h + 1) * HEAD_SIZE] = att[h * BLOCK:(h + 1) * BLOCK]
        dq_ref[:, h * HEAD_SIZE:(h + 1) * HEAD_SIZE] = dq[h * BLOCK:(h + 1) * BLOCK]


def attention_call(lo, q, q_block, kv, earlier, grad, grad_block, unit_list, att=None, prior=None,
                   own=None, *, heads, interpret=False):
    ctx_rows = q.shape[0]
    units = ctx_rows // BLOCK
    width = heads * HEAD_SIZE
    kv_cols = 2 * HEAD_SIZE
    with_prior = earlier is not None
    first_unit = unit_list[0]
    steps = len(unit_list)
    kernel = functools.partial(attention_kernel, first_unit=first_unit, units=units, heads=heads,
                               with_prior=with_prior, has_att=att is not None,
                               init_prior=prior is None, init_own=own is None)
    rows = heads * BLOCK

    def whole(x):
        return pl.BlockSpec(x.shape, lambda i: (0,) * len(x.shape))

    operands = [lo, q, kv]
    in_specs = [pl.BlockSpec(memory_space=pltpu.SMEM),
                pl.BlockSpec((BLOCK, width), lambda i: (first_unit + i, q_block)),
                pl.BlockSpec((ctx_rows, kv_cols), lambda i: (0, 0))]
    if with_prior:
        operands.append(earlier)
        in_specs.append(whole(earlier))
    out_block = pl.BlockSpec((BLOCK, width), lambda i: (first_unit + i, grad_block))
    operands.append(grad)
    in_specs.append(out_block)
    aliases = {}
    if att is not None:
        aliases[len(operands)] = 0
        aliases[len(operands) + 1] = 1
        operands += list(att)
        in_specs += [pl.BlockSpec(memory_space=pl.ANY)] * 2
    n_out = 2
    if with_prior:
        if prior is not None:
            aliases[len(operands)] = n_out
            operands.append(prior)
            in_specs.append(whole(prior))
        n_out += 1
    if own is not None:
        aliases[len(operands)] = n_out
        operands.append(own)
        in_specs.append(whole(own))
    out_shape = [jax.ShapeDtypeStruct(grad.shape, jnp.bfloat16)] * 2
    out_specs = [out_block] * 2
    if with_prior:
        out_shape.append(jax.ShapeDtypeStruct(earlier.shape, jnp.float32))
        out_specs.append(whole(earlier))
    out_shape.append(jax.ShapeDtypeStruct((ctx_rows, kv_cols), jnp.float32))
    out_specs.append(pl.BlockSpec((ctx_rows, kv_cols), lambda i: (0, 0)))
    visible_blocks = 4 * steps
    flops = 12 * rows * BLOCK * HEAD_SIZE * visible_blocks
    return pl.pallas_call(
        kernel,
        grid=(steps,),
        out_shape=tuple(out_shape),
        in_specs=in_specs,
        out_specs=tuple(out_specs),
        scratch_shapes=[
            pltpu.VMEM((units, rows, BLOCK), jnp.float32),
            pltpu.VMEM((rows, HEAD_SIZE), jnp.float32),
            pltpu.VMEM((rows, HEAD_SIZE), jnp.float32),
        ],
        input_output_aliases=aliases,
        compiler_params=pltpu.CompilerParams(
            dimension_semantics=("arbitrary",), vmem_limit_bytes=48 * 1024 * 1024),
        cost_estimate=pl.CostEstimate(flops=flops, transcendentals=2 * rows * BLOCK * visible_blocks,
                                      bytes_accessed=3 * 1024 * 1024),
        interpret=interpret,
    )(*operands)


def local(query_matrix, key_matrix, value_matrix, output_gradient, doc_start):
    token_per_shard = query_matrix.shape[0]
    head_groups = lax.axis_size("head")
    q_cols = query_matrix.shape[1] // head_groups
    k_cols = key_matrix.shape[1] // head_groups
    assert k_cols == HEAD_SIZE and 2 * token_per_shard == BLOCK
    heads = q_cols // HEAD_SIZE
    half = heads // 2
    assert half * 2 == heads and half * HEAD_SIZE == 2 * k_cols
    query_groups = query_matrix.reshape(token_per_shard, head_groups, q_cols)
    first_packed = jnp.concatenate(
        [
            key_matrix.reshape(token_per_shard, head_groups, k_cols),
            value_matrix.reshape(token_per_shard, head_groups, k_cols),
            query_groups[:, :, : half * HEAD_SIZE],
        ],
        axis=2,
    )
    first = lax.all_to_all(first_packed, "head", split_axis=1, concat_axis=0, tiled=True)
    ctx_rows = first.shape[0]
    first = first.reshape(ctx_rows, 4 * k_cols)
    earlier_kv = from_behind(first[BLOCK:, : 2 * k_cols], "ctx", 1)
    second = lax.all_to_all(
        query_groups[:, :, half * HEAD_SIZE:], "head", split_axis=1, concat_axis=0, tiled=True
    ).reshape(ctx_rows, half * HEAD_SIZE)
    units = ctx_rows // BLOCK
    ctx_index = lax.axis_index("ctx")
    unit_doc = jnp.cumsum(doc_start)
    own_units = lax.dynamic_slice_in_dim(unit_doc, ctx_index * units, units)
    prior_units = lax.dynamic_slice_in_dim(unit_doc, jnp.maximum(ctx_index - 1, 0) * units, units)
    prior_units = jnp.where(ctx_index > 0, prior_units, -1)
    joined_units = jnp.concatenate([prior_units, own_units])
    unit_ids = jnp.arange(units, dtype=jnp.int32)
    window = unit_ids[:, None] + 1 + unit_ids[None, :]
    same = (joined_units[window] == own_units[:, None]).astype(jnp.int32)
    lo = (unit_ids + units + 1 - jnp.sum(same, axis=1)).astype(jnp.int32)
    call = functools.partial(attention_call, heads=half, interpret=INTERPRET)
    last_unit = [units - 1]
    early_units = range(units - 1)
    att, dq, own = call(lo, first, 1, first, None, output_gradient, 0, last_unit)
    att, dq, prior, own = call(lo, first, 1, first, earlier_kv, output_gradient, 0, early_units,
                               (att, dq), None, own)
    att, dq, prior, own = call(lo, second, 0, first, earlier_kv, output_gradient, 1, early_units,
                               (att, dq), prior, own)
    score_scale = HEAD_SIZE ** (-0.5)
    prior_grads = jnp.concatenate(
        [(prior[:, :k_cols] * score_scale).astype(jnp.bfloat16),
         prior[:, k_cols:].astype(jnp.bfloat16)],
        axis=1,
    )
    later = from_behind(prior_grads, "ctx", -1).astype(jnp.float32)
    att, dq, own = call(lo, second, 0, first, None, output_gradient, 1, last_unit, (att, dq), None, own)
    later = jnp.concatenate([jnp.zeros((BLOCK, 2 * k_cols), jnp.float32), later], axis=0)
    summed_keys = (own[:, :k_cols] * score_scale + later[:, :k_cols]).astype(jnp.bfloat16)
    summed_values = (own[:, k_cols:] + later[:, k_cols:]).astype(jnp.bfloat16)
    return (att, dq, summed_keys, summed_values)


def solution(mesh):
    placed = (
        P(("ctx", "head"), None),
        P(("ctx", "head"), None),
        P(("ctx", "head"), None),
        P("ctx", "head"),
        P(),
    )
    return jax.shard_map(
        local,
        mesh=mesh,
        in_specs=placed,
        out_specs=(P("ctx", "head"), P("ctx", "head"), P("ctx", "head"), P("ctx", "head")),
        check_vma=False,
    )
```

time: 73.6 us -> 90.6 us (1.23)
  Pallas kernels: 15.4 us -> 28.7 us
  local copies, waits for them, and re-layouts: 5.49 us -> 8.5 us
    pallas_call x2 -> x4, Pallas kernels: 15.4 us -> 28.7 us  [attention_call(): pl.pallas_call(kernel, grid=(steps,), out_shape=tuple(out_shape), in_spec...]
    unnamed x8 -> x19, local copies, waits for them, and re-layouts: 1.62 us -> 7.32 us
    ppermute x2, waiting for transfers between devices: 24.7 us -> 20.1 us  [from_behind(): return lax.ppermute(block, axis, route)]
    all_to_all x2, waiting for transfers between devices: 9.24 us -> 13.6 us  [the longest x1 13.6 us: local(): lax.all_to_all(first_packed, 'head', split_axis=1, concat_axis=0, tiled=T...]
    reshape x2 -> x1, local copies, waits for them, and re-layouts: 1.18 us -> 0.11 us  [the longest x1 1.07 us: local(): query_matrix.reshape(token_per_shard, head_groups, q_cols)]
    reshape x1, local copies, waits for them, and re-layouts: 1.07 us -> 0.12 us  [local(): value_matrix.reshape(token_per_shard, head_groups, k_cols)]
  transfers between devices with their start and end apart: 4 -> 4, of which waited for: 3 -> 3; matrix products, arithmetic and copies ran while one was open for 5% -> 3% of each run, Pallas kernels for 7% -> 20%
where the time goes in v6:
time: 90.6 us; the launch traced here: 90 us
  waiting for transfers between devices  33.7 us (37%)
  Pallas kernels  28.7 us (32%)
  starting transfers between devices  15.6 us (17%)
  local copies, waits for them, and re-layouts  8.5 us (9%)
  other arithmetic  2.8 us (3%)
    pallas_call x4, Pallas kernels, attention_call(): pl.pallas_call(kernel, grid=(steps,), out_shape=tuple(out_shape), in_spec...  28.7 us
    ppermute x2, waiting for transfers between devices, from_behind(): return lax.ppermute(block, axis, route)  20.1 us
    all_to_all x1, waiting for transfers between devices, local(): lax.all_to_all(first_packed, 'head', split_axis=1, concat_axis=0, tiled=T...  13.6 us
    unnamed x19, local copies, waits for them, and re-layouts  7.32 us
    ppermute x2, starting transfers between devices, from_behind(): return lax.ppermute(block, axis, route)  6.87 us
    all_to_all x1, starting transfers between devices, local(): lax.all_to_all(first_packed, 'head', split_axis=1, concat_axis=0, tiled=T...  4.6 us
    all_to_all x1, starting transfers between devices, local(): lax.all_to_all(query_groups[:, :, half * HEAD_SIZE:], 'head', split_axis=...  4.16 us
  transfers between devices with their start and end apart: 4, of which 3 were waited for; matrix products, arithmetic and copies ran while one was open for 3% of the time, Pallas kernels for 20%

profile of v6, /device:TPU:102, one launch (start us, length us, event | category | flops | bytes accessed | tf_op | source)
XLA Modules:
  0.0 90.0 jit_solution(411191781746226378)
XLA Ops:
  0.6 0.0 copy-start
  0.6 1.7 %copy.33 = bf16[16,8,8,512]{3,2,1,0:T(8,128)(2,1)S(1)} copy(bf16[16,8,8,512]{3,1,2,0:T(8,128)(2,1)} %bitcast.33) | data formatting | bytes 2097152
  2.3 0.1 fusion.2
  2.4 0.0 copy-start.6
  2.4 0.1 copy.30
  2.5 0.0 copy-done
  2.5 0.8 copy-done.6
  3.3 0.1 copy_bitcast_fusion
  3.5 1.1 %pad_maximum_fusion = bf16[128,8,512]{2,0,1:T(8,128)(2,1)} fusion(bf16[128,8,256]{2,0,1:T(8,128)(2,1)S(1)} %copy.30, bf16[128,8,128]{2,0,1:T(8,128)(2,1)S(1)} %get-tuple-element.38, bf16[128,8,128]{2,0,1:T(8,128)(2,1)S(1)} %get-tuple-element.39), kind=kLoop, calls=%fused_computation.1 | loop fusion | flops 3145728 | bytes 2097152 | tf_op jit(solution)/shard_map/concatenate | solution.py:218
  4.5 0.0 copy-start.7
  4.5 4.6 %all-to-all-start.1 = ((bf16[128,8,512]{2,0,1:T(8,128)(2,1)}), bf16[128,8,512]{2,0,1:T(8,128)(2,1)S(1)}, u32[]{:S(2)}, u32[]{:S(2)}) async-start(bf16[128,8,512]{2,0,1:T(8,128)(2,1)} %pad_maximum_fusion), calls=%async_computation.1 | async-start | bytes 2097152 | tf_op jit(solution)/shard_map/all_to_all | solution.py:226
  9.2 0.1 compare_select_fusion
  9.2 0.1 reshape.87
  9.3 0.0 copy-done.7
  9.3 0.1 copy.24
  9.4 0.2 reduce-window.4
  9.6 0.1 select_reduce_fusion
  9.7 0.1 pad_add_fusion
  9.8 0.7 gather_fusion
  10.5 0.1 reshape.86
  10.6 0.9 %copy.29 = bf16[128,8,256]{2,0,1:T(8,128)(2,1)} copy(bf16[128,8,256]{2,1,0:T(8,128)(2,1)S(1)} %get-tuple-element.37) | data formatting | bytes 1048576
  11.5 0.0 copy-start.1
  11.5 13.6 %all-to-all-done.1 = bf16[128,8,512]{2,0,1:T(8,128)(2,1)S(1)} async-done(((bf16[128,8,512]{2,0,1:T(8,128)(2,1)}), bf16[128,8,512]{2,0,1:T(8,128)(2,1)S(1)}, u32[]{:S(2)}, u32[]{:S(2)}) %all-to-all-start.1) | async-done | bytes 1048608 | tf_op jit(solution)/shard_map/all_to_all | solution.py:226
  25.1 4.2 %all-to-all-start = ((bf16[128,8,256]{2,0,1:T(8,128)(2,1)}), bf16[128,8,256]{2,0,1:T(8,128)(2,1)}, u32[]{:S(2)}, u32[]{:S(2)}) async-start(bf16[128,8,256]{2,0,1:T(8,128)(2,1)} %copy.29), calls=%async_computation | async-start | bytes 1048576 | tf_op jit(solution)/shard_map/all_to_all | solution.py:230
  29.3 5.0 %collective-permute-start = (bf16[768,256]{1,0:T(8,128)(2,1)S(1)}, bf16[768,256]{1,0:T(8,128)(2,1)S(1)}, u32[]{:S(2)}, u32[]{:S(2)}) collective-permute-start(bf16[768,256]{1,0:T(8,128)(2,1)S(1)} %slice.41), channel_id=1, source_target_pairs={{0,8},{8,16},{16,24},{24,32},{32,40},{40,48},{48,56},{56,64},{64,7... | collective-permute-start | bytes 1179656 | tf_op jit(solution)/shard_map/ppermute | solution.py:19
  34.2 0.2 convert_reduce_fusion
  34.4 0.0 copy-done.1
  34.4 4.0 %shard_map.84 = (bf16[1024,512]{1,0:T(8,128)(2,1)}, bf16[1024,512]{1,0:T(8,128)(2,1)}, f32[1024,256]{1,0:T(8,128)S(1)}) custom-call(s32[4]{0:T(128)S(1)} %add_subtract_fusion.refs_0_, bf16[1024,512]{1,0:T(8,128)(2,1)S(1)} %bitcast.26, bf16[1024,512]{1,0:T(8,128)(2,1)S(1)} %bitcast.27, bf16[1024,512]{1,0:T(8,128)(2,1)S(1)} %copy-done.1), custom_call_target="tpu_custom_call" | custom-call | flops 805306368 | bytes 3145728 | tf_op jit(solution)/shard_map/pallas_call | solution.py:188
  38.5 4.7 %collective-permute-done.refs_3_ = bf16[768,256]{1,0:T(8,128)(2,1)S(1)} collective-permute-done((bf16[768,256]{1,0:T(8,128)(2,1)S(1)}, bf16[768,256]{1,0:T(8,128)(2,1)S(1)}, u32[]{:S(2)}, u32[]{:S(2)}) %collective-permute-start) | collective-permute-done | bytes 393248 | tf_op jit(solution)/shard_map/ppermute | solution.py:19
  43.1 9.9 %shard_map.85 = (bf16[1024,512]{1,0:T(8,128)(2,1)}, bf16[1024,512]{1,0:T(8,128)(2,1)}, f32[768,256]{1,0:T(8,128)S(1)}, f32[1024,256]{1,0:T(8,128)S(1)}) custom-call(s32[4]{0:T(128)S(1)} %add_subtract_fusion.refs_0_, bf16[1024,512]{1,0:T(8,128)(2,1)S(1)} %bitcast.28, ...), custom_call_target="tpu_custom_call", output_to_operand_aliasing={{0}: (5, {}), {1}: (6, {}), {3}: (7, {})} | custom-call | flops 2415919104 | bytes 3145728 | tf_op jit(solution)/shard_map/pallas_call | solution.py:188
  53.0 0.0 copy-start.2
  53.0 0.9 copy-done.2
  53.9 0.0 copy-start.4
  53.9 0.8 copy-done.4
  54.7 0.0 all-to-all-done
  54.7 0.0 copy-start.3
  54.7 1.1 %copy-done.3 = f32[768,256]{1,0:T(8,128)S(1)} copy-done((f32[768,256]{1,0:T(8,128)S(1)}, f32[768,256]{1,0:T(8,128)}, u32[]{:S(2)}) %copy-start.3) | copy-done | bytes 786456
  55.8 0.0 copy-start.5
  55.8 1.0 %copy-done.5 = bf16[768,256]{1,0:T(8,128)(2,1)S(1)} copy-done((bf16[768,256]{1,0:T(8,128)(2,1)S(1)}, bf16[768,256]{1,0:T(8,128)(2,1)}, u32[]{:S(2)}) %copy-start.5) | copy-done | bytes 393240
  56.8 10.3 %shard_map.86 = (bf16[1024,512]{1,0:T(8,128)(2,1)}, bf16[1024,512]{1,0:T(8,128)(2,1)}, f32[768,256]{1,0:T(8,128)S(1)}, f32[1024,256]{1,0:T(8,128)S(1)}) custom-call(s32[4]{0:T(128)S(1)} %add_subtract_fusion.refs_0_, bf16[1024,256]{1,0:T(8,128)(2,1)} %bitcast.3.refs_1_, ...), custom_call_target="tpu_custom_call", output_to_operand_aliasing={{0}: (5, {}), {1}: (6, {}), {2}: (7, {}), {3}: (8, {})} | custom-call | flops 2415919104 | bytes 3145728 | tf_op jit(solution)/shard_map/pallas_call | solution.py:188
  67.2 1.9 %collective-permute-start.1 = (bf16[768,256]{1,0:T(8,128)(2,1)S(1)}, bf16[768,256]{1,0:T(8,128)(2,1)S(1)}, u32[]{:S(2)}, u32[]{:S(2)}) collective-permute-start(bf16[768,256]{1,0:T(8,128)(2,1)S(1)} %pad_maximum_fusion.1), channel_id=1, source_target_pairs={{8,0},{16,8},{24,16},{32,24},{40,32},{48,40},{56,48},{64,56},{72,6... | collective-permute-start | bytes 1179656 | tf_op jit(solution)/shard_map/ppermute | solution.py:19
  69.1 4.5 %shard_map.87 = (bf16[1024,512]{1,0:T(8,128)(2,1)}, bf16[1024,512]{1,0:T(8,128)(2,1)}, f32[1024,256]{1,0:T(8,128)S(1)}) custom-call(s32[4]{0:T(128)S(1)} %add_subtract_fusion.refs_0_, bf16[1024,256]{1,0:T(8,128)(2,1)} %bitcast.3.refs_1_, bf16[1024,512]{1,0:T(8,128)(2,1)S(1)} %bitcast.31, ...), custom_call_target="tpu_custom_call", output_to_operand_aliasing={{0}: (4, {}), {1}: (5, {}), {2}: (6, {})} | custom-call | flops 805306368 | bytes 3145728 | tf_op jit(solution)/shard_map/pallas_call | solution.py:188
  73.6 15.4 %collective-permute-done.1 = bf16[768,256]{1,0:T(8,128)(2,1)S(1)} collective-permute-done((bf16[768,256]{1,0:T(8,128)(2,1)S(1)}, bf16[768,256]{1,0:T(8,128)(2,1)S(1)}, u32[]{:S(2)}, u32[]{:S(2)}) %collective-permute-start.1) | collective-permute-done | bytes 393248 | tf_op jit(solution)/shard_map/ppermute | solution.py:19
  89.0 0.1 pad_convert_fusion
  89.1 0.9 %fusion = (bf16[1024,128]{1,0:T(8,128)(2,1)}, bf16[1024,128]{1,0:T(8,128)(2,1)}) fusion(f32[1024,256]{1,0:T(8,128)S(1)} %pad_convert_fusion, f32[1024,256]{1,0:T(8,128)S(1)} %get-tuple-element.30), kind=kLoop, calls=%fused_computation.3 | loop fusion | flops 655360 | bytes 2621440 | tf_op jit(solution)/shard_map/convert_element_type | solution.py:262
  (7 shorter events, 0.2 us)
Async XLA Ops:
  0.6 1.9 %copy-start = (bf16[128,1024]{1,0:T(8,128)(2,1)S(1)}, bf16[128,1024]{1,0:T(8,128)(2,1)}, u32[]{:S(2)}) copy-start(bf16[128,1024]{1,0:T(8,128)(2,1)} %param.6) | copy-start | bytes 786436
  2.4 1.0 %copy-start.6 = (bf16[128,1024]{1,0:T(8,128)(2,1)S(1)}, bf16[128,1024]{1,0:T(8,128)(2,1)}, u32[]{:S(2)}) copy-start(bf16[128,1024]{1,0:T(8,128)(2,1)} %param.7) | copy-start | bytes 786436
  4.5 4.8 %copy-start.7 = (s32[128]{0:T(128)S(1)}, s32[128]{0:T(128)}, u32[]{:S(2)}) copy-start(s32[128]{0:T(128)} %param.9) | copy-start | bytes 1540
  4.5 20.5 %all-to-all-start.1 = ((bf16[128,8,512]{2,0,1:T(8,128)(2,1)}), bf16[128,8,512]{2,0,1:T(8,128)(2,1)S(1)}, u32[]{:S(2)}, u32[]{:S(2)}) async-start(bf16[128,8,512]{2,0,1:T(8,128)(2,1)} %pad_maximum_fusion), calls=%async_computation.1 | async-start | bytes 2097152 | tf_op jit(solution)/shard_map/all_to_all | solution.py:226
  11.5 22.9 %copy-start.1 = (bf16[1024,512]{1,0:T(8,128)(2,1)S(1)}, bf16[1024,512]{1,0:T(8,128)(2,1)}, u32[]{:S(2)}) copy-start(bf16[1024,512]{1,0:T(8,128)(2,1)} %refs_3_.3) | copy-start | bytes 3145732
  25.1 29.6 %all-to-all-start = ((bf16[128,8,256]{2,0,1:T(8,128)(2,1)}), bf16[128,8,256]{2,0,1:T(8,128)(2,1)}, u32[]{:S(2)}, u32[]{:S(2)}) async-start(bf16[128,8,256]{2,0,1:T(8,128)(2,1)} %copy.29), calls=%async_computation | async-start | bytes 1048576 | tf_op jit(solution)/shard_map/all_to_all | solution.py:230
  29.3 13.8 %collective-permute-start = (bf16[768,256]{1,0:T(8,128)(2,1)S(1)}, bf16[768,256]{1,0:T(8,128)(2,1)S(1)}, u32[]{:S(2)}, u32[]{:S(2)}) collective-permute-start(bf16[768,256]{1,0:T(8,128)(2,1)S(1)} %slice.41), channel_id=1, source_target_pairs={{0,8},{8,16},{16,24},{24,32},{32,40},{40,48},{48,56},{56,64},{64,7... | collective-permute-start | bytes 1179656 | tf_op jit(solution)/shard_map/ppermute | solution.py:19
  53.0 0.9 copy-start.2
  53.9 0.8 copy-start.4
  54.7 1.1 %copy-start.3 = (f32[768,256]{1,0:T(8,128)S(1)}, f32[768,256]{1,0:T(8,128)}, u32[]{:S(2)}) copy-start(f32[768,256]{1,0:T(8,128)} %copy-done.2) | copy-start | bytes 2359300
  55.8 1.0 %copy-start.5 = (bf16[768,256]{1,0:T(8,128)(2,1)S(1)}, bf16[768,256]{1,0:T(8,128)(2,1)}, u32[]{:S(2)}) copy-start(bf16[768,256]{1,0:T(8,128)(2,1)} %copy-done.4) | copy-start | bytes 1179652
  67.2 21.8 %collective-permute-start.1 = (bf16[768,256]{1,0:T(8,128)(2,1)S(1)}, bf16[768,256]{1,0:T(8,128)(2,1)S(1)}, u32[]{:S(2)}, u32[]{:S(2)}) collective-permute-start(bf16[768,256]{1,0:T(8,128)(2,1)S(1)} %pad_maximum_fusion.1), channel_id=1, source_target_pairs={{8,0},{16,8},{24,16},{32,24},{40,32},{48,40},{56,48},{64,56},{72,6... | collective-permute-start | bytes 1179656 | tf_op jit(solution)/shard_map/ppermute | solution.py:19

commit v7 on v5

--- a/solution.py
+++ b/solution.py
@@ -73,33 +73,38 @@
         if with_prior:
             segments = ((earlier_ref, 0, prior_ref, lo, units, 1),) + segments
 
-        def pass1(b, carry, ref, col0, off):
-            m, l = carry
+        half = BLOCK // 2
+
+        def pass1(b, m, ref, col0, off):
             k, _ = load_kv(ref, col0, b - off)
             s = _nt(qs, k) * scale
             s_scr[b - (u + 1)] = s
-            m_new = jnp.maximum(m, jnp.max(s, axis=1, keepdims=True))
-            l = l * jnp.exp(m - m_new) + jnp.sum(jnp.exp(s - m_new), axis=1, keepdims=True)
-            return m_new, l
-
-        carry = (jnp.full((rows, 1), -jnp.inf, jnp.float32), jnp.zeros((rows, 1), jnp.float32))
-        for ref, col0, _, start, stop, off in segments:
-            carry = lax.fori_loop(start, stop, functools.partial(pass1, ref=ref, col0=col0, off=off), carry)
-        m, l = carry
+            return jnp.maximum(m, jnp.maximum(s[:, :half], s[:, half:]))
+
         k_d, v_d = load_kv(kv_ref, 0, u)
         s = jnp.where(causal, _nt(qs, k_d) * scale, -jnp.inf)
-        m_new = jnp.maximum(m, jnp.max(s, axis=1, keepdims=True))
-        l = l * jnp.exp(m - m_new) + jnp.sum(jnp.exp(s - m_new), axis=1, keepdims=True)
-        lse = m_new + jnp.log(l)
+        m = jnp.maximum(s[:, :half], s[:, half:])
+        for ref, col0, _, start, stop, off in segments:
+            m = lax.fori_loop(start, stop, functools.partial(pass1, ref=ref, col0=col0, off=off), m)
+        m = jnp.max(m, axis=1, keepdims=True)
+
+        def pass1b(b, l):
+            e = jnp.exp(s_scr[b - (u + 1)] - m)
+            s_scr[b - (u + 1)] = e
+            return l + e[:, :half] + e[:, half:]
+
+        e = jnp.exp(s - m)
+        l = lax.fori_loop(lo, diag, pass1b, e[:, :half] + e[:, half:])
+        inv_total = 1.0 / jnp.sum(l, axis=1, keepdims=True)
 
         def pass2(b, _, ref, col0, off):
             _, v = load_kv(ref, col0, b - off)
-            p = jnp.exp(s_scr[b - (u + 1)] - lse)
+            p = s_scr[b - (u + 1)] * inv_total
             s_scr[b - (u + 1)] = p
             att_scr[...] += _nn(p.astype(jnp.bfloat16), v)
             return 0
 
-        p = jnp.exp(s - lse)
+        p = e * inv_total
         att_scr[...] = _nn(p.astype(jnp.bfloat16), v_d)
         for ref, col0, _, start, stop, off in segments:
             lax.fori_loop(start, stop, functools.partial(pass2, ref=ref, col0=col0, off=off), 0)

time: 73.6 us -> 72.4 us (0.984)
  waiting for transfers between devices: 34 us -> 29.6 us
  starting transfers between devices: 14.9 us -> 18.9 us
  Pallas kernels: 15.4 us -> 14.6 us
    ppermute x2, waiting for transfers between devices: 24.7 us -> 20.4 us  [from_behind(): return lax.ppermute(block, axis, route)]
    ppermute x2, starting transfers between devices: 6.86 us -> 10.9 us  [from_behind(): return lax.ppermute(block, axis, route)]
    pallas_call x2, Pallas kernels: 15.4 us -> 14.6 us  [attention_call(): pl.pallas_call(kernel, grid=(steps,), out_shape=tuple(out_shape), in_spec...]
where the time goes in v7:
time: 72.4 us; the launch traced here: 72 us
  waiting for transfers between devices  29.6 us (41%)
  starting transfers between devices  18.9 us (26%)
  Pallas kernels  14.6 us (20%)
  local copies, waits for them, and re-layouts  5.49 us (8%)
  other arithmetic  2.71 us (4%)
  between operations  0.76 us (1%)
    ppermute x2, waiting for transfers between devices, from_behind(): return lax.ppermute(block, axis, route)  20.4 us
    pallas_call x2, Pallas kernels, attention_call(): pl.pallas_call(kernel, grid=(steps,), out_shape=tuple(out_shape), in_spec...  14.6 us
    ppermute x2, starting transfers between devices, from_behind(): return lax.ppermute(block, axis, route)  10.9 us
    all_to_all x1, waiting for transfers between devices, local(): lax.all_to_all(kv_packed, 'head', split_axis=1, concat_axis=0, tiled=True)  9.24 us
    all_to_all x1, starting transfers between devices, local(): lax.all_to_all(kv_packed, 'head', split_axis=1, concat_axis=0, tiled=True)  4.47 us
    all_to_all x1, starting transfers between devices, local(): lax.all_to_all(query_matrix.reshape(token_per_shard, head_groups, q_cols)...  3.56 us
    unnamed x8, local copies, waits for them, and re-layouts  1.62 us
  transfers between devices with their start and end apart: 4, of which 3 were waited for; matrix products, arithmetic and copies ran while one was open for 5% of the time, Pallas kernels for 7%

profile of v7, /device:TPU:102, one launch (start us, length us, event | category | flops | bytes accessed | tf_op | source)
XLA Modules:
  0.0 72.0 jit_solution(17623270734918250249)
XLA Ops:
  0.6 0.0 copy-start
  0.6 0.9 %copy-done = bf16[128,1024]{1,0:T(8,128)(2,1)S(1)} copy-done((bf16[128,1024]{1,0:T(8,128)(2,1)S(1)}, bf16[128,1024]{1,0:T(8,128)(2,1)}, u32[]{:S(2)}) %copy-start) | copy-done | bytes 262168
  1.6 1.1 %copy_bitcast_fusion.1 = (bf16[128,8,128]{2,0,1:T(8,128)(2,1)S(1)}, bf16[128,8,128]{2,0,1:T(8,128)(2,1)S(1)}) fusion(bf16[128,1024]{1,0:T(8,128)(2,1)S(1)} %copy-done, bf16[128,1024]{1,0:T(8,128)(2,1)} %param.7), kind=kLoop, calls=%fused_computation.12 | loop fusion | bytes 1048576 | tf_op jit(solution)/shard_map/reshape | solution.py:199
  2.7 0.0 copy-start.2
  2.7 0.9 %pad_maximum_fusion = bf16[128,8,256]{2,0,1:T(8,128)(2,1)} fusion(bf16[128,8,128]{2,0,1:T(8,128)(2,1)S(1)} %get-tuple-element.22, bf16[128,8,128]{2,0,1:T(8,128)(2,1)S(1)} %get-tuple-element.23), kind=kLoop, calls=%fused_computation.7 | loop fusion | flops 1048576 | bytes 1048576 | tf_op jit(solution)/shard_map/concatenate | solution.py:196
  3.5 4.5 %all-to-all-start.1 = ((bf16[128,8,256]{2,0,1:T(8,128)(2,1)}), bf16[128,8,256]{2,0,1:T(8,128)(2,1)S(1)}, u32[]{:S(2)}, u32[]{:S(2)}) async-start(bf16[128,8,256]{2,0,1:T(8,128)(2,1)} %pad_maximum_fusion), calls=%async_computation.1 | async-start | bytes 1048576 | tf_op jit(solution)/shard_map/all_to_all | solution.py:203
  8.0 0.0 copy-done.2
  8.0 1.1 %copy.25 = bf16[16,8,8,512]{3,2,0,1:T(8,128)(2,1)} copy(bf16[16,8,8,512]{3,2,1,0:T(8,128)(2,1)S(1)} %bitcast.33) | data formatting | bytes 2097152 | tf_op jit(solution)/shard_map/reshape | solution.py:208
  9.1 9.2 %all-to-all-done.1 = bf16[128,8,256]{2,0,1:T(8,128)(2,1)S(1)} async-done(((bf16[128,8,256]{2,0,1:T(8,128)(2,1)}), bf16[128,8,256]{2,0,1:T(8,128)(2,1)S(1)}, u32[]{:S(2)}, u32[]{:S(2)}) %all-to-all-start.1) | async-done | bytes 524320 | tf_op jit(solution)/shard_map/all_to_all | solution.py:203
  18.3 3.6 %all-to-all-start = ((bf16[128,8,512]{2,0,1:T(8,128)(2,1)}), bf16[128,8,512]{2,0,1:T(8,128)(2,1)S(1)}, u32[]{:S(2)}, u32[]{:S(2)}) async-start(bf16[128,8,512]{2,0,1:T(8,128)(2,1)} %bitcast.27), calls=%async_computation | async-start | bytes 2097152 | tf_op jit(solution)/shard_map/all_to_all | solution.py:207
  21.9 0.1 compare_select_fusion
  22.0 0.1 reshape.88
  22.1 0.0 copy-start.3
  22.1 0.7 copy-done.3
  22.7 0.1 copy.15
  22.8 0.2 reduce-window.4
  23.0 0.1 select_reduce_fusion
  23.2 0.8 %slice.35 = bf16[6,128,1,256]{3,1,0,2:T(8,128)(2,1)} slice(bf16[8,128,1,256]{3,1,0,2:T(8,128)(2,1)S(1)} %bitcast.28), slice={[2:8], [0:128], [0:1], [0:256]} | slice | bytes 786432 | tf_op jit(solution)/shard_map/slice | solution.py:206
  23.9 4.9 %collective-permute-start = (bf16[768,256]{1,0:T(8,128)(2,1)}, bf16[768,256]{1,0:T(8,128)(2,1)S(1)}, u32[]{:S(2)}, u32[]{:S(2)}) collective-permute-start(bf16[768,256]{1,0:T(8,128)(2,1)} %bitcast.11), channel_id=1, source_target_pairs={{0,8},{8,16},{16,24},{24,32},{32,40},{40,48},{48,56},{56,64},{64,7... | collective-permute-start | bytes 1179656 | tf_op jit(solution)/shard_map/ppermute | solution.py:19
  28.9 0.1 pad_add_fusion
  29.0 0.0 copy-start.1
  29.0 0.7 gather_fusion
  29.6 0.1 reshape.87
  29.7 0.2 convert_reduce_fusion
  29.9 8.2 %collective-permute-done.refs_3_ = bf16[768,256]{1,0:T(8,128)(2,1)S(1)} collective-permute-done((bf16[768,256]{1,0:T(8,128)(2,1)}, bf16[768,256]{1,0:T(8,128)(2,1)S(1)}, u32[]{:S(2)}, u32[]{:S(2)}) %collective-permute-start) | collective-permute-done | bytes 393248 | tf_op jit(solution)/shard_map/ppermute | solution.py:19
  38.1 0.0 all-to-all-done
  38.1 0.0 copy-done.1
  38.1 9.4 %shard_map.84 = (bf16[1024,512]{1,0:T(8,128)(2,1)}, bf16[1024,512]{1,0:T(8,128)(2,1)}, f32[768,256]{1,0:T(8,128)S(1)}, f32[1024,256]{1,0:T(8,128)S(1)}) custom-call(s32[4]{0:T(128)S(1)} %add_subtract_fusion.refs_0_, bf16[1024,512]{1,0:T(8,128)(2,1)S(1)} %bitcast.31, bf16[1024,256]{1,0:T(8,128)(2,1)S(1)} %bitcast.29, ...), custom_call_target="tpu_custom_call" | custom-call | flops 4831838208 | bytes 6291456 | tf_op jit(solution)/shard_map/pallas_call | solution.py:170
  47.6 5.9 %collective-permute-start.1 = (bf16[768,256]{1,0:T(8,128)(2,1)S(1)}, bf16[768,256]{1,0:T(8,128)(2,1)S(1)}, u32[]{:S(2)}, u32[]{:S(2)}) collective-permute-start(bf16[768,256]{1,0:T(8,128)(2,1)S(1)} %pad_maximum_fusion.1), channel_id=1, source_target_pairs={{8,0},{16,8},{24,16},{32,24},{40,32},{48,40},{56,48},{64,56},{72,6... | collective-permute-start | bytes 1179656 | tf_op jit(solution)/shard_map/ppermute | solution.py:19
  53.6 5.2 %shard_map.85 = (bf16[1024,512]{1,0:T(8,128)(2,1)}, bf16[1024,512]{1,0:T(8,128)(2,1)}, f32[1024,256]{1,0:T(8,128)S(1)}) custom-call(s32[4]{0:T(128)S(1)} %add_subtract_fusion.refs_0_, bf16[1024,512]{1,0:T(8,128)(2,1)S(1)} %bitcast.32, bf16[1024,256]{1,0:T(8,128)(2,1)S(1)} %bitcast.30, ...), custom_call_target="tpu_custom_call", output_to_operand_aliasing={{0}: (4, {}), {1}: (5, {})} | custom-call | flops 1610612736 | bytes 6291456 | tf_op jit(solution)/shard_map/pallas_call | solution.py:170
  58.7 0.1 add.73
  58.9 12.2 %collective-permute-done.1 = bf16[768,256]{1,0:T(8,128)(2,1)S(1)} collective-permute-done((bf16[768,256]{1,0:T(8,128)(2,1)S(1)}, bf16[768,256]{1,0:T(8,128)(2,1)S(1)}, u32[]{:S(2)}, u32[]{:S(2)}) %collective-permute-start.1) | collective-permute-done | bytes 393248 | tf_op jit(solution)/shard_map/ppermute | solution.py:19
  71.0 0.1 pad_convert_fusion
  71.1 0.9 %fusion = (bf16[1024,128]{1,0:T(8,128)(2,1)}, bf16[1024,128]{1,0:T(8,128)(2,1)}) fusion(f32[1024,256]{1,0:T(8,128)S(1)} %pad_convert_fusion, f32[1024,256]{1,0:T(8,128)S(1)} %add.73), kind=kLoop, calls=%fused_computation.3 | loop fusion | flops 655360 | bytes 2621440 | tf_op jit(solution)/shard_map/convert_element_type | solution.py:239
  (6 shorter events, 0.1 us)
Async XLA Ops:
  0.6 1.0 %copy-start = (bf16[128,1024]{1,0:T(8,128)(2,1)S(1)}, bf16[128,1024]{1,0:T(8,128)(2,1)}, u32[]{:S(2)}) copy-start(bf16[128,1024]{1,0:T(8,128)(2,1)} %param.6) | copy-start | bytes 786436
  2.7 5.3 %copy-start.2 = (bf16[128,4096]{1,0:T(8,128)(2,1)S(1)}, bf16[128,4096]{1,0:T(8,128)(2,1)}, u32[]{:S(2)}) copy-start(bf16[128,4096]{1,0:T(8,128)(2,1)} %param.5) | copy-start | bytes 3145732
  3.5 14.8 %all-to-all-start.1 = ((bf16[128,8,256]{2,0,1:T(8,128)(2,1)}), bf16[128,8,256]{2,0,1:T(8,128)(2,1)S(1)}, u32[]{:S(2)}, u32[]{:S(2)}) async-start(bf16[128,8,256]{2,0,1:T(8,128)(2,1)} %pad_maximum_fusion), calls=%async_computation.1 | async-start | bytes 1048576 | tf_op jit(solution)/shard_map/all_to_all | solution.py:203
  18.3 19.8 %all-to-all-start = ((bf16[128,8,512]{2,0,1:T(8,128)(2,1)}), bf16[128,8,512]{2,0,1:T(8,128)(2,1)S(1)}, u32[]{:S(2)}, u32[]{:S(2)}) async-start(bf16[128,8,512]{2,0,1:T(8,128)(2,1)} %bitcast.27), calls=%async_computation | async-start | bytes 2097152 | tf_op jit(solution)/shard_map/all_to_all | solution.py:207
  22.1 0.7 copy-start.3
  23.9 14.2 %collective-permute-start = (bf16[768,256]{1,0:T(8,128)(2,1)}, bf16[768,256]{1,0:T(8,128)(2,1)S(1)}, u32[]{:S(2)}, u32[]{:S(2)}) collective-permute-start(bf16[768,256]{1,0:T(8,128)(2,1)} %bitcast.11), channel_id=1, source_target_pairs={{0,8},{8,16},{16,24},{24,32},{32,40},{40,48},{48,56},{56,64},{64,7... | collective-permute-start | bytes 1179656 | tf_op jit(solution)/shard_map/ppermute | solution.py:19
  29.0 9.2 %copy-start.1 = (bf16[1024,512]{1,0:T(8,128)(2,1)S(1)}, bf16[1024,512]{1,0:T(8,128)(2,1)}, u32[]{:S(2)}) copy-start(bf16[1024,512]{1,0:T(8,128)(2,1)} %refs_3_.1) | copy-start | bytes 3145732
  47.6 23.4 %collective-permute-start.1 = (bf16[768,256]{1,0:T(8,128)(2,1)S(1)}, bf16[768,256]{1,0:T(8,128)(2,1)S(1)}, u32[]{:S(2)}, u32[]{:S(2)}) collective-permute-start(bf16[768,256]{1,0:T(8,128)(2,1)S(1)} %pad_maximum_fusion.1), channel_id=1, source_target_pairs={{8,0},{16,8},{24,16},{32,24},{40,32},{48,40},{56,48},{64,56},{72,6... | collective-permute-start | bytes 1179656 | tf_op jit(solution)/shard_map/ppermute | solution.py:19

commit v8 on v5

--- a/solution.py
+++ b/solution.py
@@ -6,8 +6,6 @@
 from jax.experimental import pallas as pl
 from jax.experimental.pallas import tpu as pltpu
 
-QUERY_HEADS = 32
-KEY_VALUE_HEADS = 8
 HEAD_SIZE = 128
 BLOCK = 256
 INTERPRET = False
@@ -60,73 +58,77 @@
         return (ref[pl.ds(start, BLOCK), col0:col0 + HEAD_SIZE],
                 ref[pl.ds(start, BLOCK), col0 + HEAD_SIZE:col0 + 2 * HEAD_SIZE])
 
-    if True:
-        u = first_unit + step
-        qs = jnp.concatenate(
-            [q_ref[:, h * HEAD_SIZE:(h + 1) * HEAD_SIZE] for h in range(heads)], axis=0)
-        dos = jnp.concatenate(
-            [grad_ref[:, h * HEAD_SIZE:(h + 1) * HEAD_SIZE] for h in range(heads)], axis=0)
-        lo = lo_ref[u]
-        diag = units + u
-        first_own = jnp.maximum(lo, units)
-        segments = ((kv_ref, 0, own_ref, first_own, diag, units),)
-        if with_prior:
-            segments = ((earlier_ref, 0, prior_ref, lo, units, 1),) + segments
-
-        def pass1(b, carry, ref, col0, off):
-            m, l = carry
-            k, _ = load_kv(ref, col0, b - off)
-            s = _nt(qs, k) * scale
-            s_scr[b - (u + 1)] = s
-            m_new = jnp.maximum(m, jnp.max(s, axis=1, keepdims=True))
-            l = l * jnp.exp(m - m_new) + jnp.sum(jnp.exp(s - m_new), axis=1, keepdims=True)
-            return m_new, l
-
-        carry = (jnp.full((rows, 1), -jnp.inf, jnp.float32), jnp.zeros((rows, 1), jnp.float32))
-        for ref, col0, _, start, stop, off in segments:
-            carry = lax.fori_loop(start, stop, functools.partial(pass1, ref=ref, col0=col0, off=off), carry)
-        m, l = carry
-        k_d, v_d = load_kv(kv_ref, 0, u)
-        s = jnp.where(causal, _nt(qs, k_d) * scale, -jnp.inf)
-        m_new = jnp.maximum(m, jnp.max(s, axis=1, keepdims=True))
-        l = l * jnp.exp(m - m_new) + jnp.sum(jnp.exp(s - m_new), axis=1, keepdims=True)
-        lse = m_new + jnp.log(l)
-
-        def pass2(b, _, ref, col0, off):
-            _, v = load_kv(ref, col0, b - off)
-            p = jnp.exp(s_scr[b - (u + 1)] - lse)
-            s_scr[b - (u + 1)] = p
-            att_scr[...] += _nn(p.astype(jnp.bfloat16), v)
-            return 0
-
-        p = jnp.exp(s - lse)
-        att_scr[...] = _nn(p.astype(jnp.bfloat16), v_d)
-        for ref, col0, _, start, stop, off in segments:
-            lax.fori_loop(start, stop, functools.partial(pass2, ref=ref, col0=col0, off=off), 0)
-        att = att_scr[...].astype(jnp.bfloat16)
-        delta = jnp.sum(dos.astype(jnp.float32) * att.astype(jnp.float32), axis=1, keepdims=True)
-
-        def pass3(b, _, ref, col0, gref, off):
-            k, v = load_kv(ref, col0, b - off)
-            p = s_scr[b - (u + 1)]
-            ds = (p * (_nt(dos, v) - delta)).astype(jnp.bfloat16)
-            dq_scr[...] += _nn(ds, k)
-            start = pl.multiple_of((b - off) * BLOCK, BLOCK)
-            gref[pl.ds(start, BLOCK), 0:HEAD_SIZE] += _tn(ds, qs)
-            gref[pl.ds(start, BLOCK), HEAD_SIZE:2 * HEAD_SIZE] += _tn(p.astype(jnp.bfloat16), dos)
-            return 0
-
-        ds = (p * (_nt(dos, v_d) - delta)).astype(jnp.bfloat16)
-        dq_scr[...] = _nn(ds, k_d)
-        r0 = pl.multiple_of(u * BLOCK, BLOCK)
-        own_ref[pl.ds(r0, BLOCK), 0:HEAD_SIZE] += _tn(ds, qs)
-        own_ref[pl.ds(r0, BLOCK), HEAD_SIZE:2 * HEAD_SIZE] += _tn(p.astype(jnp.bfloat16), dos)
-        for ref, col0, gref, start, stop, off in segments:
-            lax.fori_loop(start, stop, functools.partial(pass3, ref=ref, col0=col0, gref=gref, off=off), 0)
-        dq = (dq_scr[...] * scale).astype(jnp.bfloat16)
-        for h in range(heads):
-            att_ref[:, h * HEAD_SIZE:(h + 1) * HEAD_SIZE] = att[h * BLOCK:(h + 1) * BLOCK]
-            dq_ref[:, h * HEAD_SIZE:(h + 1) * HEAD_SIZE] = dq[h * BLOCK:(h + 1) * BLOCK]
+    u = first_unit + step
+    qs = jnp.concatenate(
+        [q_ref[:, h * HEAD_SIZE:(h + 1) * HEAD_SIZE] for h in range(heads)], axis=0)
+    dos = jnp.concatenate(
+        [grad_ref[:, h * HEAD_SIZE:(h + 1) * HEAD_SIZE] for h in range(heads)], axis=0)
+    lo = lo_ref[u]
+    diag = units + u
+    first_own = jnp.maximum(lo, units)
+    segments = ((kv_ref, 0, own_ref, first_own, diag, units),)
+    if with_prior:
+        segments = ((earlier_ref, 0, prior_ref, lo, units, 1),) + segments
+
+    half = BLOCK // 2
+
+    def pass1(b, m, ref, col0, off):
+        k, _ = load_kv(ref, col0, b - off)
+        s = _nt(qs, k) * scale
+        s_scr[b - (u + 1)] = s
+        return jnp.maximum(m, jnp.maximum(s[:, :half], s[:, half:]))
+
+    k_d, v_d = load_kv(kv_ref, 0, u)
+    s = jnp.where(causal, _nt(qs, k_d) * scale, -jnp.inf)
+    m = jnp.maximum(s[:, :half], s[:, half:])
+    for ref, col0, _, start, stop, off in segments:
+        m = lax.fori_loop(start, stop, functools.partial(pass1, ref=ref, col0=col0, off=off), m)
+    m = jnp.max(m, axis=1, keepdims=True)
+
+    def pass1b(b, l):
+        e = jnp.exp(s_scr[b - (u + 1)] - m)
+        s_scr[b - (u + 1)] = e
+        return l + e[:, :half] + e[:, half:]
+
+    e = jnp.exp(s - m)
+    l = lax.fori_loop(lo, diag, pass1b, e[:, :half] + e[:, half:])
+    inv_total = 1.0 / jnp.sum(l, axis=1, keepdims=True)
+
+    def pass2(b, _, ref, col0, off):
+        _, v = load_kv(ref, col0, b - off)
+        p = s_scr[b - (u + 1)] * inv_total
+        s_scr[b - (u + 1)] = p
+        att_scr[...] += _nn(p.astype(jnp.bfloat16), v)
+        return 0
+
+    p = e * inv_total
+    att_scr[...] = _nn(p.astype(jnp.bfloat16), v_d)
+    for ref, col0, _, start, stop, off in segments:
+        lax.fori_loop(start, stop, functools.partial(pass2, ref=ref, col0=col0, off=off), 0)
+    att = att_scr[...].astype(jnp.bfloat16)
+    delta = jnp.sum(dos.astype(jnp.float32) * att.astype(jnp.float32), axis=1, keepdims=True)
+
+    def pass3(b, _, ref, col0, gref, off):
+        k, v = load_kv(ref, col0, b - off)
+        p = s_scr[b - (u + 1)]
+        ds = (p * (_nt(dos, v) - delta)).astype(jnp.bfloat16)
+        dq_scr[...] += _nn(ds, k)
+        start = pl.multiple_of((b - off) * BLOCK, BLOCK)
+        gref[pl.ds(start, BLOCK), 0:HEAD_SIZE] += _tn(ds, qs)
+        gref[pl.ds(start, BLOCK), HEAD_SIZE:2 * HEAD_SIZE] += _tn(p.astype(jnp.bfloat16), dos)
+        return 0
+
+    ds = (p * (_nt(dos, v_d) - delta)).astype(jnp.bfloat16)
+    dq_scr[...] = _nn(ds, k_d)
+    r0 = pl.multiple_of(u * BLOCK, BLOCK)
+    own_ref[pl.ds(r0, BLOCK), 0:HEAD_SIZE] += _tn(ds, qs)
+    own_ref[pl.ds(r0, BLOCK), HEAD_SIZE:2 * HEAD_SIZE] += _tn(p.astype(jnp.bfloat16), dos)
+    for ref, col0, gref, start, stop, off in segments:
+        lax.fori_loop(start, stop, functools.partial(pass3, ref=ref, col0=col0, gref=gref, off=off), 0)
+    dq = (dq_scr[...] * scale).astype(jnp.bfloat16)
+    for h in range(heads):
+        att_ref[:, h * HEAD_SIZE:(h + 1) * HEAD_SIZE] = att[h * BLOCK:(h + 1) * BLOCK]
+        dq_ref[:, h * HEAD_SIZE:(h + 1) * HEAD_SIZE] = dq[h * BLOCK:(h + 1) * BLOCK]
 
 
 def attention_call(lo, packed, kv, earlier, grad, unit_list, out_alias=None, *, heads, interpret=False):
@@ -182,7 +184,7 @@
     )(*operands)
 
 
-def local(query_matrix, key_matrix, value_matrix, output_gradient, doc_start):
+def local_body(query_matrix, key_matrix, value_matrix, output_gradient, doc_start):
     token_per_shard = query_matrix.shape[0]
     head_groups = lax.axis_size("head")
     q_cols = query_matrix.shape[1] // head_groups
@@ -215,21 +217,29 @@
     same = (joined_units[window] == own_units[:, None]).astype(jnp.int32)
     lo = (unit_ids + units + 1 - jnp.sum(same, axis=1)).astype(jnp.int32)
     heads = q_cols // HEAD_SIZE
-    first = attention_call(lo, packed, kv, earlier_kv, output_gradient, range(units - 1),
-                           heads=heads, interpret=INTERPRET)
-    attended_all, query_total, prior_grads, own_first = first
-    last = attention_call(lo, packed, kv, None, output_gradient, [units - 1],
-                          (attended_all, query_total), heads=heads, interpret=INTERPRET)
-    attended_all, query_total, own_last = last
-    own_grads = own_first + own_last
+    call = functools.partial(attention_call, heads=heads, interpret=INTERPRET)
     score_scale = HEAD_SIZE ** (-0.5)
-    prior_grads = jnp.concatenate(
-        [(prior_grads[:, :k_cols] * score_scale).astype(jnp.bfloat16),
-         prior_grads[:, k_cols:].astype(jnp.bfloat16)],
-        axis=1,
-    )
-    later = from_behind(prior_grads, "ctx", -1).astype(jnp.float32)
-    later = jnp.concatenate([jnp.zeros((BLOCK, 2 * k_cols), jnp.float32), later], axis=0)
+
+    def to_link(grads):
+        return jnp.concatenate(
+            [(grads[:, :k_cols] * score_scale).astype(jnp.bfloat16),
+             grads[:, k_cols:].astype(jnp.bfloat16)],
+            axis=1,
+        )
+
+    split = (units - 2) * BLOCK
+    attended_all, query_total, prior_a, own_a = call(
+        lo, packed, kv, earlier_kv, output_gradient, range(units - 2))
+    later_a = from_behind(to_link(prior_a[:split]), "ctx", -1)
+    attended_all, query_total, prior_b, own_b = call(
+        lo, packed, kv, earlier_kv, output_gradient, [units - 2], (attended_all, query_total))
+    later_b = from_behind(to_link(prior_a[split:] + prior_b[split:]), "ctx", -1)
+    attended_all, query_total, own_c = call(
+        lo, packed, kv, None, output_gradient, [units - 1], (attended_all, query_total))
+    own_grads = own_a + own_b + own_c
+    later = jnp.concatenate(
+        [jnp.zeros((BLOCK, 2 * k_cols), jnp.float32), later_a.astype(jnp.float32),
+         later_b.astype(jnp.float32)], axis=0)
     summed_keys = (own_grads[:, :k_cols] * score_scale + later[:, :k_cols]).astype(jnp.bfloat16)
     summed_values = (own_grads[:, k_cols:] + later[:, k_cols:]).astype(jnp.bfloat16)
     return (attended_all, query_total, summed_keys, summed_values)
@@ -244,7 +254,7 @@
         P(),
     )
     return jax.shard_map(
-        local,
+        local_body,
         mesh=mesh,
         in_specs=placed,
         out_specs=(P("ctx", "head"), P("ctx", "head"), P("ctx", "head"), P("ctx", "head")),

time: 73.6 us -> 74.1 us (level)
  waiting for transfers between devices: 34 us -> 23.5 us
  starting transfers between devices: 14.9 us -> 24.8 us
    ppermute x2 -> x3, waiting for transfers between devices: 24.7 us -> 14.3 us  [from_behind(): return lax.ppermute(block, axis, route)]
    ppermute x2 -> x3, starting transfers between devices: 6.86 us -> 16.7 us  [from_behind(): return lax.ppermute(block, axis, route)]
    pallas_call x2 -> x3, Pallas kernels: 15.4 us -> 16.1 us  [attention_call(): pl.pallas_call(kernel, grid=(steps,), out_shape=tuple(out_shape), in_spec...]
  transfers between devices with their start and end apart: 4 -> 5, of which waited for: 3 -> 3; matrix products, arithmetic and copies ran while one was open for 5% -> 5% of each run, Pallas kernels for 7% -> 7%
where the time goes in v8:
time: 74.1 us; the launch traced here: 73.8 us
  starting transfers between devices  24.8 us (33%)
  waiting for transfers between devices  23.5 us (32%)
  Pallas kernels  16.1 us (22%)
  local copies, waits for them, and re-layouts  5.5 us (7%)
  other arithmetic  3.1 us (4%)
  between operations  0.81 us (1%)
    ppermute x3, starting transfers between devices, from_behind(): return lax.ppermute(block, axis, route)  16.7 us
    pallas_call x3, Pallas kernels, attention_call(): pl.pallas_call(kernel, grid=(steps,), out_shape=tuple(out_shape), in_spec...  16.1 us
    ppermute x3, waiting for transfers between devices, from_behind(): return lax.ppermute(block, axis, route)  14.3 us
    all_to_all x1, waiting for transfers between devices, local_body(): lax.all_to_all(kv_packed, 'head', split_axis=1, concat_axis=0, tiled=True)  9.24 us
    all_to_all x1, starting transfers between devices, local_body(): lax.all_to_all(kv_packed, 'head', split_axis=1, concat_axis=0, tiled=True)  4.47 us
    all_to_all x1, starting transfers between devices, local_body(): lax.all_to_all(query_matrix.reshape(token_per_shard, head_groups, q_cols)...  3.56 us
    unnamed x8, local copies, waits for them, and re-layouts  1.62 us
  transfers between devices with their start and end apart: 5, of which 3 were waited for; matrix products, arithmetic and copies ran while one was open for 5% of the time, Pallas kernels for 7%

profile of v8, /device:TPU:102, one launch (start us, length us, event | category | flops | bytes accessed | tf_op | source)
XLA Modules:
  0.0 73.8 jit_solution(2985644605802020175)
XLA Ops:
  0.6 0.0 copy-start
  0.6 0.9 %copy-done = bf16[128,1024]{1,0:T(8,128)(2,1)S(1)} copy-done((bf16[128,1024]{1,0:T(8,128)(2,1)S(1)}, bf16[128,1024]{1,0:T(8,128)(2,1)}, u32[]{:S(2)}) %copy-start) | copy-done | bytes 262168
  1.6 1.1 %copy_bitcast_fusion.1 = (bf16[128,8,128]{2,0,1:T(8,128)(2,1)S(1)}, bf16[128,8,128]{2,0,1:T(8,128)(2,1)S(1)}) fusion(bf16[128,1024]{1,0:T(8,128)(2,1)S(1)} %copy-done, bf16[128,1024]{1,0:T(8,128)(2,1)} %param.7), kind=kLoop, calls=%fused_computation.10 | loop fusion | bytes 1048576 | tf_op jit(solution)/shard_map/reshape | solution.py:196
  2.7 0.0 copy-start.2
  2.7 0.9 %pad_maximum_fusion.1 = bf16[128,8,256]{2,0,1:T(8,128)(2,1)} fusion(bf16[128,8,128]{2,0,1:T(8,128)(2,1)S(1)} %get-tuple-element.30, bf16[128,8,128]{2,0,1:T(8,128)(2,1)S(1)} %get-tuple-element.31), kind=kLoop, calls=%fused_computation.9 | loop fusion | flops 1048576 | bytes 1048576 | tf_op jit(solution)/shard_map/concatenate | solution.py:193
  3.5 4.5 %all-to-all-start.1 = ((bf16[128,8,256]{2,0,1:T(8,128)(2,1)}), bf16[128,8,256]{2,0,1:T(8,128)(2,1)S(1)}, u32[]{:S(2)}, u32[]{:S(2)}) async-start(bf16[128,8,256]{2,0,1:T(8,128)(2,1)} %pad_maximum_fusion.1), calls=%async_computation.1 | async-start | bytes 1048576 | tf_op jit(solution)/shard_map/all_to_all | solution.py:200
  8.0 0.0 copy-done.2
  8.0 1.1 %copy.27 = bf16[16,8,8,512]{3,2,0,1:T(8,128)(2,1)} copy(bf16[16,8,8,512]{3,2,1,0:T(8,128)(2,1)S(1)} %bitcast.35) | data formatting | bytes 2097152 | tf_op jit(solution)/shard_map/reshape | solution.py:205
  9.1 9.2 %all-to-all-done.1 = bf16[128,8,256]{2,0,1:T(8,128)(2,1)S(1)} async-done(((bf16[128,8,256]{2,0,1:T(8,128)(2,1)}), bf16[128,8,256]{2,0,1:T(8,128)(2,1)S(1)}, u32[]{:S(2)}, u32[]{:S(2)}) %all-to-all-start.1) | async-done | bytes 524320 | tf_op jit(solution)/shard_map/all_to_all | solution.py:200
  18.3 3.6 %all-to-all-start = ((bf16[128,8,512]{2,0,1:T(8,128)(2,1)}), bf16[128,8,512]{2,0,1:T(8,128)(2,1)S(1)}, u32[]{:S(2)}, u32[]{:S(2)}) async-start(bf16[128,8,512]{2,0,1:T(8,128)(2,1)} %bitcast.27), calls=%async_computation | async-start | bytes 2097152 | tf_op jit(solution)/shard_map/all_to_all | solution.py:204
  21.9 0.1 compare_select_fusion
  22.0 0.1 reshape.88
  22.1 0.0 copy-start.3
  22.1 0.7 copy-done.3
  22.7 0.1 copy.17
  22.8 0.2 reduce-window.4
  23.0 0.1 select_reduce_fusion
  23.2 0.8 %slice.55 = bf16[6,128,1,256]{3,1,0,2:T(8,128)(2,1)} slice(bf16[8,128,1,256]{3,1,0,2:T(8,128)(2,1)S(1)} %bitcast.28), slice={[2:8], [0:128], [0:1], [0:256]} | slice | bytes 786432 | tf_op jit(solution)/shard_map/slice | solution.py:203
  23.9 4.9 %collective-permute-start = (bf16[768,256]{1,0:T(8,128)(2,1)}, bf16[768,256]{1,0:T(8,128)(2,1)S(1)}, u32[]{:S(2)}, u32[]{:S(2)}) collective-permute-start(bf16[768,256]{1,0:T(8,128)(2,1)} %bitcast.11), channel_id=1, source_target_pairs={{0,8},{8,16},{16,24},{24,32},{32,40},{40,48},{48,56},{56,64},{64,7... | collective-permute-start | bytes 1179656 | tf_op jit(solution)/shard_map/ppermute | solution.py:17
  28.9 0.1 pad_add_fusion
  29.0 0.0 copy-start.1
  29.0 0.7 gather_fusion
  29.6 0.1 reshape.87
  29.7 0.2 convert_reduce_fusion
  29.9 8.2 %collective-permute-done.refs_3_ = bf16[768,256]{1,0:T(8,128)(2,1)S(1)} collective-permute-done((bf16[768,256]{1,0:T(8,128)(2,1)}, bf16[768,256]{1,0:T(8,128)(2,1)S(1)}, u32[]{:S(2)}, u32[]{:S(2)}) %collective-permute-start) | collective-permute-done | bytes 393248 | tf_op jit(solution)/shard_map/ppermute | solution.py:17
  38.1 0.0 all-to-all-done
  38.1 0.0 copy-done.1
  38.1 7.3 %shard_map.84 = (bf16[1024,512]{1,0:T(8,128)(2,1)}, bf16[1024,512]{1,0:T(8,128)(2,1)}, f32[768,256]{1,0:T(8,128)S(1)}, f32[1024,256]{1,0:T(8,128)S(1)}) custom-call(s32[4]{0:T(128)S(1)} %add_subtract_fusion.refs_0_, bf16[1024,512]{1,0:T(8,128)(2,1)S(1)} %bitcast.32, bf16[1024,256]{1,0:T(8,128)(2,1)S(1)} %bitcast.29, ...), custom_call_target="tpu_custom_call" | custom-call | flops 3221225472 | bytes 6291456 | tf_op jit(solution)/shard_map/pallas_call | solution.py:167
  45.5 3.4 %shard_map.85 = (bf16[1024,512]{1,0:T(8,128)(2,1)}, bf16[1024,512]{1,0:T(8,128)(2,1)}, f32[768,256]{1,0:T(8,128)S(1)}, f32[1024,256]{1,0:T(8,128)S(1)}) custom-call(s32[4]{0:T(128)S(1)} %add_subtract_fusion.refs_0_, bf16[1024,512]{1,0:T(8,128)(2,1)S(1)} %bitcast.33, bf16[1024,256]{1,0:T(8,128)(2,1)S(1)} %bitcast.30, ...), custom_call_target="tpu_custom_call", output_to_operand_aliasing={{0}: (5, {}), {1}: (6, {})} | custom-call | flops 1610612736 | bytes 6291456 | tf_op jit(solution)/shard_map/pallas_call | solution.py:167
  49.1 5.9 %collective-permute-start.1 = (bf16[512,256]{1,0:T(8,128)(2,1)S(1)}, bf16[512,256]{1,0:T(8,128)(2,1)S(1)}, u32[]{:S(2)}, u32[]{:S(2)}) collective-permute-start(bf16[512,256]{1,0:T(8,128)(2,1)S(1)} %pad_maximum_fusion.2), channel_id=1, source_target_pairs={{8,0},{16,8},{24,16},{32,24},{40,32},{48,40},{56,48},{64,56},{72,6... | collective-permute-start | bytes 786440 | tf_op jit(solution)/shard_map/ppermute | solution.py:17
  55.0 5.9 %collective-permute-start.2 = (bf16[256,256]{1,0:T(8,128)(2,1)S(1)}, bf16[256,256]{1,0:T(8,128)(2,1)S(1)}, u32[]{:S(2)}, u32[]{:S(2)}) collective-permute-start(bf16[256,256]{1,0:T(8,128)(2,1)S(1)} %pad_maximum_fusion.3), channel_id=1, source_target_pairs={{8,0},{16,8},{24,16},{32,24},{40,32},{48,40},{56,48},{64,56},{72,6... | collective-permute-start | bytes 393224 | tf_op jit(solution)/shard_map/ppermute | solution.py:17
  60.9 5.3 %shard_map.86 = (bf16[1024,512]{1,0:T(8,128)(2,1)}, bf16[1024,512]{1,0:T(8,128)(2,1)}, f32[1024,256]{1,0:T(8,128)S(1)}) custom-call(s32[4]{0:T(128)S(1)} %add_subtract_fusion.refs_0_, bf16[1024,512]{1,0:T(8,128)(2,1)S(1)} %bitcast.34, bf16[1024,256]{1,0:T(8,128)(2,1)S(1)} %bitcast.31, ...), custom_call_target="tpu_custom_call", output_to_operand_aliasing={{0}: (4, {}), {1}: (5, {})} | custom-call | flops 1610612736 | bytes 6291456 | tf_op jit(solution)/shard_map/pallas_call | solution.py:167
  66.2 0.2 add_add_fusion
  66.4 6.1 %collective-permute-done.2 = bf16[256,256]{1,0:T(8,128)(2,1)S(1)} collective-permute-done((bf16[256,256]{1,0:T(8,128)(2,1)S(1)}, bf16[256,256]{1,0:T(8,128)(2,1)S(1)}, u32[]{:S(2)}, u32[]{:S(2)}) %collective-permute-start.2) | collective-permute-done | bytes 131104 | tf_op jit(solution)/shard_map/ppermute | solution.py:17
  72.5 0.0 collective-permute-done.1
  72.6 0.2 pad_maximum_fusion
  72.8 1.0 %fusion = (bf16[1024,128]{1,0:T(8,128)(2,1)}, bf16[1024,128]{1,0:T(8,128)(2,1)}) fusion(f32[1024,256]{1,0:T(8,128)S(1)} %pad_maximum_fusion, f32[1024,256]{1,0:T(8,128)S(1)} %add_add_fusion), kind=kLoop, calls=%fused_computation.5 | loop fusion | flops 655360 | bytes 2621440 | tf_op jit(solution)/shard_map/convert_element_type | solution.py:244
  (14 shorter events, 0.2 us)
Async XLA Ops:
  0.6 1.0 %copy-start = (bf16[128,1024]{1,0:T(8,128)(2,1)S(1)}, bf16[128,1024]{1,0:T(8,128)(2,1)}, u32[]{:S(2)}) copy-start(bf16[128,1024]{1,0:T(8,128)(2,1)} %param.6) | copy-start | bytes 786436
  2.7 5.3 %copy-start.2 = (bf16[128,4096]{1,0:T(8,128)(2,1)S(1)}, bf16[128,4096]{1,0:T(8,128)(2,1)}, u32[]{:S(2)}) copy-start(bf16[128,4096]{1,0:T(8,128)(2,1)} %param.5) | copy-start | bytes 3145732
  3.5 14.8 %all-to-all-start.1 = ((bf16[128,8,256]{2,0,1:T(8,128)(2,1)}), bf16[128,8,256]{2,0,1:T(8,128)(2,1)S(1)}, u32[]{:S(2)}, u32[]{:S(2)}) async-start(bf16[128,8,256]{2,0,1:T(8,128)(2,1)} %pad_maximum_fusion.1), calls=%async_computation.1 | async-start | bytes 1048576 | tf_op jit(solution)/shard_map/all_to_all | solution.py:200
  18.3 19.8 %all-to-all-start = ((bf16[128,8,512]{2,0,1:T(8,128)(2,1)}), bf16[128,8,512]{2,0,1:T(8,128)(2,1)S(1)}, u32[]{:S(2)}, u32[]{:S(2)}) async-start(bf16[128,8,512]{2,0,1:T(8,128)(2,1)} %bitcast.27), calls=%async_computation | async-start | bytes 2097152 | tf_op jit(solution)/shard_map/all_to_all | solution.py:204
  22.1 0.7 copy-start.3
  23.9 14.2 %collective-permute-start = (bf16[768,256]{1,0:T(8,128)(2,1)}, bf16[768,256]{1,0:T(8,128)(2,1)S(1)}, u32[]{:S(2)}, u32[]{:S(2)}) collective-permute-start(bf16[768,256]{1,0:T(8,128)(2,1)} %bitcast.11), channel_id=1, source_target_pairs={{0,8},{8,16},{16,24},{24,32},{32,40},{40,48},{48,56},{56,64},{64,7... | collective-permute-start | bytes 1179656 | tf_op jit(solution)/shard_map/ppermute | solution.py:17
  29.0 9.2 %copy-start.1 = (bf16[1024,512]{1,0:T(8,128)(2,1)S(1)}, bf16[1024,512]{1,0:T(8,128)(2,1)}, u32[]{:S(2)}) copy-start(bf16[1024,512]{1,0:T(8,128)(2,1)} %refs_3_.1) | copy-start | bytes 3145732
  49.1 23.5 %collective-permute-start.1 = (bf16[512,256]{1,0:T(8,128)(2,1)S(1)}, bf16[512,256]{1,0:T(8,128)(2,1)S(1)}, u32[]{:S(2)}, u32[]{:S(2)}) collective-permute-start(bf16[512,256]{1,0:T(8,128)(2,1)S(1)} %pad_maximum_fusion.2), channel_id=1, source_target_pairs={{8,0},{16,8},{24,16},{32,24},{40,32},{48,40},{56,48},{64,56},{72,6... | collective-permute-start | bytes 786440 | tf_op jit(solution)/shard_map/ppermute | solution.py:17
  55.0 17.5 %collective-permute-start.2 = (bf16[256,256]{1,0:T(8,128)(2,1)S(1)}, bf16[256,256]{1,0:T(8,128)(2,1)S(1)}, u32[]{:S(2)}, u32[]{:S(2)}) collective-permute-start(bf16[256,256]{1,0:T(8,128)(2,1)S(1)} %pad_maximum_fusion.3), channel_id=1, source_target_pairs={{8,0},{16,8},{24,16},{32,24},{40,32},{48,40},{56,48},{64,56},{72,6... | collective-permute-start | bytes 393224 | tf_op jit(solution)/shard_map/ppermute | solution.py:17

commit v9 on v7

--- a/solution.py
+++ b/solution.py
@@ -31,7 +31,7 @@
     return lax.dot_general(a, b, (((1,), (0,)), ((), ())), preferred_element_type=jnp.float32)
 
 
-def attention_kernel(*refs, first_unit, units, heads, with_prior, aliased):
+def attention_kernel(*refs, first_unit, units, heads, with_prior, aliased, steps):
     refs = list(refs)
     lo_ref, q_ref, kv_ref = refs[:3]
     refs = refs[3:]
@@ -40,8 +40,9 @@
     refs = refs[aliased:]
     att_ref, dq_ref = refs[:2]
     refs = refs[2:]
-    prior_ref = refs.pop(0) if with_prior else None
-    own_ref, s_scr, att_scr, dq_scr = refs
+    prior_out = refs.pop(0) if with_prior else None
+    own_ref, s_scr, att_scr, dq_scr = refs[:4]
+    prior_ref = refs[4] if with_prior else None
     scale = HEAD_SIZE ** (-0.5)
     step = pl.program_id(0)
 
@@ -133,6 +134,12 @@
             att_ref[:, h * HEAD_SIZE:(h + 1) * HEAD_SIZE] = att[h * BLOCK:(h + 1) * BLOCK]
             dq_ref[:, h * HEAD_SIZE:(h + 1) * HEAD_SIZE] = dq[h * BLOCK:(h + 1) * BLOCK]
 
+    if with_prior:
+        @pl.when(step == steps - 1)
+        def _():
+            prior_out[:, 0:HEAD_SIZE] = (prior_ref[:, 0:HEAD_SIZE] * scale).astype(prior_out.dtype)
+            prior_out[:, HEAD_SIZE:] = prior_ref[:, HEAD_SIZE:].astype(prior_out.dtype)
+
 
 def attention_call(lo, packed, kv, earlier, grad, unit_list, out_alias=None, *, heads, interpret=False):
     ctx_rows = packed.shape[0]
@@ -144,7 +151,7 @@
     first_unit = unit_list[0]
     steps = len(unit_list)
     kernel = functools.partial(attention_kernel, first_unit=first_unit, units=units, heads=heads,
-                               with_prior=with_prior, aliased=aliased)
+                               with_prior=with_prior, aliased=aliased, steps=steps)
     rows = heads * BLOCK
 
     def whole(x):
@@ -160,7 +167,7 @@
     out_shape = [jax.ShapeDtypeStruct((ctx_rows, q_cols), jnp.bfloat16)] * 2
     out_specs = [unit_block] * 2
     if with_prior:
-        out_shape.append(jax.ShapeDtypeStruct(earlier.shape, jnp.float32))
+        out_shape.append(jax.ShapeDtypeStruct(earlier.shape, jnp.bfloat16))
         out_specs.append(pl.BlockSpec(earlier.shape, lambda i: (0, 0)))
     out_shape.append(jax.ShapeDtypeStruct((ctx_rows, kv_cols), jnp.float32))
     out_specs.append(pl.BlockSpec((ctx_rows, kv_cols), lambda i: (0, 0)))
@@ -177,7 +184,7 @@
             pltpu.VMEM((units, rows, BLOCK), jnp.float32),
             pltpu.VMEM((rows, HEAD_SIZE), jnp.float32),
             pltpu.VMEM((rows, HEAD_SIZE), jnp.float32),
-        ],
+        ] + ([pltpu.VMEM(earlier.shape, jnp.float32)] if with_prior else []),
         input_output_aliases=aliases,
         compiler_params=pltpu.CompilerParams(
             dimension_semantics=("arbitrary",), vmem_limit_bytes=48 * 1024 * 1024),
@@ -210,11 +217,11 @@
     ).reshape(ctx_rows, q_cols)
     units = ctx_rows // BLOCK
     ctx_index = lax.axis_index("ctx")
-    unit_doc = jnp.cumsum(doc_start)
-    own_units = lax.dynamic_slice_in_dim(unit_doc, ctx_index * units, units)
-    prior_units = lax.dynamic_slice_in_dim(unit_doc, jnp.maximum(ctx_index - 1, 0) * units, units)
-    prior_units = jnp.where(ctx_index > 0, prior_units, -1)
-    joined_units = jnp.concatenate([prior_units, own_units])
+    wanted = (ctx_index - 1) * units + jnp.arange(2 * units, dtype=jnp.int32)
+    unit_at = jnp.arange(doc_start.shape[0], dtype=jnp.int32)
+    joined_units = jnp.sum(jnp.where(unit_at[None, :] <= wanted[:, None], doc_start[None, :], 0), axis=1)
+    joined_units = jnp.where(wanted >= 0, joined_units, -1)
+    own_units = joined_units[units:]
     unit_ids = jnp.arange(units, dtype=jnp.int32)
     window = unit_ids[:, None] + 1 + unit_ids[None, :]
     same = (joined_units[window] == own_units[:, None]).astype(jnp.int32)
@@ -228,11 +235,6 @@
     attended_all, query_total, own_last = last
     own_grads = own_first + own_last
     score_scale = HEAD_SIZE ** (-0.5)
-    prior_grads = jnp.concatenate(
-        [(prior_grads[:, :k_cols] * score_scale).astype(jnp.bfloat16),
-         prior_grads[:, k_cols:].astype(jnp.bfloat16)],
-        axis=1,
-    )
     later = from_behind(prior_grads, "ctx", -1).astype(jnp.float32)
     later = jnp.concatenate([jnp.zeros((BLOCK, 2 * k_cols), jnp.float32), later], axis=0)
     summed_keys = (own_grads[:, :k_cols] * score_scale + later[:, :k_cols]).astype(jnp.bfloat16)

time: 72.4 us -> 72.1 us (level)
  no operation moved by 1% of the time
where the time goes in v9:
time: 72.1 us; the launch traced here: 71.7 us
  waiting for transfers between devices  29.4 us (41%)
  starting transfers between devices  19.1 us (26%)
  Pallas kernels  14.7 us (20%)
  local copies, waits for them, and re-layouts  5.42 us (8%)
  other arithmetic  2.43 us (3%)
    ppermute x2, waiting for transfers between devices, from_behind(): return lax.ppermute(block, axis, route)  20.2 us
    pallas_call x2, Pallas kernels, attention_call(): pl.pallas_call(kernel, grid=(steps,), out_shape=tuple(out_shape), in_spec...  14.7 us
    ppermute x2, starting transfers between devices, from_behind(): return lax.ppermute(block, axis, route)  11 us
    all_to_all x1, waiting for transfers between devices, local(): lax.all_to_all(kv_packed, 'head', split_axis=1, concat_axis=0, tiled=True)  9.24 us
    all_to_all x1, starting transfers between devices, local(): lax.all_to_all(kv_packed, 'head', split_axis=1, concat_axis=0, tiled=True)  4.47 us
    all_to_all x1, starting transfers between devices, local(): lax.all_to_all(query_matrix.reshape(token_per_shard, head_groups, q_cols)...  3.56 us
    unnamed x8, local copies, waits for them, and re-layouts  1.61 us
  transfers between devices with their start and end apart: 4, of which 3 were waited for; matrix products, arithmetic and copies ran while one was open for 5% of the time, Pallas kernels for 7%

profile of v9, /device:TPU:102, one launch (start us, length us, event | category | flops | bytes accessed | tf_op | source)
XLA Modules:
  0.0 71.7 jit_solution(10015613115540578593)
XLA Ops:
  0.6 0.0 copy-start
  0.6 0.9 %copy-done = bf16[128,1024]{1,0:T(8,128)(2,1)S(1)} copy-done((bf16[128,1024]{1,0:T(8,128)(2,1)S(1)}, bf16[128,1024]{1,0:T(8,128)(2,1)}, u32[]{:S(2)}) %copy-start) | copy-done | bytes 262168
  1.6 1.1 %copy_bitcast_fusion.1 = (bf16[128,8,128]{2,0,1:T(8,128)(2,1)S(1)}, bf16[128,8,128]{2,0,1:T(8,128)(2,1)S(1)}) fusion(bf16[128,1024]{1,0:T(8,128)(2,1)S(1)} %copy-done, bf16[128,1024]{1,0:T(8,128)(2,1)} %param.7), kind=kLoop, calls=%fused_computation.9 | loop fusion | bytes 1048576 | tf_op jit(solution)/shard_map/reshape | solution.py:206
  2.7 0.0 copy-start.2
  2.7 0.9 %pad_maximum_fusion = bf16[128,8,256]{2,0,1:T(8,128)(2,1)} fusion(bf16[128,8,128]{2,0,1:T(8,128)(2,1)S(1)} %get-tuple-element.20, bf16[128,8,128]{2,0,1:T(8,128)(2,1)S(1)} %get-tuple-element.21), kind=kLoop, calls=%fused_computation.7 | loop fusion | flops 1048576 | bytes 1048576 | tf_op jit(solution)/shard_map/concatenate | solution.py:203
  3.5 4.5 %all-to-all-start.1 = ((bf16[128,8,256]{2,0,1:T(8,128)(2,1)}), bf16[128,8,256]{2,0,1:T(8,128)(2,1)S(1)}, u32[]{:S(2)}, u32[]{:S(2)}) async-start(bf16[128,8,256]{2,0,1:T(8,128)(2,1)} %pad_maximum_fusion), calls=%async_computation.1 | async-start | bytes 1048576 | tf_op jit(solution)/shard_map/all_to_all | solution.py:210
  8.0 0.0 copy-done.2
  8.0 1.1 %copy.26 = bf16[16,8,8,512]{3,2,0,1:T(8,128)(2,1)} copy(bf16[16,8,8,512]{3,2,1,0:T(8,128)(2,1)S(1)} %bitcast.32) | data formatting | bytes 2097152 | tf_op jit(solution)/shard_map/reshape | solution.py:215
  9.1 9.2 %all-to-all-done.1 = bf16[128,8,256]{2,0,1:T(8,128)(2,1)S(1)} async-done(((bf16[128,8,256]{2,0,1:T(8,128)(2,1)}), bf16[128,8,256]{2,0,1:T(8,128)(2,1)S(1)}, u32[]{:S(2)}, u32[]{:S(2)}) %all-to-all-start.1) | async-done | bytes 524320 | tf_op jit(solution)/shard_map/all_to_all | solution.py:210
  18.3 3.6 %all-to-all-start = ((bf16[128,8,512]{2,0,1:T(8,128)(2,1)}), bf16[128,8,512]{2,0,1:T(8,128)(2,1)S(1)}, u32[]{:S(2)}, u32[]{:S(2)}) async-start(bf16[128,8,512]{2,0,1:T(8,128)(2,1)} %bitcast.26), calls=%async_computation | async-start | bytes 2097152 | tf_op jit(solution)/shard_map/all_to_all | solution.py:214
  21.9 0.1 compare_select_fusion
  22.0 0.1 reshape.83
  22.0 0.0 copy-start.3
  22.1 0.7 copy-done.3
  22.7 0.2 select_reduce_fusion
  22.9 0.8 %slice.30 = bf16[6,128,1,256]{3,1,0,2:T(8,128)(2,1)} slice(bf16[8,128,1,256]{3,1,0,2:T(8,128)(2,1)S(1)} %bitcast.27), slice={[2:8], [0:128], [0:1], [0:256]} | slice | bytes 786432 | tf_op jit(solution)/shard_map/slice | solution.py:213
  23.7 4.9 %collective-permute-start = (bf16[768,256]{1,0:T(8,128)(2,1)}, bf16[768,256]{1,0:T(8,128)(2,1)S(1)}, u32[]{:S(2)}, u32[]{:S(2)}) collective-permute-start(bf16[768,256]{1,0:T(8,128)(2,1)} %bitcast.10), channel_id=1, source_target_pairs={{0,8},{8,16},{16,24},{24,32},{32,40},{40,48},{48,56},{56,64},{64,7... | collective-permute-start | bytes 1179656 | tf_op jit(solution)/shard_map/ppermute | solution.py:19
  28.6 0.1 slice.21
  28.7 0.0 copy-start.1
  28.7 0.7 gather_fusion
  29.4 0.1 reshape.82
  29.4 0.2 convert_reduce_fusion
  29.6 8.2 %collective-permute-done.refs_3_ = bf16[768,256]{1,0:T(8,128)(2,1)S(1)} collective-permute-done((bf16[768,256]{1,0:T(8,128)(2,1)}, bf16[768,256]{1,0:T(8,128)(2,1)S(1)}, u32[]{:S(2)}, u32[]{:S(2)}) %collective-permute-start) | collective-permute-done | bytes 393248 | tf_op jit(solution)/shard_map/ppermute | solution.py:19
  37.9 0.0 all-to-all-done
  37.9 0.0 copy-done.1
  37.9 9.5 %shard_map.84 = (bf16[1024,512]{1,0:T(8,128)(2,1)}, bf16[1024,512]{1,0:T(8,128)(2,1)}, bf16[768,256]{1,0:T(8,128)(2,1)S(1)}, f32[1024,256]{1,0:T(8,128)S(1)}) custom-call(s32[4]{0:T(128)S(1)} %add_subtract_fusion.refs_0_, bf16[1024,512]{1,0:T(8,128)(2,1)S(1)} %bitcast.30, bf16[1024,256]{1,0:T(8,128)(2,1)S(1)} %bitcast.28, ...), custom_call_target="tpu_custom_call" | custom-call | flops 4831838208 | bytes 6291456 | tf_op jit(solution)/shard_map/pallas_call | solution.py:177
  47.3 6.1 %collective-permute-start.1 = (bf16[768,256]{1,0:T(8,128)(2,1)S(1)}, bf16[768,256]{1,0:T(8,128)(2,1)S(1)}, u32[]{:S(2)}, u32[]{:S(2)}) collective-permute-start(bf16[768,256]{1,0:T(8,128)(2,1)S(1)} %get-tuple-element.17), channel_id=1, source_target_pairs={{8,0},{16,8},{24,16},{32,24},{40,32},{48,40},{56,48},{64,56},{72,6... | collective-permute-start | bytes 1179656 | tf_op jit(solution)/shard_map/ppermute | solution.py:19
  53.4 5.2 %shard_map.85 = (bf16[1024,512]{1,0:T(8,128)(2,1)}, bf16[1024,512]{1,0:T(8,128)(2,1)}, f32[1024,256]{1,0:T(8,128)S(1)}) custom-call(s32[4]{0:T(128)S(1)} %add_subtract_fusion.refs_0_, bf16[1024,512]{1,0:T(8,128)(2,1)S(1)} %bitcast.31, bf16[1024,256]{1,0:T(8,128)(2,1)S(1)} %bitcast.29, ...), custom_call_target="tpu_custom_call", output_to_operand_aliasing={{0}: (4, {}), {1}: (5, {})} | custom-call | flops 1610612736 | bytes 6291456 | tf_op jit(solution)/shard_map/pallas_call | solution.py:177
  58.6 0.1 add.77
  58.8 12.0 %collective-permute-done.1 = bf16[768,256]{1,0:T(8,128)(2,1)S(1)} collective-permute-done((bf16[768,256]{1,0:T(8,128)(2,1)S(1)}, bf16[768,256]{1,0:T(8,128)(2,1)S(1)}, u32[]{:S(2)}, u32[]{:S(2)}) %collective-permute-start.1) | collective-permute-done | bytes 393248 | tf_op jit(solution)/shard_map/ppermute | solution.py:19
  70.8 0.1 pad_convert_fusion
  70.8 0.9 %fusion = (bf16[1024,128]{1,0:T(8,128)(2,1)}, bf16[1024,128]{1,0:T(8,128)(2,1)}) fusion(f32[1024,256]{1,0:T(8,128)S(1)} %pad_convert_fusion, f32[1024,256]{1,0:T(8,128)S(1)} %add.77), kind=kLoop, calls=%fused_computation.3 | loop fusion | flops 655360 | bytes 2621440 | tf_op jit(solution)/shard_map/convert_element_type | solution.py:241
  (5 shorter events, 0.0 us)
Async XLA Ops:
  0.6 1.0 %copy-start = (bf16[128,1024]{1,0:T(8,128)(2,1)S(1)}, bf16[128,1024]{1,0:T(8,128)(2,1)}, u32[]{:S(2)}) copy-start(bf16[128,1024]{1,0:T(8,128)(2,1)} %param.6) | copy-start | bytes 786436
  2.7 5.3 %copy-start.2 = (bf16[128,4096]{1,0:T(8,128)(2,1)S(1)}, bf16[128,4096]{1,0:T(8,128)(2,1)}, u32[]{:S(2)}) copy-start(bf16[128,4096]{1,0:T(8,128)(2,1)} %param.5) | copy-start | bytes 3145732
  3.5 14.8 %all-to-all-start.1 = ((bf16[128,8,256]{2,0,1:T(8,128)(2,1)}), bf16[128,8,256]{2,0,1:T(8,128)(2,1)S(1)}, u32[]{:S(2)}, u32[]{:S(2)}) async-start(bf16[128,8,256]{2,0,1:T(8,128)(2,1)} %pad_maximum_fusion), calls=%async_computation.1 | async-start | bytes 1048576 | tf_op jit(solution)/shard_map/all_to_all | solution.py:210
  18.3 19.5 %all-to-all-start = ((bf16[128,8,512]{2,0,1:T(8,128)(2,1)}), bf16[128,8,512]{2,0,1:T(8,128)(2,1)S(1)}, u32[]{:S(2)}, u32[]{:S(2)}) async-start(bf16[128,8,512]{2,0,1:T(8,128)(2,1)} %bitcast.26), calls=%async_computation | async-start | bytes 2097152 | tf_op jit(solution)/shard_map/all_to_all | solution.py:214
  22.0 0.7 copy-start.3
  23.7 14.2 %collective-permute-start = (bf16[768,256]{1,0:T(8,128)(2,1)}, bf16[768,256]{1,0:T(8,128)(2,1)S(1)}, u32[]{:S(2)}, u32[]{:S(2)}) collective-permute-start(bf16[768,256]{1,0:T(8,128)(2,1)} %bitcast.10), channel_id=1, source_target_pairs={{0,8},{8,16},{16,24},{24,32},{32,40},{40,48},{48,56},{56,64},{64,7... | collective-permute-start | bytes 1179656 | tf_op jit(solution)/shard_map/ppermute | solution.py:19
  28.7 9.2 %copy-start.1 = (bf16[1024,512]{1,0:T(8,128)(2,1)S(1)}, bf16[1024,512]{1,0:T(8,128)(2,1)}, u32[]{:S(2)}) copy-start(bf16[1024,512]{1,0:T(8,128)(2,1)} %refs_3_.1) | copy-start | bytes 3145732
  47.3 23.4 %collective-permute-start.1 = (bf16[768,256]{1,0:T(8,128)(2,1)S(1)}, bf16[768,256]{1,0:T(8,128)(2,1)S(1)}, u32[]{:S(2)}, u32[]{:S(2)}) collective-permute-start(bf16[768,256]{1,0:T(8,128)(2,1)S(1)} %get-tuple-element.17), channel_id=1, source_target_pairs={{8,0},{16,8},{24,16},{32,24},{40,32},{48,40},{56,48},{64,56},{72,6... | collective-permute-start | bytes 1179656 | tf_op jit(solution)/shard_map/ppermute | solution.py:19

commit v10 on v9

--- a/solution.py
+++ b/solution.py
@@ -141,7 +141,8 @@
             prior_out[:, HEAD_SIZE:] = prior_ref[:, HEAD_SIZE:].astype(prior_out.dtype)
 
 
-def attention_call(lo, packed, kv, earlier, grad, unit_list, out_alias=None, *, heads, interpret=False):
+def attention_call(lo, packed, kv, earlier, grad, unit_list, out_alias=None, *, heads, kv_block=0,
+                   interpret=False):
     ctx_rows = packed.shape[0]
     units = ctx_rows // BLOCK
     q_cols = heads * HEAD_SIZE
@@ -160,7 +161,8 @@
     operands = [lo, packed, kv] + ([earlier] if with_prior else []) + [grad]
     unit_block = pl.BlockSpec((BLOCK, q_cols), lambda i: (first_unit + i, 0))
     in_specs = [pl.BlockSpec(memory_space=pltpu.SMEM), unit_block]
-    in_specs += [whole(x) for x in operands[2:-1]] + [unit_block]
+    kv_spec = pl.BlockSpec((ctx_rows, kv_cols), lambda i: (0, kv_block))
+    in_specs += [kv_spec] + [whole(x) for x in operands[3:-1]] + [unit_block]
     if out_alias is not None:
         operands += list(out_alias)
         in_specs += [pl.BlockSpec(memory_space=pl.ANY)] * 2
@@ -200,21 +202,18 @@
     q_cols = query_matrix.shape[1] // head_groups
     k_cols = key_matrix.shape[1] // head_groups
     assert k_cols == HEAD_SIZE and 2 * token_per_shard == BLOCK
-    kv_packed = jnp.concatenate(
+    packed = jnp.concatenate(
         [
+            query_matrix.reshape(token_per_shard, head_groups, q_cols),
             key_matrix.reshape(token_per_shard, head_groups, k_cols),
             value_matrix.reshape(token_per_shard, head_groups, k_cols),
         ],
         axis=2,
     )
-    kv = lax.all_to_all(kv_packed, "head", split_axis=1, concat_axis=0, tiled=True)
-    ctx_rows = kv.shape[0]
-    kv = kv.reshape(ctx_rows, 2 * k_cols)
-    earlier_kv = from_behind(kv[BLOCK:], "ctx", 1)
-    packed = lax.all_to_all(
-        query_matrix.reshape(token_per_shard, head_groups, q_cols),
-        "head", split_axis=1, concat_axis=0, tiled=True,
-    ).reshape(ctx_rows, q_cols)
+    packed = lax.all_to_all(packed, "head", split_axis=1, concat_axis=0, tiled=True)
+    ctx_rows = packed.shape[0]
+    packed = packed.reshape(ctx_rows, q_cols + 2 * k_cols)
+    earlier_kv = from_behind(packed[BLOCK:, q_cols:], "ctx", 1)
     units = ctx_rows // BLOCK
     ctx_index = lax.axis_index("ctx")
     wanted = (ctx_index - 1) * units + jnp.arange(2 * units, dtype=jnp.int32)
@@ -227,12 +226,13 @@
     same = (joined_units[window] == own_units[:, None]).astype(jnp.int32)
     lo = (unit_ids + units + 1 - jnp.sum(same, axis=1)).astype(jnp.int32)
     heads = q_cols // HEAD_SIZE
-    first = attention_call(lo, packed, kv, earlier_kv, output_gradient, range(units - 1),
-                           heads=heads, interpret=INTERPRET)
-    attended_all, query_total, prior_grads, own_first = first
-    last = attention_call(lo, packed, kv, None, output_gradient, [units - 1],
-                          (attended_all, query_total), heads=heads, interpret=INTERPRET)
-    attended_all, query_total, own_last = last
+    kv_block = q_cols // (2 * k_cols)
+    attended_all, query_total, own_last = attention_call(
+        lo, packed, packed, None, output_gradient, [units - 1],
+        heads=heads, kv_block=kv_block, interpret=INTERPRET)
+    attended_all, query_total, prior_grads, own_first = attention_call(
+        lo, packed, packed, earlier_kv, output_gradient, range(units - 1), (attended_all, query_total),
+        heads=heads, kv_block=kv_block, interpret=INTERPRET)
     own_grads = own_first + own_last
     score_scale = HEAD_SIZE ** (-0.5)
     later = from_behind(prior_grads, "ctx", -1).astype(jnp.float32)

time: 72.1 us -> 76.1 us (1.055)
  waiting for transfers between devices: 29.4 us -> 40 us
  starting transfers between devices: 19.1 us -> 15.2 us
  local copies, waits for them, and re-layouts: 5.42 us -> 2.43 us
    all_to_all x2 -> x1, waiting for transfers between devices: 9.24 us -> 20.3 us  [local(): lax.all_to_all(packed, 'head', split_axis=1, concat_axis=0, tiled=True)]
    all_to_all x2 -> x1, starting transfers between devices: 8.03 us -> 4.6 us  [local(): lax.all_to_all(packed, 'head', split_axis=1, concat_axis=0, tiled=True)]
    unnamed x8, local copies, waits for them, and re-layouts: 1.61 us -> 0.02 us
    reshape x1, local copies, waits for them, and re-layouts: 1.07 us -> 0.12 us  [local(): value_matrix.reshape(token_per_shard, head_groups, k_cols)]
  transfers between devices with their start and end apart: 4 -> 3, of which waited for: 3 -> 3; matrix products, arithmetic and copies ran while one was open for 5% -> 2% of each run, Pallas kernels for 7% -> 7%
where the time goes in v10:
time: 76.1 us; the launch traced here: 75.9 us
  waiting for transfers between devices  40 us (53%)
  starting transfers between devices  15.2 us (20%)
  Pallas kernels  14.7 us (19%)
  other arithmetic  2.87 us (4%)
  local copies, waits for them, and re-layouts  2.43 us (3%)
    all_to_all x1, waiting for transfers between devices, local(): lax.all_to_all(packed, 'head', split_axis=1, concat_axis=0, tiled=True)  20.3 us
    ppermute x2, waiting for transfers between devices, from_behind(): return lax.ppermute(block, axis, route)  19.6 us
    pallas_call x2, Pallas kernels, attention_call(): pl.pallas_call(kernel, grid=(steps,), out_shape=tuple(out_shape), in_spec...  14.7 us
    ppermute x2, starting transfers between devices, from_behind(): return lax.ppermute(block, axis, route)  10.6 us
    all_to_all x1, starting transfers between devices, local(): lax.all_to_all(packed, 'head', split_axis=1, concat_axis=0, tiled=True)  4.6 us
  transfers between devices with their start and end apart: 3, of which 3 were waited for; matrix products, arithmetic and copies ran while one was open for 2% of the time, Pallas kernels for 7%

profile of v10, /device:TPU:102, one launch (start us, length us, event | category | flops | bytes accessed | tf_op | source)
XLA Modules:
  0.0 75.9 jit_solution(12525433585186134925)
XLA Ops:
  0.6 0.0 copy-start
  0.6 0.0 copy-start.2
  0.7 1.4 %copy.26 = bf16[16,8,8,512]{3,2,0,1:T(8,128)(2,1)S(1)} copy(bf16[16,8,8,512]{3,2,1,0:T(8,128)(2,1)} %bitcast.27) | data formatting | bytes 2097152 | tf_op jit(solution)/shard_map/reshape | solution.py:207
  2.0 0.0 copy-done
  2.0 0.0 copy-done.2
  2.0 0.1 copy_bitcast_fusion.1
  2.2 1.3 %pad_maximum_fusion = bf16[128,8,768]{2,0,1:T(8,128)(2,1)} fusion(bf16[128,8,128]{2,0,1:T(8,128)(2,1)S(1)} %get-tuple-element.20, bf16[128,8,128]{2,0,1:T(8,128)(2,1)S(1)} %get-tuple-element.21, bf16[128,8,512]{2,0,1:T(8,128)(2,1)S(1)} %bitcast.26), kind=kLoop, calls=%fused_computation.1 | loop fusion | flops 4718592 | bytes 3145728 | tf_op jit(solution)/shard_map/concatenate | solution.py:205
  3.5 0.0 copy-start.3
  3.5 4.6 %all-to-all-start = ((bf16[128,8,768]{2,0,1:T(8,128)(2,1)}), bf16[128,8,768]{2,0,1:T(8,128)(2,1)S(1)}, u32[]{:S(2)}, u32[]{:S(2)}) async-start(bf16[128,8,768]{2,0,1:T(8,128)(2,1)} %pad_maximum_fusion), calls=%async_computation | async-start | bytes 3145728 | tf_op jit(solution)/shard_map/all_to_all | solution.py:213
  8.1 0.0 copy-start.1
  8.1 0.0 copy-done.3
  8.1 0.2 select_reduce_fusion
  8.3 0.1 slice.18
  8.4 0.1 compare_select_fusion
  8.4 0.1 reshape.77
  8.5 0.7 gather_fusion
  9.2 0.1 reshape.76
  9.3 20.3 %all-to-all-done = bf16[128,8,768]{2,0,1:T(8,128)(2,1)S(1)} async-done(((bf16[128,8,768]{2,0,1:T(8,128)(2,1)}), bf16[128,8,768]{2,0,1:T(8,128)(2,1)S(1)}, u32[]{:S(2)}, u32[]{:S(2)}) %all-to-all-start) | async-done | bytes 1572896 | tf_op jit(solution)/shard_map/all_to_all | solution.py:213
  29.6 5.0 %collective-permute-start = (bf16[768,256]{1,0:T(8,128)(2,1)S(1)}, bf16[768,256]{1,0:T(8,128)(2,1)S(1)}, u32[]{:S(2)}, u32[]{:S(2)}) collective-permute-start(bf16[768,256]{1,0:T(8,128)(2,1)S(1)} %slice.26), channel_id=1, source_target_pairs={{0,8},{8,16},{16,24},{24,32},{32,40},{40,48},{48,56},{56,64},{64,7... | collective-permute-start | bytes 1179656 | tf_op jit(solution)/shard_map/ppermute | solution.py:19
  34.6 0.2 convert_reduce_fusion
  34.8 0.0 copy-done.1
  34.8 5.2 %shard_map.84 = (bf16[1024,512]{1,0:T(8,128)(2,1)}, bf16[1024,512]{1,0:T(8,128)(2,1)}, f32[1024,256]{1,0:T(8,128)S(1)}) custom-call(s32[4]{0:T(128)S(1)} %add_subtract_fusion.refs_0_, bf16[1024,768]{1,0:T(8,128)(2,1)S(1)} %bitcast.22, bf16[1024,768]{1,0:T(8,128)(2,1)S(1)} %bitcast.23, bf16[1024,512]{1,0:T(8,128)(2,1)S(1)} %copy-done.1), custom_call_target="tpu_custom_call" | custom-call | flops 1610612736 | bytes 6291456 | tf_op jit(solution)/shard_map/pallas_call | solution.py:179
  40.0 2.7 %collective-permute-done.refs_3_ = bf16[768,256]{1,0:T(8,128)(2,1)S(1)} collective-permute-done((bf16[768,256]{1,0:T(8,128)(2,1)S(1)}, bf16[768,256]{1,0:T(8,128)(2,1)S(1)}, u32[]{:S(2)}, u32[]{:S(2)}) %collective-permute-start) | collective-permute-done | bytes 393248 | tf_op jit(solution)/shard_map/ppermute | solution.py:19
  42.7 9.6 %shard_map.85 = (bf16[1024,512]{1,0:T(8,128)(2,1)}, bf16[1024,512]{1,0:T(8,128)(2,1)}, bf16[768,256]{1,0:T(8,128)(2,1)S(1)}, f32[1024,256]{1,0:T(8,128)S(1)}) custom-call(s32[4]{0:T(128)S(1)} %add_subtract_fusion.refs_0_, bf16[1024,768]{1,0:T(8,128)(2,1)S(1)} %bitcast.24, ...), custom_call_target="tpu_custom_call", output_to_operand_aliasing={{0}: (5, {}), {1}: (6, {})} | custom-call | flops 4831838208 | bytes 6291456 | tf_op jit(solution)/shard_map/pallas_call | solution.py:179
  52.2 5.6 %collective-permute-start.1 = (bf16[768,256]{1,0:T(8,128)(2,1)S(1)}, bf16[768,256]{1,0:T(8,128)(2,1)S(1)}, u32[]{:S(2)}, u32[]{:S(2)}) collective-permute-start(bf16[768,256]{1,0:T(8,128)(2,1)S(1)} %get-tuple-element.17), channel_id=1, source_target_pairs={{8,0},{16,8},{24,16},{32,24},{40,32},{48,40},{56,48},{64,56},{72,6... | collective-permute-start | bytes 1179656 | tf_op jit(solution)/shard_map/ppermute | solution.py:19
  57.9 0.1 add.77
  58.0 16.9 %collective-permute-done.1 = bf16[768,256]{1,0:T(8,128)(2,1)S(1)} collective-permute-done((bf16[768,256]{1,0:T(8,128)(2,1)S(1)}, bf16[768,256]{1,0:T(8,128)(2,1)S(1)}, u32[]{:S(2)}, u32[]{:S(2)}) %collective-permute-start.1) | collective-permute-done | bytes 393248 | tf_op jit(solution)/shard_map/ppermute | solution.py:19
  74.9 0.1 pad_convert_fusion
  75.0 0.9 %fusion = (bf16[1024,128]{1,0:T(8,128)(2,1)}, bf16[1024,128]{1,0:T(8,128)(2,1)}) fusion(f32[1024,256]{1,0:T(8,128)S(1)} %pad_convert_fusion, f32[1024,256]{1,0:T(8,128)S(1)} %add.77), kind=kLoop, calls=%fused_computation.4 | loop fusion | flops 655360 | bytes 2621440 | tf_op jit(solution)/shard_map/convert_element_type | solution.py:241
  (6 shorter events, 0.1 us)
Async XLA Ops:
  0.6 1.4 %copy-start = (bf16[128,1024]{1,0:T(8,128)(2,1)S(1)}, bf16[128,1024]{1,0:T(8,128)(2,1)}, u32[]{:S(2)}) copy-start(bf16[128,1024]{1,0:T(8,128)(2,1)} %param.6) | copy-start | bytes 786436
  0.6 1.4 %copy-start.2 = (bf16[128,1024]{1,0:T(8,128)(2,1)S(1)}, bf16[128,1024]{1,0:T(8,128)(2,1)}, u32[]{:S(2)}) copy-start(bf16[128,1024]{1,0:T(8,128)(2,1)} %param.7) | copy-start | bytes 786436
  3.5 4.6 %copy-start.3 = (s32[128]{0:T(128)S(1)}, s32[128]{0:T(128)}, u32[]{:S(2)}) copy-start(s32[128]{0:T(128)} %param.9) | copy-start | bytes 1540
  3.5 26.2 %all-to-all-start = ((bf16[128,8,768]{2,0,1:T(8,128)(2,1)}), bf16[128,8,768]{2,0,1:T(8,128)(2,1)S(1)}, u32[]{:S(2)}, u32[]{:S(2)}) async-start(bf16[128,8,768]{2,0,1:T(8,128)(2,1)} %pad_maximum_fusion), calls=%async_computation | async-start | bytes 3145728 | tf_op jit(solution)/shard_map/all_to_all | solution.py:213
  8.1 26.7 %copy-start.1 = (bf16[1024,512]{1,0:T(8,128)(2,1)S(1)}, bf16[1024,512]{1,0:T(8,128)(2,1)}, u32[]{:S(2)}) copy-start(bf16[1024,512]{1,0:T(8,128)(2,1)} %refs_4_.1) | copy-start | bytes 3145732
  29.6 13.0 %collective-permute-start = (bf16[768,256]{1,0:T(8,128)(2,1)S(1)}, bf16[768,256]{1,0:T(8,128)(2,1)S(1)}, u32[]{:S(2)}, u32[]{:S(2)}) collective-permute-start(bf16[768,256]{1,0:T(8,128)(2,1)S(1)} %slice.26), channel_id=1, source_target_pairs={{0,8},{8,16},{16,24},{24,32},{32,40},{40,48},{48,56},{56,64},{64,7... | collective-permute-start | bytes 1179656 | tf_op jit(solution)/shard_map/ppermute | solution.py:19
  52.2 22.7 %collective-permute-start.1 = (bf16[768,256]{1,0:T(8,128)(2,1)S(1)}, bf16[768,256]{1,0:T(8,128)(2,1)S(1)}, u32[]{:S(2)}, u32[]{:S(2)}) collective-permute-start(bf16[768,256]{1,0:T(8,128)(2,1)S(1)} %get-tuple-element.17), channel_id=1, source_target_pairs={{8,0},{16,8},{24,16},{32,24},{40,32},{48,40},{56,48},{64,56},{72,6... | collective-permute-start | bytes 1179656 | tf_op jit(solution)/shard_map/ppermute | solution.py:19

commit v11 on v9

--- a/solution.py
+++ b/solution.py
@@ -31,13 +31,14 @@
     return lax.dot_general(a, b, (((1,), (0,)), ((), ())), preferred_element_type=jnp.float32)
 
 
-def attention_kernel(*refs, first_unit, units, heads, with_prior, aliased, steps):
+def attention_kernel(*refs, first_unit, units, heads, with_prior, aliased, steps, own_in):
     refs = list(refs)
     lo_ref, q_ref, kv_ref = refs[:3]
     refs = refs[3:]
     earlier_ref = refs.pop(0) if with_prior else None
     grad_ref = refs.pop(0)
     refs = refs[aliased:]
+    own_init = refs.pop(0) if own_in else None
     att_ref, dq_ref = refs[:2]
     refs = refs[2:]
     prior_out = refs.pop(0) if with_prior else None
@@ -50,7 +51,10 @@
     def _():
         if with_prior:
             prior_ref[...] = jnp.zeros(prior_ref.shape, prior_ref.dtype)
-        own_ref[...] = jnp.zeros(own_ref.shape, own_ref.dtype)
+        if own_in:
+            own_ref[...] = own_init[...]
+        else:
+            own_ref[...] = jnp.zeros(own_ref.shape, own_ref.dtype)
 
     rows = heads * BLOCK
     causal = (lax.broadcasted_iota(jnp.int32, (rows, BLOCK), 0) % BLOCK
@@ -141,7 +145,8 @@
             prior_out[:, HEAD_SIZE:] = prior_ref[:, HEAD_SIZE:].astype(prior_out.dtype)
 
 
-def attention_call(lo, packed, kv, earlier, grad, unit_list, out_alias=None, *, heads, interpret=False):
+def attention_call(lo, packed, kv, earlier, grad, unit_list, out_alias=None, own=None, *, heads,
+                   interpret=False):
     ctx_rows = packed.shape[0]
     units = ctx_rows // BLOCK
     q_cols = heads * HEAD_SIZE
@@ -151,7 +156,8 @@
     first_unit = unit_list[0]
     steps = len(unit_list)
     kernel = functools.partial(attention_kernel, first_unit=first_unit, units=units, heads=heads,
-                               with_prior=with_prior, aliased=aliased, steps=steps)
+                               with_prior=with_prior, aliased=aliased, steps=steps,
+                               own_in=own is not None)
     rows = heads * BLOCK
 
     def whole(x):
@@ -174,6 +180,10 @@
     visible_blocks = 4 * len(unit_list)
     flops = 12 * rows * BLOCK * HEAD_SIZE * visible_blocks
     aliases = {} if out_alias is None else {len(operands) - 2: 0, len(operands) - 1: 1}
+    if own is not None:
+        aliases[len(operands)] = len(out_shape) - 1
+        operands.append(own)
+        in_specs.append(whole(own))
     return pl.pallas_call(
         kernel,
         grid=(steps,),
@@ -231,9 +241,8 @@
                            heads=heads, interpret=INTERPRET)
     attended_all, query_total, prior_grads, own_first = first
     last = attention_call(lo, packed, kv, None, output_gradient, [units - 1],
-                          (attended_all, query_total), heads=heads, interpret=INTERPRET)
-    attended_all, query_total, own_last = last
-    own_grads = own_first + own_last
+                          (attended_all, query_total), own_first, heads=heads, interpret=INTERPRET)
+    attended_all, query_total, own_grads = last
     score_scale = HEAD_SIZE ** (-0.5)
     later = from_behind(prior_grads, "ctx", -1).astype(jnp.float32)
     later = jnp.concatenate([jnp.zeros((BLOCK, 2 * k_cols), jnp.float32), later], axis=0)

time: 72.1 us -> 72.1 us (level)
  Pallas kernels: 14.7 us -> 18.3 us
  starting transfers between devices: 19.1 us -> 17.2 us
  waiting for transfers between devices: 29.4 us -> 27.9 us
    pallas_call x2, Pallas kernels: 14.7 us -> 18.3 us  [attention_call(): pl.pallas_call(kernel, grid=(steps,), out_shape=tuple(out_shape), in_spec...]
    ppermute x2, starting transfers between devices: 11 us -> 9.14 us  [from_behind(): return lax.ppermute(block, axis, route)]
    ppermute x2, waiting for transfers between devices: 20.2 us -> 18.6 us  [from_behind(): return lax.ppermute(block, axis, route)]
  transfers between devices with their start and end apart: 4 -> 4, of which waited for: 3 -> 3; matrix products, arithmetic and copies ran while one was open for 5% -> 4% of each run, Pallas kernels for 7% -> 7%
where the time goes in v11:
time: 72.1 us; the launch traced here: 71.7 us
  waiting for transfers between devices  27.9 us (39%)
  Pallas kernels  18.3 us (25%)
  starting transfers between devices  17.2 us (24%)
  local copies, waits for them, and re-layouts  5.42 us (8%)
  other arithmetic  2.3 us (3%)
    ppermute x2, waiting for transfers between devices, from_behind(): return lax.ppermute(block, axis, route)  18.6 us
    pallas_call x2, Pallas kernels, attention_call(): pl.pallas_call(kernel, grid=(steps,), out_shape=tuple(out_shape), in_spec...  18.3 us
    all_to_all x1, waiting for transfers between devices, local(): lax.all_to_all(kv_packed, 'head', split_axis=1, concat_axis=0, tiled=True)  9.24 us
    ppermute x2, starting transfers between devices, from_behind(): return lax.ppermute(block, axis, route)  9.14 us
    all_to_all x1, starting transfers between devices, local(): lax.all_to_all(kv_packed, 'head', split_axis=1, concat_axis=0, tiled=True)  4.47 us
    all_to_all x1, starting transfers between devices, local(): lax.all_to_all(query_matrix.reshape(token_per_shard, head_groups, q_cols)...  3.56 us
    unnamed x8, local copies, waits for them, and re-layouts  1.61 us
  transfers between devices with their start and end apart: 4, of which 3 were waited for; matrix products, arithmetic and copies ran while one was open for 4% of the time, Pallas kernels for 7%

profile of v11, /device:TPU:102, one launch (start us, length us, event | category | flops | bytes accessed | tf_op | source)
XLA Modules:
  0.0 71.7 jit_solution(18326799398079978230)
XLA Ops:
  0.6 0.0 copy-start
  0.6 0.9 %copy-done = bf16[128,1024]{1,0:T(8,128)(2,1)S(1)} copy-done((bf16[128,1024]{1,0:T(8,128)(2,1)S(1)}, bf16[128,1024]{1,0:T(8,128)(2,1)}, u32[]{:S(2)}) %copy-start) | copy-done | bytes 262168
  1.6 1.1 %copy_bitcast_fusion.1 = (bf16[128,8,128]{2,0,1:T(8,128)(2,1)S(1)}, bf16[128,8,128]{2,0,1:T(8,128)(2,1)S(1)}) fusion(bf16[128,1024]{1,0:T(8,128)(2,1)S(1)} %copy-done, bf16[128,1024]{1,0:T(8,128)(2,1)} %param.7), kind=kLoop, calls=%fused_computation.8 | loop fusion | bytes 1048576 | tf_op jit(solution)/shard_map/reshape | solution.py:216
  2.7 0.0 copy-start.2
  2.7 0.9 %pad_maximum_fusion = bf16[128,8,256]{2,0,1:T(8,128)(2,1)} fusion(bf16[128,8,128]{2,0,1:T(8,128)(2,1)S(1)} %get-tuple-element.20, bf16[128,8,128]{2,0,1:T(8,128)(2,1)S(1)} %get-tuple-element.21), kind=kLoop, calls=%fused_computation.6 | loop fusion | flops 1048576 | bytes 1048576 | tf_op jit(solution)/shard_map/concatenate | solution.py:213
  3.5 4.5 %all-to-all-start.1 = ((bf16[128,8,256]{2,0,1:T(8,128)(2,1)}), bf16[128,8,256]{2,0,1:T(8,128)(2,1)S(1)}, u32[]{:S(2)}, u32[]{:S(2)}) async-start(bf16[128,8,256]{2,0,1:T(8,128)(2,1)} %pad_maximum_fusion), calls=%async_computation.1 | async-start | bytes 1048576 | tf_op jit(solution)/shard_map/all_to_all | solution.py:220
  8.0 0.0 copy-done.2
  8.0 1.1 %copy.27 = bf16[16,8,8,512]{3,2,0,1:T(8,128)(2,1)} copy(bf16[16,8,8,512]{3,2,1,0:T(8,128)(2,1)S(1)} %bitcast.32) | data formatting | bytes 2097152 | tf_op jit(solution)/shard_map/reshape | solution.py:225
  9.1 9.2 %all-to-all-done.1 = bf16[128,8,256]{2,0,1:T(8,128)(2,1)S(1)} async-done(((bf16[128,8,256]{2,0,1:T(8,128)(2,1)}), bf16[128,8,256]{2,0,1:T(8,128)(2,1)S(1)}, u32[]{:S(2)}, u32[]{:S(2)}) %all-to-all-start.1) | async-done | bytes 524320 | tf_op jit(solution)/shard_map/all_to_all | solution.py:220
  18.3 3.6 %all-to-all-start = ((bf16[128,8,512]{2,0,1:T(8,128)(2,1)}), bf16[128,8,512]{2,0,1:T(8,128)(2,1)S(1)}, u32[]{:S(2)}, u32[]{:S(2)}) async-start(bf16[128,8,512]{2,0,1:T(8,128)(2,1)} %bitcast.26), calls=%async_computation | async-start | bytes 2097152 | tf_op jit(solution)/shard_map/all_to_all | solution.py:224
  21.9 0.1 compare_select_fusion
  22.0 0.1 reshape.83
  22.0 0.0 copy-start.3
  22.1 0.7 copy-done.3
  22.7 0.2 select_reduce_fusion
  22.9 0.8 %slice.30 = bf16[6,128,1,256]{3,1,0,2:T(8,128)(2,1)} slice(bf16[8,128,1,256]{3,1,0,2:T(8,128)(2,1)S(1)} %bitcast.27), slice={[2:8], [0:128], [0:1], [0:256]} | slice | bytes 786432 | tf_op jit(solution)/shard_map/slice | solution.py:223
  23.7 4.9 %collective-permute-start = (bf16[768,256]{1,0:T(8,128)(2,1)}, bf16[768,256]{1,0:T(8,128)(2,1)S(1)}, u32[]{:S(2)}, u32[]{:S(2)}) collective-permute-start(bf16[768,256]{1,0:T(8,128)(2,1)} %bitcast.10), channel_id=1, source_target_pairs={{0,8},{8,16},{16,24},{24,32},{32,40},{40,48},{48,56},{56,64},{64,7... | collective-permute-start | bytes 1179656 | tf_op jit(solution)/shard_map/ppermute | solution.py:19
  28.6 0.1 slice.21
  28.7 0.0 copy-start.1
  28.7 0.7 gather_fusion
  29.4 0.1 reshape.82
  29.4 0.2 convert_reduce_fusion
  29.6 8.2 %collective-permute-done.refs_3_ = bf16[768,256]{1,0:T(8,128)(2,1)S(1)} collective-permute-done((bf16[768,256]{1,0:T(8,128)(2,1)}, bf16[768,256]{1,0:T(8,128)(2,1)S(1)}, u32[]{:S(2)}, u32[]{:S(2)}) %collective-permute-start) | collective-permute-done | bytes 393248 | tf_op jit(solution)/shard_map/ppermute | solution.py:19
  37.9 0.0 all-to-all-done
  37.9 0.0 copy-done.1
  37.9 13.1 %shard_map.84 = (bf16[1024,512]{1,0:T(8,128)(2,1)}, bf16[1024,512]{1,0:T(8,128)(2,1)}, bf16[768,256]{1,0:T(8,128)(2,1)S(1)}, f32[1024,256]{1,0:T(8,128)S(1)}) custom-call(s32[4]{0:T(128)S(1)} %add_subtract_fusion.refs_0_, bf16[1024,512]{1,0:T(8,128)(2,1)S(1)} %bitcast.30, bf16[1024,256]{1,0:T(8,128)(2,1)S(1)} %bitcast.28, ...), custom_call_target="tpu_custom_call" | custom-call | flops 4831838208 | bytes 6291456 | tf_op jit(solution)/shard_map/pallas_call | solution.py:187
  50.9 4.2 %collective-permute-start.1 = (bf16[768,256]{1,0:T(8,128)(2,1)S(1)}, bf16[768,256]{1,0:T(8,128)(2,1)S(1)}, u32[]{:S(2)}, u32[]{:S(2)}) collective-permute-start(bf16[768,256]{1,0:T(8,128)(2,1)S(1)} %get-tuple-element.17), channel_id=1, source_target_pairs={{8,0},{16,8},{24,16},{32,24},{40,32},{48,40},{56,48},{64,56},{72,6... | collective-permute-start | bytes 1179656 | tf_op jit(solution)/shard_map/ppermute | solution.py:19
  55.1 5.2 %shard_map.85 = (bf16[1024,512]{1,0:T(8,128)(2,1)}, bf16[1024,512]{1,0:T(8,128)(2,1)}, f32[1024,256]{1,0:T(8,128)S(1)}) custom-call(s32[4]{0:T(128)S(1)} %add_subtract_fusion.refs_0_, bf16[1024,512]{1,0:T(8,128)(2,1)S(1)} %bitcast.31, bf16[1024,256]{1,0:T(8,128)(2,1)S(1)} %bitcast.29, ...), custom_call_target="tpu_custom_call", output_to_operand_aliasing={{0}: (4, {}), {1}: (5, {}), {2}: (6, {})} | custom-call | flops 1610612736 | bytes 6291456 | tf_op jit(solution)/shard_map/pallas_call | solution.py:187
  60.3 10.4 %collective-permute-done.1 = bf16[768,256]{1,0:T(8,128)(2,1)S(1)} collective-permute-done((bf16[768,256]{1,0:T(8,128)(2,1)S(1)}, bf16[768,256]{1,0:T(8,128)(2,1)S(1)}, u32[]{:S(2)}, u32[]{:S(2)}) %collective-permute-start.1) | collective-permute-done | bytes 393248 | tf_op jit(solution)/shard_map/ppermute | solution.py:19
  70.8 0.1 pad_convert_fusion
  70.8 0.9 %fusion = (bf16[1024,128]{1,0:T(8,128)(2,1)}, bf16[1024,128]{1,0:T(8,128)(2,1)}) fusion(f32[1024,256]{1,0:T(8,128)S(1)} %pad_convert_fusion, f32[1024,256]{1,0:T(8,128)S(1)} %get-tuple-element.16), kind=kLoop, calls=%fused_computation.3 | loop fusion | flops 655360 | bytes 2621440 | tf_op jit(solution)/shard_map/convert_element_type | solution.py:250
  (5 shorter events, 0.0 us)
Async XLA Ops:
  0.6 1.0 %copy-start = (bf16[128,1024]{1,0:T(8,128)(2,1)S(1)}, bf16[128,1024]{1,0:T(8,128)(2,1)}, u32[]{:S(2)}) copy-start(bf16[128,1024]{1,0:T(8,128)(2,1)} %param.6) | copy-start | bytes 786436
  2.7 5.3 %copy-start.2 = (bf16[128,4096]{1,0:T(8,128)(2,1)S(1)}, bf16[128,4096]{1,0:T(8,128)(2,1)}, u32[]{:S(2)}) copy-start(bf16[128,4096]{1,0:T(8,128)(2,1)} %param.5) | copy-start | bytes 3145732
  3.5 14.8 %all-to-all-start.1 = ((bf16[128,8,256]{2,0,1:T(8,128)(2,1)}), bf16[128,8,256]{2,0,1:T(8,128)(2,1)S(1)}, u32[]{:S(2)}, u32[]{:S(2)}) async-start(bf16[128,8,256]{2,0,1:T(8,128)(2,1)} %pad_maximum_fusion), calls=%async_computation.1 | async-start | bytes 1048576 | tf_op jit(solution)/shard_map/all_to_all | solution.py:220
  18.3 19.5 %all-to-all-start = ((bf16[128,8,512]{2,0,1:T(8,128)(2,1)}), bf16[128,8,512]{2,0,1:T(8,128)(2,1)S(1)}, u32[]{:S(2)}, u32[]{:S(2)}) async-start(bf16[128,8,512]{2,0,1:T(8,128)(2,1)} %bitcast.26), calls=%async_computation | async-start | bytes 2097152 | tf_op jit(solution)/shard_map/all_to_all | solution.py:224
  22.0 0.7 copy-start.3
  23.7 14.2 %collective-permute-start = (bf16[768,256]{1,0:T(8,128)(2,1)}, bf16[768,256]{1,0:T(8,128)(2,1)S(1)}, u32[]{:S(2)}, u32[]{:S(2)}) collective-permute-start(bf16[768,256]{1,0:T(8,128)(2,1)} %bitcast.10), channel_id=1, source_target_pairs={{0,8},{8,16},{16,24},{24,32},{32,40},{40,48},{48,56},{56,64},{64,7... | collective-permute-start | bytes 1179656 | tf_op jit(solution)/shard_map/ppermute | solution.py:19
  28.7 9.2 %copy-start.1 = (bf16[1024,512]{1,0:T(8,128)(2,1)S(1)}, bf16[1024,512]{1,0:T(8,128)(2,1)}, u32[]{:S(2)}) copy-start(bf16[1024,512]{1,0:T(8,128)(2,1)} %refs_3_.1) | copy-start | bytes 3145732
  50.9 19.8 %collective-permute-start.1 = (bf16[768,256]{1,0:T(8,128)(2,1)S(1)}, bf16[768,256]{1,0:T(8,128)(2,1)S(1)}, u32[]{:S(2)}, u32[]{:S(2)}) collective-permute-start(bf16[768,256]{1,0:T(8,128)(2,1)S(1)} %get-tuple-element.17), channel_id=1, source_target_pairs={{8,0},{16,8},{24,16},{32,24},{40,32},{48,40},{56,48},{64,56},{72,6... | collective-permute-start | bytes 1179656 | tf_op jit(solution)/shard_map/ppermute | solution.py:19

commit v12 on v11

--- a/solution.py
+++ b/solution.py
@@ -143,6 +143,24 @@
         def _():
             prior_out[:, 0:HEAD_SIZE] = (prior_ref[:, 0:HEAD_SIZE] * scale).astype(prior_out.dtype)
             prior_out[:, HEAD_SIZE:] = prior_ref[:, HEAD_SIZE:].astype(prior_out.dtype)
+
+
+def kv_pack_kernel(k_ref, v_ref, o_ref, *, groups, rows):
+    for g in range(groups):
+        o_ref[g * rows:(g + 1) * rows, 0:HEAD_SIZE] = k_ref[:, g * HEAD_SIZE:(g + 1) * HEAD_SIZE]
+        o_ref[g * rows:(g + 1) * rows, HEAD_SIZE:] = v_ref[:, g * HEAD_SIZE:(g + 1) * HEAD_SIZE]
+
+
+def kv_pack(key_matrix, value_matrix, groups, interpret=False):
+    rows = key_matrix.shape[0]
+    vmem = pltpu.MemorySpace.VMEM
+    return pl.pallas_call(
+        functools.partial(kv_pack_kernel, groups=groups, rows=rows),
+        out_shape=jax.ShapeDtypeStruct((groups * rows, 2 * HEAD_SIZE), key_matrix.dtype),
+        in_specs=[pl.BlockSpec(memory_space=vmem)] * 2,
+        out_specs=pl.BlockSpec(memory_space=vmem),
+        interpret=interpret,
+    )(key_matrix, value_matrix)
 
 
 def attention_call(lo, packed, kv, earlier, grad, unit_list, out_alias=None, own=None, *, heads,
@@ -210,16 +228,9 @@
     q_cols = query_matrix.shape[1] // head_groups
     k_cols = key_matrix.shape[1] // head_groups
     assert k_cols == HEAD_SIZE and 2 * token_per_shard == BLOCK
-    kv_packed = jnp.concatenate(
-        [
-            key_matrix.reshape(token_per_shard, head_groups, k_cols),
-            value_matrix.reshape(token_per_shard, head_groups, k_cols),
-        ],
-        axis=2,
-    )
-    kv = lax.all_to_all(kv_packed, "head", split_axis=1, concat_axis=0, tiled=True)
+    kv_packed = kv_pack(key_matrix, value_matrix, head_groups, interpret=INTERPRET)
+    kv = lax.all_to_all(kv_packed, "head", split_axis=0, concat_axis=0, tiled=True)
     ctx_rows = kv.shape[0]
-    kv = kv.reshape(ctx_rows, 2 * k_cols)
     earlier_kv = from_behind(kv[BLOCK:], "ctx", 1)
     packed = lax.all_to_all(
         query_matrix.reshape(token_per_shard, head_groups, q_cols),

time: 72.1 us -> 70.6 us (0.979)
  local copies, waits for them, and re-layouts: 5.42 us -> 2.66 us
  starting transfers between devices: 17.2 us -> 14.9 us
  waiting for transfers between devices: 27.9 us -> 30 us
  Pallas kernels: 18.3 us -> 20.2 us
  other arithmetic: 2.3 us -> 1.44 us
    ppermute x2, starting transfers between devices: 9.14 us -> 6.86 us  [from_behind(): return lax.ppermute(block, axis, route)]
    pallas_call x0 -> x1, Pallas kernels: none -> 2 us  [kv_pack(): pl.pallas_call(functools.partial(kv_pack_kernel, groups=groups, rows=rows...]
    ppermute x2, waiting for transfers between devices: 18.6 us -> 19.8 us  [from_behind(): return lax.ppermute(block, axis, route)]
    reshape x1 -> x0, local copies, waits for them, and re-layouts: 1.07 us -> none  [local(): value_matrix.reshape(token_per_shard, head_groups, k_cols)]
    unnamed x8 -> x6, local copies, waits for them, and re-layouts: 1.61 us -> 0.66 us
    all_to_all x1, waiting for transfers between devices: 0.01 us -> 0.94 us  [local(): lax.all_to_all(query_matrix.reshape(token_per_shard, head_groups, q_cols)...]
    concatenate x1 -> x0, other arithmetic: 0.86 us -> none  [local(): jnp.concatenate([key_matrix.reshape(token_per_shard, head_groups, k_cols)...]
    slice x1, local copies, waits for them, and re-layouts: 0.77 us -> 0.03 us  [local(): earlier_kv = from_behind(kv[BLOCK:], 'ctx', 1)]
  transfers between devices with their start and end apart: 4 -> 4, of which waited for: 3 -> 4; matrix products, arithmetic and copies ran while one was open for 4% -> 4% of each run, Pallas kernels for 7% -> 7%
where the time goes in v12:
time: 70.6 us; the launch traced here: 69.9 us
  waiting for transfers between devices  30 us (42%)
  Pallas kernels  20.2 us (29%)
  starting transfers between devices  14.9 us (21%)
  local copies, waits for them, and re-layouts  2.66 us (4%)
  other arithmetic  1.44 us (2%)
  between operations  0.71 us (1%)
    ppermute x2, waiting for transfers between devices, from_behind(): return lax.ppermute(block, axis, route)  19.8 us
    pallas_call x2, Pallas kernels, attention_call(): pl.pallas_call(kernel, grid=(steps,), out_shape=tuple(out_shape), in_spec...  18.2 us
    all_to_all x1, waiting for transfers between devices, local(): lax.all_to_all(kv_packed, 'head', split_axis=0, concat_axis=0, tiled=True)  9.24 us
    ppermute x2, starting transfers between devices, from_behind(): return lax.ppermute(block, axis, route)  6.86 us
    all_to_all x1, starting transfers between devices, local(): lax.all_to_all(kv_packed, 'head', split_axis=0, concat_axis=0, tiled=True)  4.47 us
    all_to_all x1, starting transfers between devices, local(): lax.all_to_all(query_matrix.reshape(token_per_shard, head_groups, q_cols)...  3.56 us
    pallas_call x1, Pallas kernels, kv_pack(): pl.pallas_call(functools.partial(kv_pack_kernel, groups=groups, rows=rows...  2 us
  transfers between devices with their start and end apart: 4, of which 4 were waited for; matrix products, arithmetic and copies ran while one was open for 4% of the time, Pallas kernels for 7%

profile of v12, /device:TPU:102, one launch (start us, length us, event | category | flops | bytes accessed | tf_op | source)
XLA Modules:
  0.0 69.9 jit_solution(5592268942340292497)
XLA Ops:
  0.6 0.0 copy-start.1
  0.6 2.0 %shard_map.84 = bf16[1024,256]{1,0:T(8,128)(2,1)} custom-call(bf16[128,1024]{1,0:T(8,128)(2,1)} %k_ref.1, bf16[128,1024]{1,0:T(8,128)(2,1)} %v_ref.1), custom_call_target="tpu_custom_call" | custom-call | tf_op jit(solution)/shard_map/pallas_call | solution.py:157
  2.6 4.5 %all-to-all-start.1 = ((bf16[8,128,256]{2,1,0:T(8,128)(2,1)}), bf16[8,128,256]{2,1,0:T(8,128)(2,1)S(1)}, u32[]{:S(2)}, u32[]{:S(2)}) async-start(bf16[8,128,256]{2,1,0:T(8,128)(2,1)} %bitcast.18), calls=%async_computation.1 | async-start | bytes 1048576 | tf_op jit(solution)/shard_map/all_to_all | solution.py:232
  7.1 0.0 copy-done.1
  7.1 1.1 %copy.17 = bf16[16,8,8,512]{3,2,0,1:T(8,128)(2,1)} copy(bf16[16,8,8,512]{3,2,1,0:T(8,128)(2,1)S(1)} %bitcast.19) | data formatting | bytes 2097152 | tf_op jit(solution)/shard_map/reshape | solution.py:236
  8.2 9.2 %all-to-all-done.1 = bf16[8,128,256]{2,1,0:T(8,128)(2,1)S(1)} async-done(((bf16[8,128,256]{2,1,0:T(8,128)(2,1)}), bf16[8,128,256]{2,1,0:T(8,128)(2,1)S(1)}, u32[]{:S(2)}, u32[]{:S(2)}) %all-to-all-start.1) | async-done | bytes 524320 | tf_op jit(solution)/shard_map/all_to_all | solution.py:232
  17.4 3.6 %all-to-all-start = ((bf16[128,8,512]{2,0,1:T(8,128)(2,1)}), bf16[128,8,512]{2,0,1:T(8,128)(2,1)S(1)}, u32[]{:S(2)}, u32[]{:S(2)}) async-start(bf16[128,8,512]{2,0,1:T(8,128)(2,1)} %bitcast.13), calls=%async_computation | async-start | bytes 2097152 | tf_op jit(solution)/shard_map/all_to_all | solution.py:235
  21.0 0.1 compare_select_fusion
  21.1 0.1 reshape.72
  21.2 0.0 copy-start.2
  21.2 0.7 copy-done.2
  21.8 0.2 select_reduce_fusion
  22.0 5.0 %collective-permute-start = (bf16[768,256]{1,0:T(8,128)(2,1)S(1)}, bf16[768,256]{1,0:T(8,128)(2,1)S(1)}, u32[]{:S(2)}, u32[]{:S(2)}) collective-permute-start(bf16[768,256]{1,0:T(8,128)(2,1)S(1)} %bitcast.20), channel_id=1, source_target_pairs={{0,8},{8,16},{16,24},{24,32},{32,40},{40,48},{48,56},{56,64},{64,7... | collective-permute-start | bytes 1179656 | tf_op jit(solution)/shard_map/ppermute | solution.py:19
  27.0 0.1 slice.21
  27.1 0.0 copy-start
  27.1 0.7 gather_fusion
  27.7 0.1 reshape.71
  27.8 0.2 convert_reduce_fusion
  28.0 7.9 %collective-permute-done.refs_3_ = bf16[768,256]{1,0:T(8,128)(2,1)S(1)} collective-permute-done((bf16[768,256]{1,0:T(8,128)(2,1)S(1)}, bf16[768,256]{1,0:T(8,128)(2,1)S(1)}, u32[]{:S(2)}, u32[]{:S(2)}) %collective-permute-start) | collective-permute-done | bytes 393248 | tf_op jit(solution)/shard_map/ppermute | solution.py:19
  35.9 0.9 %all-to-all-done = bf16[128,8,512]{2,0,1:T(8,128)(2,1)S(1)} async-done(((bf16[128,8,512]{2,0,1:T(8,128)(2,1)}), bf16[128,8,512]{2,0,1:T(8,128)(2,1)S(1)}, u32[]{:S(2)}, u32[]{:S(2)}) %all-to-all-start) | async-done | bytes 1048608 | tf_op jit(solution)/shard_map/all_to_all | solution.py:235
  36.9 0.0 copy-done
  36.9 13.0 %shard_map.85 = (bf16[1024,512]{1,0:T(8,128)(2,1)}, bf16[1024,512]{1,0:T(8,128)(2,1)}, bf16[768,256]{1,0:T(8,128)(2,1)S(1)}, f32[1024,256]{1,0:T(8,128)S(1)}) custom-call(s32[4]{0:T(128)S(1)} %add_subtract_fusion.refs_0_, bf16[1024,512]{1,0:T(8,128)(2,1)S(1)} %bitcast.16, bf16[1024,256]{1,0:T(8,128)(2,1)S(1)} %bitcast.14, ...), custom_call_target="tpu_custom_call" | custom-call | flops 4831838208 | bytes 6291456 | tf_op jit(solution)/shard_map/pallas_call | solution.py:205
  49.9 1.9 %collective-permute-start.1 = (bf16[768,256]{1,0:T(8,128)(2,1)S(1)}, bf16[768,256]{1,0:T(8,128)(2,1)S(1)}, u32[]{:S(2)}, u32[]{:S(2)}) collective-permute-start(bf16[768,256]{1,0:T(8,128)(2,1)S(1)} %get-tuple-element.17), channel_id=1, source_target_pairs={{8,0},{16,8},{24,16},{32,24},{40,32},{48,40},{56,48},{64,56},{72,6... | collective-permute-start | bytes 1179656 | tf_op jit(solution)/shard_map/ppermute | solution.py:19
  51.8 5.2 %shard_map.86 = (bf16[1024,512]{1,0:T(8,128)(2,1)}, bf16[1024,512]{1,0:T(8,128)(2,1)}, f32[1024,256]{1,0:T(8,128)S(1)}) custom-call(s32[4]{0:T(128)S(1)} %add_subtract_fusion.refs_0_, bf16[1024,512]{1,0:T(8,128)(2,1)S(1)} %bitcast.17, bf16[1024,256]{1,0:T(8,128)(2,1)S(1)} %bitcast.15, ...), custom_call_target="tpu_custom_call", output_to_operand_aliasing={{0}: (4, {}), {1}: (5, {}), {2}: (6, {})} | custom-call | flops 1610612736 | bytes 6291456 | tf_op jit(solution)/shard_map/pallas_call | solution.py:205
  57.0 11.9 %collective-permute-done.1 = bf16[768,256]{1,0:T(8,128)(2,1)S(1)} collective-permute-done((bf16[768,256]{1,0:T(8,128)(2,1)S(1)}, bf16[768,256]{1,0:T(8,128)(2,1)S(1)}, u32[]{:S(2)}, u32[]{:S(2)}) %collective-permute-start.1) | collective-permute-done | bytes 393248 | tf_op jit(solution)/shard_map/ppermute | solution.py:19
  68.9 0.1 pad_convert_fusion
  69.0 0.9 %fusion = (bf16[1024,128]{1,0:T(8,128)(2,1)}, bf16[1024,128]{1,0:T(8,128)(2,1)}) fusion(f32[1024,256]{1,0:T(8,128)S(1)} %pad_convert_fusion, f32[1024,256]{1,0:T(8,128)S(1)} %get-tuple-element.16), kind=kLoop, calls=%fused_computation.3 | loop fusion | flops 655360 | bytes 2621440 | tf_op jit(solution)/shard_map/convert_element_type | solution.py:261
  (6 shorter events, 0.1 us)
Async XLA Ops:
  0.6 6.5 %copy-start.1 = (bf16[128,4096]{1,0:T(8,128)(2,1)S(1)}, bf16[128,4096]{1,0:T(8,128)(2,1)}, u32[]{:S(2)}) copy-start(bf16[128,4096]{1,0:T(8,128)(2,1)} %param.5) | copy-start | bytes 3145732
  2.6 14.8 %all-to-all-start.1 = ((bf16[8,128,256]{2,1,0:T(8,128)(2,1)}), bf16[8,128,256]{2,1,0:T(8,128)(2,1)S(1)}, u32[]{:S(2)}, u32[]{:S(2)}) async-start(bf16[8,128,256]{2,1,0:T(8,128)(2,1)} %bitcast.18), calls=%async_computation.1 | async-start | bytes 1048576 | tf_op jit(solution)/shard_map/all_to_all | solution.py:232
  17.4 19.4 %all-to-all-start = ((bf16[128,8,512]{2,0,1:T(8,128)(2,1)}), bf16[128,8,512]{2,0,1:T(8,128)(2,1)S(1)}, u32[]{:S(2)}, u32[]{:S(2)}) async-start(bf16[128,8,512]{2,0,1:T(8,128)(2,1)} %bitcast.13), calls=%async_computation | async-start | bytes 2097152 | tf_op jit(solution)/shard_map/all_to_all | solution.py:235
  21.2 0.7 copy-start.2
  22.0 13.9 %collective-permute-start = (bf16[768,256]{1,0:T(8,128)(2,1)S(1)}, bf16[768,256]{1,0:T(8,128)(2,1)S(1)}, u32[]{:S(2)}, u32[]{:S(2)}) collective-permute-start(bf16[768,256]{1,0:T(8,128)(2,1)S(1)} %bitcast.20), channel_id=1, source_target_pairs={{0,8},{8,16},{16,24},{24,32},{32,40},{40,48},{48,56},{56,64},{64,7... | collective-permute-start | bytes 1179656 | tf_op jit(solution)/shard_map/ppermute | solution.py:19
  27.1 9.8 %copy-start = (bf16[1024,512]{1,0:T(8,128)(2,1)S(1)}, bf16[1024,512]{1,0:T(8,128)(2,1)}, u32[]{:S(2)}) copy-start(bf16[1024,512]{1,0:T(8,128)(2,1)} %refs_3_.1) | copy-start | bytes 3145732
  49.9 19.0 %collective-permute-start.1 = (bf16[768,256]{1,0:T(8,128)(2,1)S(1)}, bf16[768,256]{1,0:T(8,128)(2,1)S(1)}, u32[]{:S(2)}, u32[]{:S(2)}) collective-permute-start(bf16[768,256]{1,0:T(8,128)(2,1)S(1)} %get-tuple-element.17), channel_id=1, source_target_pairs={{8,0},{16,8},{24,16},{32,24},{40,32},{48,40},{56,48},{64,56},{72,6... | collective-permute-start | bytes 1179656 | tf_op jit(solution)/shard_map/ppermute | solution.py:19

commit v13 on v12

--- a/solution.py
+++ b/solution.py
@@ -145,20 +145,29 @@
             prior_out[:, HEAD_SIZE:] = prior_ref[:, HEAD_SIZE:].astype(prior_out.dtype)
 
 
-def kv_pack_kernel(k_ref, v_ref, o_ref, *, groups, rows):
+def kv_pack_kernel(k_hbm, v_hbm, o_hbm, sems, *, groups, rows):
+    copies = []
     for g in range(groups):
-        o_ref[g * rows:(g + 1) * rows, 0:HEAD_SIZE] = k_ref[:, g * HEAD_SIZE:(g + 1) * HEAD_SIZE]
-        o_ref[g * rows:(g + 1) * rows, HEAD_SIZE:] = v_ref[:, g * HEAD_SIZE:(g + 1) * HEAD_SIZE]
+        for i, source in enumerate((k_hbm, v_hbm)):
+            copy = pltpu.make_async_copy(
+                source.at[:, pl.ds(g * HEAD_SIZE, HEAD_SIZE)],
+                o_hbm.at[pl.ds(g * rows, rows), pl.ds(i * HEAD_SIZE, HEAD_SIZE)],
+                sems.at[2 * g + i],
+            )
+            copy.start()
+            copies.append(copy)
+    for copy in copies:
+        copy.wait()
 
 
 def kv_pack(key_matrix, value_matrix, groups, interpret=False):
     rows = key_matrix.shape[0]
-    vmem = pltpu.MemorySpace.VMEM
     return pl.pallas_call(
         functools.partial(kv_pack_kernel, groups=groups, rows=rows),
         out_shape=jax.ShapeDtypeStruct((groups * rows, 2 * HEAD_SIZE), key_matrix.dtype),
-        in_specs=[pl.BlockSpec(memory_space=vmem)] * 2,
-        out_specs=pl.BlockSpec(memory_space=vmem),
+        in_specs=[pl.BlockSpec(memory_space=pl.ANY)] * 2,
+        out_specs=pl.BlockSpec(memory_space=pl.ANY),
+        scratch_shapes=[pltpu.SemaphoreType.DMA((2 * groups,))],
         interpret=interpret,
     )(key_matrix, value_matrix)
 

time: 70.6 us -> 85.8 us (1.22)
  Pallas kernels: 20.2 us -> 35.4 us
  waiting for transfers between devices: 30 us -> 27.5 us
  starting transfers between devices: 14.9 us -> 17.3 us
    pallas_call x1, Pallas kernels: 2 us -> 17.1 us  [kv_pack(): pl.pallas_call(functools.partial(kv_pack_kernel, groups=groups, rows=rows...]
    ppermute x2, waiting for transfers between devices: 19.8 us -> 17.3 us  [from_behind(): return lax.ppermute(block, axis, route)]
    ppermute x2, starting transfers between devices: 6.86 us -> 9.29 us  [from_behind(): return lax.ppermute(block, axis, route)]
  transfers between devices with their start and end apart: 4 -> 4, of which waited for: 4 -> 4; matrix products, arithmetic and copies ran while one was open for 4% -> 3% of each run, Pallas kernels for 7% -> 6%
where the time goes in v13:
time: 85.8 us; the launch traced here: 85 us
  Pallas kernels  35.4 us (41%)
  waiting for transfers between devices  27.5 us (32%)
  starting transfers between devices  17.3 us (20%)
  local copies, waits for them, and re-layouts  2.66 us (3%)
  other arithmetic  1.44 us (2%)
    pallas_call x2, Pallas kernels, attention_call(): pl.pallas_call(kernel, grid=(steps,), out_shape=tuple(out_shape), in_spec...  18.3 us
    ppermute x2, waiting for transfers between devices, from_behind(): return lax.ppermute(block, axis, route)  17.3 us
    pallas_call x1, Pallas kernels, kv_pack(): pl.pallas_call(functools.partial(kv_pack_kernel, groups=groups, rows=rows...  17.1 us
    ppermute x2, starting transfers between devices, from_behind(): return lax.ppermute(block, axis, route)  9.29 us
    all_to_all x1, waiting for transfers between devices, local(): lax.all_to_all(kv_packed, 'head', split_axis=0, concat_axis=0, tiled=True)  9.24 us
    all_to_all x1, starting transfers between devices, local(): lax.all_to_all(kv_packed, 'head', split_axis=0, concat_axis=0, tiled=True)  4.48 us
    all_to_all x1, starting transfers between devices, local(): lax.all_to_all(query_matrix.reshape(token_per_shard, head_groups, q_cols)...  3.56 us
  transfers between devices with their start and end apart: 4, of which 4 were waited for; matrix products, arithmetic and copies ran while one was open for 3% of the time, Pallas kernels for 6%

profile of v13, /device:TPU:102, one launch (start us, length us, event | category | flops | bytes accessed | tf_op | source)
XLA Modules:
  0.0 85.0 jit_solution(11437494299669787458)
XLA Ops:
  0.6 0.0 copy-start.1
  0.6 17.1 %shard_map.84 = bf16[1024,256]{1,0:T(8,128)(2,1)} custom-call(bf16[128,1024]{1,0:T(8,128)(2,1)} %k_hbm.1, bf16[128,1024]{1,0:T(8,128)(2,1)} %v_hbm.1), custom_call_target="tpu_custom_call" | custom-call | tf_op jit(solution)/shard_map/pallas_call | solution.py:165
  17.8 4.5 %all-to-all-start.1 = ((bf16[8,128,256]{2,1,0:T(8,128)(2,1)}), bf16[8,128,256]{2,1,0:T(8,128)(2,1)S(1)}, u32[]{:S(2)}, u32[]{:S(2)}) async-start(bf16[8,128,256]{2,1,0:T(8,128)(2,1)} %bitcast.18), calls=%async_computation.1 | async-start | bytes 1048576 | tf_op jit(solution)/shard_map/all_to_all | solution.py:241
  22.3 0.0 copy-done.1
  22.3 1.1 %copy.17 = bf16[16,8,8,512]{3,2,0,1:T(8,128)(2,1)} copy(bf16[16,8,8,512]{3,2,1,0:T(8,128)(2,1)S(1)} %bitcast.19) | data formatting | bytes 2097152 | tf_op jit(solution)/shard_map/reshape | solution.py:245
  23.3 9.2 %all-to-all-done.1 = bf16[8,128,256]{2,1,0:T(8,128)(2,1)S(1)} async-done(((bf16[8,128,256]{2,1,0:T(8,128)(2,1)}), bf16[8,128,256]{2,1,0:T(8,128)(2,1)S(1)}, u32[]{:S(2)}, u32[]{:S(2)}) %all-to-all-start.1) | async-done | bytes 524320 | tf_op jit(solution)/shard_map/all_to_all | solution.py:241
  32.6 3.6 %all-to-all-start = ((bf16[128,8,512]{2,0,1:T(8,128)(2,1)}), bf16[128,8,512]{2,0,1:T(8,128)(2,1)S(1)}, u32[]{:S(2)}, u32[]{:S(2)}) async-start(bf16[128,8,512]{2,0,1:T(8,128)(2,1)} %bitcast.13), calls=%async_computation | async-start | bytes 2097152 | tf_op jit(solution)/shard_map/all_to_all | solution.py:244
  36.1 0.1 compare_select_fusion
  36.2 0.1 reshape.72
  36.3 0.0 copy-start.2
  36.3 0.7 copy-done.2
  37.0 0.2 select_reduce_fusion
  37.2 5.0 %collective-permute-start = (bf16[768,256]{1,0:T(8,128)(2,1)S(1)}, bf16[768,256]{1,0:T(8,128)(2,1)S(1)}, u32[]{:S(2)}, u32[]{:S(2)}) collective-permute-start(bf16[768,256]{1,0:T(8,128)(2,1)S(1)} %bitcast.20), channel_id=1, source_target_pairs={{0,8},{8,16},{16,24},{24,32},{32,40},{40,48},{48,56},{56,64},{64,7... | collective-permute-start | bytes 1179656 | tf_op jit(solution)/shard_map/ppermute | solution.py:19
  42.2 0.1 slice.21
  42.2 0.0 copy-start
  42.2 0.7 gather_fusion
  42.9 0.1 reshape.71
  43.0 0.2 convert_reduce_fusion
  43.2 7.9 %collective-permute-done.refs_3_ = bf16[768,256]{1,0:T(8,128)(2,1)S(1)} collective-permute-done((bf16[768,256]{1,0:T(8,128)(2,1)S(1)}, bf16[768,256]{1,0:T(8,128)(2,1)S(1)}, u32[]{:S(2)}, u32[]{:S(2)}) %collective-permute-start) | collective-permute-done | bytes 393248 | tf_op jit(solution)/shard_map/ppermute | solution.py:19
  51.1 0.9 %all-to-all-done = bf16[128,8,512]{2,0,1:T(8,128)(2,1)S(1)} async-done(((bf16[128,8,512]{2,0,1:T(8,128)(2,1)}), bf16[128,8,512]{2,0,1:T(8,128)(2,1)S(1)}, u32[]{:S(2)}, u32[]{:S(2)}) %all-to-all-start) | async-done | bytes 1048608 | tf_op jit(solution)/shard_map/all_to_all | solution.py:244
  52.0 0.0 copy-done
  52.0 13.1 %shard_map.85 = (bf16[1024,512]{1,0:T(8,128)(2,1)}, bf16[1024,512]{1,0:T(8,128)(2,1)}, bf16[768,256]{1,0:T(8,128)(2,1)S(1)}, f32[1024,256]{1,0:T(8,128)S(1)}) custom-call(s32[4]{0:T(128)S(1)} %add_subtract_fusion.refs_0_, bf16[1024,512]{1,0:T(8,128)(2,1)S(1)} %bitcast.16, bf16[1024,256]{1,0:T(8,128)(2,1)S(1)} %bitcast.14, ...), custom_call_target="tpu_custom_call" | custom-call | flops 4831838208 | bytes 6291456 | tf_op jit(solution)/shard_map/pallas_call | solution.py:214
  65.1 4.3 %collective-permute-start.1 = (bf16[768,256]{1,0:T(8,128)(2,1)S(1)}, bf16[768,256]{1,0:T(8,128)(2,1)S(1)}, u32[]{:S(2)}, u32[]{:S(2)}) collective-permute-start(bf16[768,256]{1,0:T(8,128)(2,1)S(1)} %get-tuple-element.17), channel_id=1, source_target_pairs={{8,0},{16,8},{24,16},{32,24},{40,32},{48,40},{56,48},{64,56},{72,6... | collective-permute-start | bytes 1179656 | tf_op jit(solution)/shard_map/ppermute | solution.py:19
  69.4 5.2 %shard_map.86 = (bf16[1024,512]{1,0:T(8,128)(2,1)}, bf16[1024,512]{1,0:T(8,128)(2,1)}, f32[1024,256]{1,0:T(8,128)S(1)}) custom-call(s32[4]{0:T(128)S(1)} %add_subtract_fusion.refs_0_, bf16[1024,512]{1,0:T(8,128)(2,1)S(1)} %bitcast.17, bf16[1024,256]{1,0:T(8,128)(2,1)S(1)} %bitcast.15, ...), custom_call_target="tpu_custom_call", output_to_operand_aliasing={{0}: (4, {}), {1}: (5, {}), {2}: (6, {})} | custom-call | flops 1610612736 | bytes 6291456 | tf_op jit(solution)/shard_map/pallas_call | solution.py:214
  74.6 9.4 %collective-permute-done.1 = bf16[768,256]{1,0:T(8,128)(2,1)S(1)} collective-permute-done((bf16[768,256]{1,0:T(8,128)(2,1)S(1)}, bf16[768,256]{1,0:T(8,128)(2,1)S(1)}, u32[]{:S(2)}, u32[]{:S(2)}) %collective-permute-start.1) | collective-permute-done | bytes 393248 | tf_op jit(solution)/shard_map/ppermute | solution.py:19
  84.1 0.1 pad_convert_fusion
  84.1 0.9 %fusion = (bf16[1024,128]{1,0:T(8,128)(2,1)}, bf16[1024,128]{1,0:T(8,128)(2,1)}) fusion(f32[1024,256]{1,0:T(8,128)S(1)} %pad_convert_fusion, f32[1024,256]{1,0:T(8,128)S(1)} %get-tuple-element.16), kind=kLoop, calls=%fused_computation.3 | loop fusion | flops 655360 | bytes 2621440 | tf_op jit(solution)/shard_map/convert_element_type | solution.py:270
  (6 shorter events, 0.1 us)
Async XLA Ops:
  0.6 21.6 %copy-start.1 = (bf16[128,4096]{1,0:T(8,128)(2,1)S(1)}, bf16[128,4096]{1,0:T(8,128)(2,1)}, u32[]{:S(2)}) copy-start(bf16[128,4096]{1,0:T(8,128)(2,1)} %param.5) | copy-start | bytes 3145732
  17.8 14.8 %all-to-all-start.1 = ((bf16[8,128,256]{2,1,0:T(8,128)(2,1)}), bf16[8,128,256]{2,1,0:T(8,128)(2,1)S(1)}, u32[]{:S(2)}, u32[]{:S(2)}) async-start(bf16[8,128,256]{2,1,0:T(8,128)(2,1)} %bitcast.18), calls=%async_computation.1 | async-start | bytes 1048576 | tf_op jit(solution)/shard_map/all_to_all | solution.py:241
  32.6 19.4 %all-to-all-start = ((bf16[128,8,512]{2,0,1:T(8,128)(2,1)}), bf16[128,8,512]{2,0,1:T(8,128)(2,1)S(1)}, u32[]{:S(2)}, u32[]{:S(2)}) async-start(bf16[128,8,512]{2,0,1:T(8,128)(2,1)} %bitcast.13), calls=%async_computation | async-start | bytes 2097152 | tf_op jit(solution)/shard_map/all_to_all | solution.py:244
  36.3 0.7 copy-start.2
  37.2 13.9 %collective-permute-start = (bf16[768,256]{1,0:T(8,128)(2,1)S(1)}, bf16[768,256]{1,0:T(8,128)(2,1)S(1)}, u32[]{:S(2)}, u32[]{:S(2)}) collective-permute-start(bf16[768,256]{1,0:T(8,128)(2,1)S(1)} %bitcast.20), channel_id=1, source_target_pairs={{0,8},{8,16},{16,24},{24,32},{32,40},{40,48},{48,56},{56,64},{64,7... | collective-permute-start | bytes 1179656 | tf_op jit(solution)/shard_map/ppermute | solution.py:19
  42.2 9.8 %copy-start = (bf16[1024,512]{1,0:T(8,128)(2,1)S(1)}, bf16[1024,512]{1,0:T(8,128)(2,1)}, u32[]{:S(2)}) copy-start(bf16[1024,512]{1,0:T(8,128)(2,1)} %refs_3_.1) | copy-start | bytes 3145732
  65.1 19.0 %collective-permute-start.1 = (bf16[768,256]{1,0:T(8,128)(2,1)S(1)}, bf16[768,256]{1,0:T(8,128)(2,1)S(1)}, u32[]{:S(2)}, u32[]{:S(2)}) collective-permute-start(bf16[768,256]{1,0:T(8,128)(2,1)S(1)} %get-tuple-element.17), channel_id=1, source_target_pairs={{8,0},{16,8},{24,16},{32,24},{40,32},{48,40},{56,48},{64,56},{72,6... | collective-permute-start | bytes 1179656 | tf_op jit(solution)/shard_map/ppermute | solution.py:19

commit v14 on v12

--- a/solution.py
+++ b/solution.py
@@ -145,20 +145,20 @@
             prior_out[:, HEAD_SIZE:] = prior_ref[:, HEAD_SIZE:].astype(prior_out.dtype)
 
 
-def kv_pack_kernel(k_ref, v_ref, o_ref, *, groups, rows):
-    for g in range(groups):
-        o_ref[g * rows:(g + 1) * rows, 0:HEAD_SIZE] = k_ref[:, g * HEAD_SIZE:(g + 1) * HEAD_SIZE]
-        o_ref[g * rows:(g + 1) * rows, HEAD_SIZE:] = v_ref[:, g * HEAD_SIZE:(g + 1) * HEAD_SIZE]
+def kv_pack_kernel(k_ref, v_ref, o_ref):
+    o_ref[:, 0:HEAD_SIZE] = k_ref[...]
+    o_ref[:, HEAD_SIZE:] = v_ref[...]
 
 
 def kv_pack(key_matrix, value_matrix, groups, interpret=False):
     rows = key_matrix.shape[0]
-    vmem = pltpu.MemorySpace.VMEM
+    column_block = pl.BlockSpec((rows, HEAD_SIZE), lambda g: (0, g))
     return pl.pallas_call(
-        functools.partial(kv_pack_kernel, groups=groups, rows=rows),
+        kv_pack_kernel,
+        grid=(groups,),
         out_shape=jax.ShapeDtypeStruct((groups * rows, 2 * HEAD_SIZE), key_matrix.dtype),
-        in_specs=[pl.BlockSpec(memory_space=vmem)] * 2,
-        out_specs=pl.BlockSpec(memory_space=vmem),
+        in_specs=[column_block, column_block],
+        out_specs=pl.BlockSpec((rows, 2 * HEAD_SIZE), lambda g: (g, 0)),
         interpret=interpret,
     )(key_matrix, value_matrix)
 

time: 70.6 us -> 73.1 us (1.035)
  starting transfers between devices: 14.9 us -> 19.2 us
  Pallas kernels: 20.2 us -> 19.3 us
  waiting for transfers between devices: 30 us -> 29.2 us
    ppermute x2, starting transfers between devices: 6.86 us -> 11.2 us  [from_behind(): return lax.ppermute(block, axis, route)]
    pallas_call x2, Pallas kernels: 18.2 us -> 14.7 us  [attention_call(): pl.pallas_call(kernel, grid=(steps,), out_shape=tuple(out_shape), in_spec...]
    pallas_call x1, Pallas kernels: 2 us -> 4.61 us  [kv_pack(): pl.pallas_call(kv_pack_kernel, grid=(groups,), out_shape=jax.ShapeDtypeSt...]
    ppermute x2, waiting for transfers between devices: 19.8 us -> 19 us  [from_behind(): return lax.ppermute(block, axis, route)]
  transfers between devices with their start and end apart: 4 -> 4, of which waited for: 4 -> 4; matrix products, arithmetic and copies ran while one was open for 4% -> 3% of each run, Pallas kernels for 7% -> 7%
where the time goes in v14:
time: 73.1 us; the launch traced here: 72.5 us
  waiting for transfers between devices  29.2 us (40%)
  Pallas kernels  19.3 us (26%)
  starting transfers between devices  19.2 us (26%)
  local copies, waits for them, and re-layouts  2.66 us (4%)
  other arithmetic  1.44 us (2%)
    ppermute x2, waiting for transfers between devices, from_behind(): return lax.ppermute(block, axis, route)  19 us
    pallas_call x2, Pallas kernels, attention_call(): pl.pallas_call(kernel, grid=(steps,), out_shape=tuple(out_shape), in_spec...  14.7 us
    ppermute x2, starting transfers between devices, from_behind(): return lax.ppermute(block, axis, route)  11.2 us
    all_to_all x1, waiting for transfers between devices, local(): lax.all_to_all(kv_packed, 'head', split_axis=0, concat_axis=0, tiled=True)  9.24 us
    pallas_call x1, Pallas kernels, kv_pack(): pl.pallas_call(kv_pack_kernel, grid=(groups,), out_shape=jax.ShapeDtypeSt...  4.61 us
    all_to_all x1, starting transfers between devices, local(): lax.all_to_all(kv_packed, 'head', split_axis=0, concat_axis=0, tiled=True)  4.47 us
    all_to_all x1, starting transfers between devices, local(): lax.all_to_all(query_matrix.reshape(token_per_shard, head_groups, q_cols)...  3.56 us
  transfers between devices with their start and end apart: 4, of which 4 were waited for; matrix products, arithmetic and copies ran while one was open for 3% of the time, Pallas kernels for 7%

profile of v14, /device:TPU:102, one launch (start us, length us, event | category | flops | bytes accessed | tf_op | source)
XLA Modules:
  0.0 72.5 jit_solution(16976676228377236779)
XLA Ops:
  0.6 0.0 copy-start.1
  0.6 4.6 %shard_map.84 = bf16[1024,256]{1,0:T(8,128)(2,1)} custom-call(bf16[128,1024]{1,0:T(8,128)(2,1)} %k_ref.1, bf16[128,1024]{1,0:T(8,128)(2,1)} %v_ref.1), custom_call_target="tpu_custom_call" | custom-call | tf_op jit(solution)/shard_map/pallas_call | solution.py:156
  5.3 4.5 %all-to-all-start.1 = ((bf16[8,128,256]{2,1,0:T(8,128)(2,1)}), bf16[8,128,256]{2,1,0:T(8,128)(2,1)S(1)}, u32[]{:S(2)}, u32[]{:S(2)}) async-start(bf16[8,128,256]{2,1,0:T(8,128)(2,1)} %bitcast.18), calls=%async_computation.1 | async-start | bytes 1048576 | tf_op jit(solution)/shard_map/all_to_all | solution.py:232
  9.7 0.0 copy-done.1
  9.7 1.1 %copy.17 = bf16[16,8,8,512]{3,2,0,1:T(8,128)(2,1)} copy(bf16[16,8,8,512]{3,2,1,0:T(8,128)(2,1)S(1)} %bitcast.19) | data formatting | bytes 2097152 | tf_op jit(solution)/shard_map/reshape | solution.py:236
  10.8 9.2 %all-to-all-done.1 = bf16[8,128,256]{2,1,0:T(8,128)(2,1)S(1)} async-done(((bf16[8,128,256]{2,1,0:T(8,128)(2,1)}), bf16[8,128,256]{2,1,0:T(8,128)(2,1)S(1)}, u32[]{:S(2)}, u32[]{:S(2)}) %all-to-all-start.1) | async-done | bytes 524320 | tf_op jit(solution)/shard_map/all_to_all | solution.py:232
  20.0 3.6 %all-to-all-start = ((bf16[128,8,512]{2,0,1:T(8,128)(2,1)}), bf16[128,8,512]{2,0,1:T(8,128)(2,1)S(1)}, u32[]{:S(2)}, u32[]{:S(2)}) async-start(bf16[128,8,512]{2,0,1:T(8,128)(2,1)} %bitcast.13), calls=%async_computation | async-start | bytes 2097152 | tf_op jit(solution)/shard_map/all_to_all | solution.py:235
  23.6 0.1 compare_select_fusion
  23.7 0.1 reshape.72
  23.8 0.0 copy-start.2
  23.8 0.7 copy-done.2
  24.4 0.2 select_reduce_fusion
  24.6 5.0 %collective-permute-start = (bf16[768,256]{1,0:T(8,128)(2,1)S(1)}, bf16[768,256]{1,0:T(8,128)(2,1)S(1)}, u32[]{:S(2)}, u32[]{:S(2)}) collective-permute-start(bf16[768,256]{1,0:T(8,128)(2,1)S(1)} %bitcast.20), channel_id=1, source_target_pairs={{0,8},{8,16},{16,24},{24,32},{32,40},{40,48},{48,56},{56,64},{64,7... | collective-permute-start | bytes 1179656 | tf_op jit(solution)/shard_map/ppermute | solution.py:19
  29.6 0.1 slice.21
  29.7 0.0 copy-start
  29.7 0.7 gather_fusion
  30.4 0.1 reshape.71
  30.4 0.2 convert_reduce_fusion
  30.6 7.9 %collective-permute-done.refs_3_ = bf16[768,256]{1,0:T(8,128)(2,1)S(1)} collective-permute-done((bf16[768,256]{1,0:T(8,128)(2,1)S(1)}, bf16[768,256]{1,0:T(8,128)(2,1)S(1)}, u32[]{:S(2)}, u32[]{:S(2)}) %collective-permute-start) | collective-permute-done | bytes 393248 | tf_op jit(solution)/shard_map/ppermute | solution.py:19
  38.5 0.9 %all-to-all-done = bf16[128,8,512]{2,0,1:T(8,128)(2,1)S(1)} async-done(((bf16[128,8,512]{2,0,1:T(8,128)(2,1)}), bf16[128,8,512]{2,0,1:T(8,128)(2,1)S(1)}, u32[]{:S(2)}, u32[]{:S(2)}) %all-to-all-start) | async-done | bytes 1048608 | tf_op jit(solution)/shard_map/all_to_all | solution.py:235
  39.5 0.0 copy-done
  39.5 9.5 %shard_map.85 = (bf16[1024,512]{1,0:T(8,128)(2,1)}, bf16[1024,512]{1,0:T(8,128)(2,1)}, bf16[768,256]{1,0:T(8,128)(2,1)S(1)}, f32[1024,256]{1,0:T(8,128)S(1)}) custom-call(s32[4]{0:T(128)S(1)} %add_subtract_fusion.refs_0_, bf16[1024,512]{1,0:T(8,128)(2,1)S(1)} %bitcast.16, bf16[1024,256]{1,0:T(8,128)(2,1)S(1)} %bitcast.14, ...), custom_call_target="tpu_custom_call" | custom-call | flops 4831838208 | bytes 6291456 | tf_op jit(solution)/shard_map/pallas_call | solution.py:205
  48.9 6.2 %collective-permute-start.1 = (bf16[768,256]{1,0:T(8,128)(2,1)S(1)}, bf16[768,256]{1,0:T(8,128)(2,1)S(1)}, u32[]{:S(2)}, u32[]{:S(2)}) collective-permute-start(bf16[768,256]{1,0:T(8,128)(2,1)S(1)} %get-tuple-element.17), channel_id=1, source_target_pairs={{8,0},{16,8},{24,16},{32,24},{40,32},{48,40},{56,48},{64,56},{72,6... | collective-permute-start | bytes 1179656 | tf_op jit(solution)/shard_map/ppermute | solution.py:19
  55.2 5.2 %shard_map.86 = (bf16[1024,512]{1,0:T(8,128)(2,1)}, bf16[1024,512]{1,0:T(8,128)(2,1)}, f32[1024,256]{1,0:T(8,128)S(1)}) custom-call(s32[4]{0:T(128)S(1)} %add_subtract_fusion.refs_0_, bf16[1024,512]{1,0:T(8,128)(2,1)S(1)} %bitcast.17, bf16[1024,256]{1,0:T(8,128)(2,1)S(1)} %bitcast.15, ...), custom_call_target="tpu_custom_call", output_to_operand_aliasing={{0}: (4, {}), {1}: (5, {}), {2}: (6, {})} | custom-call | flops 1610612736 | bytes 6291456 | tf_op jit(solution)/shard_map/pallas_call | solution.py:205
  60.4 11.2 %collective-permute-done.1 = bf16[768,256]{1,0:T(8,128)(2,1)S(1)} collective-permute-done((bf16[768,256]{1,0:T(8,128)(2,1)S(1)}, bf16[768,256]{1,0:T(8,128)(2,1)S(1)}, u32[]{:S(2)}, u32[]{:S(2)}) %collective-permute-start.1) | collective-permute-done | bytes 393248 | tf_op jit(solution)/shard_map/ppermute | solution.py:19
  71.5 0.1 pad_convert_fusion
  71.6 0.9 %fusion = (bf16[1024,128]{1,0:T(8,128)(2,1)}, bf16[1024,128]{1,0:T(8,128)(2,1)}) fusion(f32[1024,256]{1,0:T(8,128)S(1)} %pad_convert_fusion, f32[1024,256]{1,0:T(8,128)S(1)} %get-tuple-element.16), kind=kLoop, calls=%fused_computation.3 | loop fusion | flops 655360 | bytes 2621440 | tf_op jit(solution)/shard_map/convert_element_type | solution.py:261
  (6 shorter events, 0.1 us)
Async XLA Ops:
  0.6 9.1 %copy-start.1 = (bf16[128,4096]{1,0:T(8,128)(2,1)S(1)}, bf16[128,4096]{1,0:T(8,128)(2,1)}, u32[]{:S(2)}) copy-start(bf16[128,4096]{1,0:T(8,128)(2,1)} %param.5) | copy-start | bytes 3145732
  5.3 14.8 %all-to-all-start.1 = ((bf16[8,128,256]{2,1,0:T(8,128)(2,1)}), bf16[8,128,256]{2,1,0:T(8,128)(2,1)S(1)}, u32[]{:S(2)}, u32[]{:S(2)}) async-start(bf16[8,128,256]{2,1,0:T(8,128)(2,1)} %bitcast.18), calls=%async_computation.1 | async-start | bytes 1048576 | tf_op jit(solution)/shard_map/all_to_all | solution.py:232
  20.0 19.4 %all-to-all-start = ((bf16[128,8,512]{2,0,1:T(8,128)(2,1)}), bf16[128,8,512]{2,0,1:T(8,128)(2,1)S(1)}, u32[]{:S(2)}, u32[]{:S(2)}) async-start(bf16[128,8,512]{2,0,1:T(8,128)(2,1)} %bitcast.13), calls=%async_computation | async-start | bytes 2097152 | tf_op jit(solution)/shard_map/all_to_all | solution.py:235
  23.8 0.7 copy-start.2
  24.6 13.9 %collective-permute-start = (bf16[768,256]{1,0:T(8,128)(2,1)S(1)}, bf16[768,256]{1,0:T(8,128)(2,1)S(1)}, u32[]{:S(2)}, u32[]{:S(2)}) collective-permute-start(bf16[768,256]{1,0:T(8,128)(2,1)S(1)} %bitcast.20), channel_id=1, source_target_pairs={{0,8},{8,16},{16,24},{24,32},{32,40},{40,48},{48,56},{56,64},{64,7... | collective-permute-start | bytes 1179656 | tf_op jit(solution)/shard_map/ppermute | solution.py:19
  29.7 9.8 %copy-start = (bf16[1024,512]{1,0:T(8,128)(2,1)S(1)}, bf16[1024,512]{1,0:T(8,128)(2,1)}, u32[]{:S(2)}) copy-start(bf16[1024,512]{1,0:T(8,128)(2,1)} %refs_3_.1) | copy-start | bytes 3145732
  48.9 22.6 %collective-permute-start.1 = (bf16[768,256]{1,0:T(8,128)(2,1)S(1)}, bf16[768,256]{1,0:T(8,128)(2,1)S(1)}, u32[]{:S(2)}, u32[]{:S(2)}) collective-permute-start(bf16[768,256]{1,0:T(8,128)(2,1)S(1)} %get-tuple-element.17), channel_id=1, source_target_pairs={{8,0},{16,8},{24,16},{32,24},{40,32},{48,40},{56,48},{64,56},{72,6... | collective-permute-start | bytes 1179656 | tf_op jit(solution)/shard_map/ppermute | solution.py:19

commit v15 on v12

--- a/solution.py
+++ b/solution.py
@@ -153,12 +153,14 @@
 
 def kv_pack(key_matrix, value_matrix, groups, interpret=False):
     rows = key_matrix.shape[0]
-    vmem = pltpu.MemorySpace.VMEM
+    per_step = groups // 2
+    column_block = pl.BlockSpec((rows, per_step * HEAD_SIZE), lambda s: (0, s))
     return pl.pallas_call(
-        functools.partial(kv_pack_kernel, groups=groups, rows=rows),
+        functools.partial(kv_pack_kernel, groups=per_step, rows=rows),
+        grid=(groups // per_step,),
         out_shape=jax.ShapeDtypeStruct((groups * rows, 2 * HEAD_SIZE), key_matrix.dtype),
-        in_specs=[pl.BlockSpec(memory_space=vmem)] * 2,
-        out_specs=pl.BlockSpec(memory_space=vmem),
+        in_specs=[column_block, column_block],
+        out_specs=pl.BlockSpec((per_step * rows, 2 * HEAD_SIZE), lambda s: (s, 0)),
         interpret=interpret,
     )(key_matrix, value_matrix)
 

time: 70.6 us -> 70.1 us (level)
  no operation moved by 1% of the time
where the time goes in v15:
time: 70.1 us; the launch traced here: 69.8 us
  waiting for transfers between devices  30.2 us (43%)
  Pallas kernels  20 us (29%)
  starting transfers between devices  14.9 us (21%)
  local copies, waits for them, and re-layouts  2.66 us (4%)
  other arithmetic  1.44 us (2%)
  between operations  0.71 us (1%)
    ppermute x2, waiting for transfers between devices, from_behind(): return lax.ppermute(block, axis, route)  20 us
    pallas_call x2, Pallas kernels, attention_call(): pl.pallas_call(kernel, grid=(steps,), out_shape=tuple(out_shape), in_spec...  18 us
    all_to_all x1, waiting for transfers between devices, local(): lax.all_to_all(kv_packed, 'head', split_axis=0, concat_axis=0, tiled=True)  9.24 us
    ppermute x2, starting transfers between devices, from_behind(): return lax.ppermute(block, axis, route)  6.86 us
    all_to_all x1, starting transfers between devices, local(): lax.all_to_all(kv_packed, 'head', split_axis=0, concat_axis=0, tiled=True)  4.47 us
    all_to_all x1, starting transfers between devices, local(): lax.all_to_all(query_matrix.reshape(token_per_shard, head_groups, q_cols)...  3.56 us
    pallas_call x1, Pallas kernels, kv_pack(): pl.pallas_call(functools.partial(kv_pack_kernel, groups=per_step, rows=ro...  1.94 us
  transfers between devices with their start and end apart: 4, of which 4 were waited for; matrix products, arithmetic and copies ran while one was open for 4% of the time, Pallas kernels for 7%

profile of v15, /device:TPU:102, one launch (start us, length us, event | category | flops | bytes accessed | tf_op | source)
XLA Modules:
  0.0 69.8 jit_solution(811088363834751394)
XLA Ops:
  0.6 0.0 copy-start.1
  0.6 1.9 %shard_map.84 = bf16[1024,256]{1,0:T(8,128)(2,1)} custom-call(bf16[128,1024]{1,0:T(8,128)(2,1)} %k_ref.1, bf16[128,1024]{1,0:T(8,128)(2,1)} %v_ref.1), custom_call_target="tpu_custom_call" | custom-call | tf_op jit(solution)/shard_map/pallas_call | solution.py:158
  2.6 4.5 %all-to-all-start.1 = ((bf16[8,128,256]{2,1,0:T(8,128)(2,1)}), bf16[8,128,256]{2,1,0:T(8,128)(2,1)S(1)}, u32[]{:S(2)}, u32[]{:S(2)}) async-start(bf16[8,128,256]{2,1,0:T(8,128)(2,1)} %bitcast.18), calls=%async_computation.1 | async-start | bytes 1048576 | tf_op jit(solution)/shard_map/all_to_all | solution.py:234
  7.1 0.0 copy-done.1
  7.1 1.1 %copy.17 = bf16[16,8,8,512]{3,2,0,1:T(8,128)(2,1)} copy(bf16[16,8,8,512]{3,2,1,0:T(8,128)(2,1)S(1)} %bitcast.19) | data formatting | bytes 2097152 | tf_op jit(solution)/shard_map/reshape | solution.py:238
  8.1 9.2 %all-to-all-done.1 = bf16[8,128,256]{2,1,0:T(8,128)(2,1)S(1)} async-done(((bf16[8,128,256]{2,1,0:T(8,128)(2,1)}), bf16[8,128,256]{2,1,0:T(8,128)(2,1)S(1)}, u32[]{:S(2)}, u32[]{:S(2)}) %all-to-all-start.1) | async-done | bytes 524320 | tf_op jit(solution)/shard_map/all_to_all | solution.py:234
  17.4 3.6 %all-to-all-start = ((bf16[128,8,512]{2,0,1:T(8,128)(2,1)}), bf16[128,8,512]{2,0,1:T(8,128)(2,1)S(1)}, u32[]{:S(2)}, u32[]{:S(2)}) async-start(bf16[128,8,512]{2,0,1:T(8,128)(2,1)} %bitcast.13), calls=%async_computation | async-start | bytes 2097152 | tf_op jit(solution)/shard_map/all_to_all | solution.py:237
  20.9 0.1 compare_select_fusion
  21.0 0.1 reshape.72
  21.1 0.0 copy-start.2
  21.1 0.7 copy-done.2
  21.8 0.2 select_reduce_fusion
  22.0 5.0 %collective-permute-start = (bf16[768,256]{1,0:T(8,128)(2,1)S(1)}, bf16[768,256]{1,0:T(8,128)(2,1)S(1)}, u32[]{:S(2)}, u32[]{:S(2)}) collective-permute-start(bf16[768,256]{1,0:T(8,128)(2,1)S(1)} %bitcast.20), channel_id=1, source_target_pairs={{0,8},{8,16},{16,24},{24,32},{32,40},{40,48},{48,56},{56,64},{64,7... | collective-permute-start | bytes 1179656 | tf_op jit(solution)/shard_map/ppermute | solution.py:19
  26.9 0.1 slice.21
  27.0 0.0 copy-start
  27.0 0.7 gather_fusion
  27.7 0.1 reshape.71
  27.8 0.2 convert_reduce_fusion
  28.0 7.9 %collective-permute-done.refs_3_ = bf16[768,256]{1,0:T(8,128)(2,1)S(1)} collective-permute-done((bf16[768,256]{1,0:T(8,128)(2,1)S(1)}, bf16[768,256]{1,0:T(8,128)(2,1)S(1)}, u32[]{:S(2)}, u32[]{:S(2)}) %collective-permute-start) | collective-permute-done | bytes 393248 | tf_op jit(solution)/shard_map/ppermute | solution.py:19
  35.9 0.9 %all-to-all-done = bf16[128,8,512]{2,0,1:T(8,128)(2,1)S(1)} async-done(((bf16[128,8,512]{2,0,1:T(8,128)(2,1)}), bf16[128,8,512]{2,0,1:T(8,128)(2,1)S(1)}, u32[]{:S(2)}, u32[]{:S(2)}) %all-to-all-start) | async-done | bytes 1048608 | tf_op jit(solution)/shard_map/all_to_all | solution.py:237
  36.8 0.0 copy-done
  36.8 12.8 %shard_map.85 = (bf16[1024,512]{1,0:T(8,128)(2,1)}, bf16[1024,512]{1,0:T(8,128)(2,1)}, bf16[768,256]{1,0:T(8,128)(2,1)S(1)}, f32[1024,256]{1,0:T(8,128)S(1)}) custom-call(s32[4]{0:T(128)S(1)} %add_subtract_fusion.refs_0_, bf16[1024,512]{1,0:T(8,128)(2,1)S(1)} %bitcast.16, bf16[1024,256]{1,0:T(8,128)(2,1)S(1)} %bitcast.14, ...), custom_call_target="tpu_custom_call" | custom-call | flops 4831838208 | bytes 6291456 | tf_op jit(solution)/shard_map/pallas_call | solution.py:207
  49.6 1.9 %collective-permute-start.1 = (bf16[768,256]{1,0:T(8,128)(2,1)S(1)}, bf16[768,256]{1,0:T(8,128)(2,1)S(1)}, u32[]{:S(2)}, u32[]{:S(2)}) collective-permute-start(bf16[768,256]{1,0:T(8,128)(2,1)S(1)} %get-tuple-element.17), channel_id=1, source_target_pairs={{8,0},{16,8},{24,16},{32,24},{40,32},{48,40},{56,48},{64,56},{72,6... | collective-permute-start | bytes 1179656 | tf_op jit(solution)/shard_map/ppermute | solution.py:19
  51.6 5.2 %shard_map.86 = (bf16[1024,512]{1,0:T(8,128)(2,1)}, bf16[1024,512]{1,0:T(8,128)(2,1)}, f32[1024,256]{1,0:T(8,128)S(1)}) custom-call(s32[4]{0:T(128)S(1)} %add_subtract_fusion.refs_0_, bf16[1024,512]{1,0:T(8,128)(2,1)S(1)} %bitcast.17, bf16[1024,256]{1,0:T(8,128)(2,1)S(1)} %bitcast.15, ...), custom_call_target="tpu_custom_call", output_to_operand_aliasing={{0}: (4, {}), {1}: (5, {}), {2}: (6, {})} | custom-call | flops 1610612736 | bytes 6291456 | tf_op jit(solution)/shard_map/pallas_call | solution.py:207
  56.8 12.1 %collective-permute-done.1 = bf16[768,256]{1,0:T(8,128)(2,1)S(1)} collective-permute-done((bf16[768,256]{1,0:T(8,128)(2,1)S(1)}, bf16[768,256]{1,0:T(8,128)(2,1)S(1)}, u32[]{:S(2)}, u32[]{:S(2)}) %collective-permute-start.1) | collective-permute-done | bytes 393248 | tf_op jit(solution)/shard_map/ppermute | solution.py:19
  68.9 0.1 pad_convert_fusion
  68.9 0.9 %fusion = (bf16[1024,128]{1,0:T(8,128)(2,1)}, bf16[1024,128]{1,0:T(8,128)(2,1)}) fusion(f32[1024,256]{1,0:T(8,128)S(1)} %pad_convert_fusion, f32[1024,256]{1,0:T(8,128)S(1)} %get-tuple-element.16), kind=kLoop, calls=%fused_computation.3 | loop fusion | flops 655360 | bytes 2621440 | tf_op jit(solution)/shard_map/convert_element_type | solution.py:263
  (6 shorter events, 0.1 us)
Async XLA Ops:
  0.6 6.4 %copy-start.1 = (bf16[128,4096]{1,0:T(8,128)(2,1)S(1)}, bf16[128,4096]{1,0:T(8,128)(2,1)}, u32[]{:S(2)}) copy-start(bf16[128,4096]{1,0:T(8,128)(2,1)} %param.5) | copy-start | bytes 3145732
  2.6 14.8 %all-to-all-start.1 = ((bf16[8,128,256]{2,1,0:T(8,128)(2,1)}), bf16[8,128,256]{2,1,0:T(8,128)(2,1)S(1)}, u32[]{:S(2)}, u32[]{:S(2)}) async-start(bf16[8,128,256]{2,1,0:T(8,128)(2,1)} %bitcast.18), calls=%async_computation.1 | async-start | bytes 1048576 | tf_op jit(solution)/shard_map/all_to_all | solution.py:234
  17.4 19.4 %all-to-all-start = ((bf16[128,8,512]{2,0,1:T(8,128)(2,1)}), bf16[128,8,512]{2,0,1:T(8,128)(2,1)S(1)}, u32[]{:S(2)}, u32[]{:S(2)}) async-start(bf16[128,8,512]{2,0,1:T(8,128)(2,1)} %bitcast.13), calls=%async_computation | async-start | bytes 2097152 | tf_op jit(solution)/shard_map/all_to_all | solution.py:237
  21.1 0.7 copy-start.2
  22.0 13.9 %collective-permute-start = (bf16[768,256]{1,0:T(8,128)(2,1)S(1)}, bf16[768,256]{1,0:T(8,128)(2,1)S(1)}, u32[]{:S(2)}, u32[]{:S(2)}) collective-permute-start(bf16[768,256]{1,0:T(8,128)(2,1)S(1)} %bitcast.20), channel_id=1, source_target_pairs={{0,8},{8,16},{16,24},{24,32},{32,40},{40,48},{48,56},{56,64},{64,7... | collective-permute-start | bytes 1179656 | tf_op jit(solution)/shard_map/ppermute | solution.py:19
  27.0 9.8 %copy-start = (bf16[1024,512]{1,0:T(8,128)(2,1)S(1)}, bf16[1024,512]{1,0:T(8,128)(2,1)}, u32[]{:S(2)}) copy-start(bf16[1024,512]{1,0:T(8,128)(2,1)} %refs_3_.1) | copy-start | bytes 3145732
  49.6 19.2 %collective-permute-start.1 = (bf16[768,256]{1,0:T(8,128)(2,1)S(1)}, bf16[768,256]{1,0:T(8,128)(2,1)S(1)}, u32[]{:S(2)}, u32[]{:S(2)}) collective-permute-start(bf16[768,256]{1,0:T(8,128)(2,1)S(1)} %get-tuple-element.17), channel_id=1, source_target_pairs={{8,0},{16,8},{24,16},{32,24},{40,32},{48,40},{56,48},{64,56},{72,6... | collective-permute-start | bytes 1179656 | tf_op jit(solution)/shard_map/ppermute | solution.py:19
